TPU v7x, 32 devices: a whole 2x2x4 slice. The times are simulated.
32 devices in a mesh: vocab: 8 (over z, y), grp: 4 (over x, core).
Axes of the slice: x: 2, y: 2, z: 4, core: 2. Of those that a mesh axis runs over, the one named last changes fastest.
Arguments:
- states: bfloat16 [4, 96, 4096], P('grp', 'vocab'), may hold values from -256 to 256
- target_ids: int32 [4, 96], P('grp', 'vocab'), may hold values from 0 to 65535
- lengths: int32 [4, 8], P('grp'), may hold values from 1 to 12, 72 in all within a row
- order: int32 [4, 8], replicated, may hold values from 0 to 7, each once within a row
- gain: float32 [4096], replicated, may hold values from 0.25 to 1.75
- head: bfloat16 [4096, 65536], P(None, 'vocab'), may hold values from -16 to 16
Outputs:
- log_prob: float32 [4, 96], P('grp', 'vocab')
- entropy: float32 [4, 96], P('grp', 'vocab')
- state_norm: float32 [4, 96], P('grp', 'vocab')
- peak_logit: float32 [4, 96], P('grp', 'vocab')
Inputs may be any that keep to these rules, and one draw needn't show every extreme that they name: `order`: each row is a permutation of 0 to 7. `lengths`: each row sums to 72.
All inputs are finite; a program needn't handle non-finite values.
Results may differ from a plain program's by a relative error of at most 0.011.
The roundings to bfloat16 on the way count: a program that leaves them out, or rounds other values in their place, can miss the bound.
Values may be sent and summed in bfloat16 or wider, within the bound.
No kernel may reach another device: no remote copies, remote signals or barrier semaphores. Data moves between devices by JAX's collectives and lax.ppermute only.
A program may use at most 256 MiB of HBM per device.

v0:
```python
import jax
import jax.numpy as jnp
from jax import lax
from jax.sharding import PartitionSpec as P

EPSILON = 1e-05


def normalize(block_states, gain):
    values = block_states.astype(jnp.float32)
    mean_square = jnp.mean(values * values, axis=-1)
    normed = (values * lax.rsqrt(mean_square + EPSILON)[:, None] * gain).astype(jnp.bfloat16)
    return (normed, jnp.sqrt(mean_square))


def score_rows(normed, columns, token_ids, offset):
    logits = jnp.dot(normed, columns, preferred_element_type=jnp.float32)
    local_max = jnp.max(logits, axis=1)
    width = columns.shape[1]
    within = token_ids - offset
    inside = (within >= 0) & (within < width)
    picked = jnp.take_along_axis(logits, jnp.clip(within, 0, width - 1)[:, None], axis=1)[:, 0]
    return (logits, local_max, jnp.where(inside, picked, 0.0))


def exp_sums(logits, center):
    weights = jnp.exp(logits - center[:, None])
    return (jnp.sum(weights, axis=1), jnp.sum(weights * logits, axis=1))


def route_blocks(terms, destination):
    blocks = terms.shape[1]
    one_hot = (destination[:, None] == jnp.arange(blocks, dtype=jnp.int32)[None, :]).astype(
        jnp.float32
    )
    return jnp.einsum("kj,ckr->cjr", one_hot, terms, precision=lax.Precision.HIGHEST)


def own_block(values, position, count):
    return lax.dynamic_slice_in_dim(values, position * count, count)


def shards(states, target_ids, lengths, order, gain, head):
    count = states.shape[1]
    vocab_size = lax.axis_size("vocab")
    group_size = lax.axis_size("grp")
    vocab_index = lax.axis_index("vocab")
    group_index = lax.axis_index("grp")
    own_order = lax.dynamic_index_in_dim(order, group_index, 0, keepdims=False)
    block_ids = jnp.arange(vocab_size, dtype=jnp.int32)
    source_block = jnp.sum(jnp.where(own_order == vocab_index, block_ids, 0))
    length_own = jnp.sum(jnp.where(block_ids == source_block, lengths[0], 0))
    gathered, gathered_ids = (
        lax.all_gather(states, ("vocab", "grp"), axis=1, tiled=True),
        lax.all_gather(target_ids, ("vocab", "grp"), axis=1, tiled=True),
    )
    normed, root_mean = normalize(gathered[0], gain)
    width = head.shape[1] // group_size
    columns = lax.dynamic_slice_in_dim(head, group_index * width, width, 1)
    offset = (vocab_index * group_size + group_index) * width
    logits, local_max, target_logit = score_rows(normed, columns, gathered_ids[0], offset)
    peak = lax.pmax(local_max, ("vocab", "grp"))
    totals, expected = exp_sums(logits, peak)
    blocks = vocab_size * group_size
    terms = jnp.stack([totals, expected, target_logit]).reshape(3, blocks, count)
    group_ids = jnp.arange(group_size, dtype=jnp.int32)[None, :]
    destination = (order.T * group_size + group_ids).reshape(blocks)
    moved = route_blocks(terms, destination).reshape(3, blocks * count)
    mine = lax.psum_scatter(moved, ("vocab", "grp"), scatter_dimension=1, tiled=True)
    position = source_block * group_size + group_index
    own_totals, own_expected, own_target = (mine[0], mine[1], mine[2])
    own_peak = own_block(peak, position, count)
    own_root = own_block(root_mean, position, count)
    keep = (jnp.arange(count, dtype=jnp.int32) < length_own).astype(jnp.float32)
    log_total = jnp.log(own_totals)
    log_prob = (own_target - own_peak - log_total) * keep
    entropy = (own_peak + log_total - own_expected / own_totals) * keep
    return (log_prob[None], entropy[None], (own_root * keep)[None], (own_peak * keep)[None])


def solution(mesh):
    in_specs = (
        P("grp", "vocab", None),
        P("grp", "vocab"),
        P("grp", None),
        P(),
        P(),
        P(None, "vocab"),
    )
    out_specs = (P("grp", "vocab"), P("grp", "vocab"), P("grp", "vocab"), P("grp", "vocab"))
    return jax.shard_map(shards, mesh=mesh, in_specs=in_specs, out_specs=out_specs, check_vma=False)
```

profile of v0, /device:TPU:0, one launch (start us, length us, event | category | flops | bytes accessed | tf_op | source)
XLA Modules:
  0.0 204.1 jit_solution(16833374858033421563)
XLA Ops:
  7.2 0.0 all-gather.2.cloned.1.call-start
  7.2 1.7 copy.16
  9.0 0.0 all-gather.2.cloned.1.call-update
  9.0 0.7 bitcast_add_fusion
  9.7 0.1 copy.20
  9.8 0.1 eq.35
  9.9 1.3 fusion.23
  11.9 0.8 bitcast_dynamic-update-slice_fusion
  12.6 42.2 %all-reduce = s32[384]{0:T(512)S(1)} all-reduce(s32[384]{0:T(512)S(1)} %bitcast_dynamic-update-slice_fusion), channel_id=1, replica_groups=mesh['vocab'=8,'grp'=4] {'vocab','grp'}, use_global_device_ids=true, to_apply=%add | all-reduce | flops 384 | bytes 3072
  54.8 2.0 fusion.22
  56.9 26.3 %all-gather.2.cloned.1.call-done = bf16[1,384,4096]{2,0,1:T(2,128)(2,1)} async-done(((bf16[1,12,4096]{2,0,1:T(2,128)(2,1)}), bf16[1,384,4096]{2,0,1:T(2,128)(2,1)}) %all-gather.2.cloned.1.call-update) | async-done | bytes 3145744 | tf_op jit(solution)/shard_map/all_gather | solution.py:54
  83.2 7.7 %convert_element_type.14 = f32[1,384,4096]{2,0,1:T(1,128)S(1)} convert(bf16[1,384,4096]{2,0,1:T(2,128)(2,1)} %all-gather.2.cloned.1.call-done) | non-fusion elementwise | flops 1572864 | bytes 9437184 | tf_op jit(solution)/shard_map/convert_element_type | solution.py:10
  90.9 0.0 copy-start
  90.9 3.3 %fusion.2 = f32[384]{0:T(512)S(1)} fusion(f32[1,384,4096]{2,0,1:T(1,128)S(1)} %convert_element_type.14), kind=kLoop, calls=%fused_computation.5 | loop fusion | flops 3145344 | bytes 6292992 | tf_op jit(solution)/shard_map/reduce_sum | solution.py:11
  94.3 0.0 copy-done
  94.3 15.6 %fusion.30 = (f32[384]{0:T(512)S(1)}, f32[384,2048]{1,0:T(8,128)S(1)}) fusion(bf16[4096,8192]{1,0:T(8,128)(2,1)} %param.11, s32[]{:T(128)S(6)} %select_n.61, f32[1,384,4096]{2,0,1:T(1,128)S(1)} %convert_element_type.14, f32[4096]{0:T(1024)S(1)} %copy-done, f32[384]{0:T(512)S(1)} %get-tuple-element.10), kind=kOutput, calls=%fused_computation.59 | convolution fusion | flops 6447955456 | bytes 26233860 | tf_op jit(solution)/shard_map/dot_general | solution.py:17
  109.8 3.5 %gather_fusion = f32[384]{0:T(512)S(1)} fusion(f32[384,2048]{1,0:T(8,128)S(1)} %get-tuple-element.12, s32[384]{0:T(512)S(1)} %fusion.21), kind=kCustom, calls=%fused_computation | custom fusion | bytes 6144 | tf_op jit(solution)/shard_map/jit(take_along_axis)/gather | solution.py:22
  113.3 0.1 stack.14
  113.4 0.1 copy.19
  113.5 39.4 %pmax.7 = f32[384]{0:T(512)S(1)} all-reduce(f32[384]{0:T(512)S(1)} %get-tuple-element.11), channel_id=1, replica_groups=mesh['vocab'=8,'grp'=4] {'vocab','grp'}, use_global_device_ids=true, to_apply=%region_4.5 | all-reduce | flops 384 | bytes 3072 | tf_op jit(solution)/shard_map/pmax | solution.py:62
  152.9 1.0 fusion.6
  153.9 0.1 stack.12
  154.0 0.1 copy.17
  154.1 0.1 stack.13
  154.2 0.1 copy.18
  154.3 0.2 convolution_bitcast_fusion
  154.5 0.1 copy.21
  154.6 0.1 reshape.85
  154.7 40.0 %all-reduce.1 = f32[3,384]{1,0:T(4,128)S(1)} all-reduce(f32[3,384]{1,0:T(4,128)S(1)} %reshape.85), channel_id=2, replica_groups=mesh['vocab'=8,'grp'=4] {'vocab','grp'}, use_global_device_ids=true, to_apply=%region_7.8.clone | all-reduce | flops 1152 | bytes 9216
  194.7 0.1 constant_dynamic-slice_fusion
  194.8 1.2 fusion.25
  196.0 1.2 select_bitcast_fusion.1
  (9 shorter events, 0.1 us)
Async XLA Ops:
  7.2 76.0 %all-gather.2.cloned.1.call-start = ((), (), s32[]{:S(2)}) async-start(), calls=%async_computation | async-start | bytes 6488064 | tf_op jit(solution)/shard_map/all_gather | solution.py:54
  90.9 3.3 %copy-start = (f32[4096]{0:T(1024)S(1)}, f32[4096]{0:T(1024)}, u32[]{:S(2)}) copy-start(f32[4096]{0:T(1024)} %param.10) | copy-start | bytes 49156
Sparse Core Ops, SparseCore 0:
  10.9 72.2 all-gather.1
where the time goes:
time: 205 us; the launch traced here: 204 us
  blocking collectives  122 us (60%)
  waiting for transfers between devices  26.3 us (13%)
  other arithmetic  18.6 us (9%)
  matrix products  15.8 us (8%)
  between operations  14.8 us (7%)
  local copies, waits for them, and re-layouts  6.96 us (3%)
    unnamed x2, blocking collectives  82.2 us
    pmax x1, blocking collectives, shards(): peak = lax.pmax(local_max, ('vocab', 'grp'))  39.4 us
    all_gather x1, waiting for transfers between devices, shards(): lax.all_gather(states, ('vocab', 'grp'), axis=1, tiled=True)  26.3 us
    dot_general x1, matrix products, score_rows(): logits = jnp.dot(normed, columns, preferred_element_type=jnp.float32)  15.6 us
    convert_element_type x1, other arithmetic, normalize(): values = block_states.astype(jnp.float32)  7.72 us
  transfers between devices with their start and end apart: 1, of which 1 were waited for; matrix products, arithmetic and copies ran while one was open for 2% of the time, Pallas kernels for 0%

commit v1 on v0

v1 whole, which is shorter than its diff:
```python
import jax
import jax.numpy as jnp
from jax import lax
from jax.sharding import PartitionSpec as P

EPSILON = 1e-05
RADIX = 256
LANES = 128


def digit_count(total):
    digits = 1
    while RADIX**digits < total:
        digits += 1
    return digits


def normalize(block_states, gain):
    values = block_states.astype(jnp.float32)
    mean_square = jnp.mean(values * values, axis=-1)
    normed = (values * lax.rsqrt(mean_square + EPSILON)[:, None] * gain).astype(jnp.bfloat16)
    return (normed, jnp.sqrt(mean_square))


def partial_stats(normed, columns, token_ids, offset):
    logits = jnp.dot(normed, columns, preferred_element_type=jnp.float32)
    local_max = jnp.max(logits, axis=1)
    weights = jnp.exp(logits - local_max[:, None])
    width = columns.shape[1]
    within = token_ids - offset
    inside = (within >= 0) & (within < width)
    picked = jnp.take_along_axis(logits, jnp.clip(within, 0, width - 1)[:, None], axis=1)[:, 0]
    return (
        local_max,
        jnp.sum(weights, axis=1),
        jnp.sum(weights * logits, axis=1),
        jnp.where(inside, picked, 0.0),
    )


def shards(states, target_ids, lengths, order, gain, head):
    count = states.shape[1]
    vocab_size = lax.axis_size("vocab")
    vocab_index = lax.axis_index("vocab")
    group_index = lax.axis_index("grp")
    own_order = lax.dynamic_index_in_dim(order, group_index, 0, keepdims=False)
    block_ids = jnp.arange(vocab_size, dtype=jnp.int32)
    normed, root_mean = normalize(states[0], gain)
    width = head.shape[1]
    features = normed.shape[1]
    digits = digit_count(width * vocab_size)
    place = RADIX ** jnp.arange(digits, dtype=jnp.int32)
    coded = ((target_ids[0][:, None] // place[None, :]) % RADIX).astype(jnp.bfloat16)
    coded = jnp.pad(coded, ((0, 0), (0, LANES - digits)))
    packed = lax.all_gather(jnp.concatenate([normed, coded], axis=1), "vocab", axis=0, tiled=True)
    group_normed = packed[:, :features]
    group_ids = jnp.sum(packed[:, features : features + digits].astype(jnp.int32) * place[None, :], axis=1)
    offset = vocab_index * width
    local_max, sums, expected, target = partial_stats(group_normed, head, group_ids, offset)
    rows = vocab_size * count
    home = own_order[vocab_index]
    root_rows = jnp.where(block_ids[:, None] == home, root_mean[None, :], 0.0)
    terms = jnp.stack([local_max, sums, expected, target]).reshape(4, vocab_size, count)
    source_of = jnp.sum(
        jnp.where(own_order[None, :] == block_ids[:, None], block_ids[None, :], 0), axis=1
    )
    routed = jnp.take(terms, source_of, axis=1)
    payload = jnp.concatenate([routed, root_rows[None]], axis=0).transpose(1, 0, 2)
    received = lax.all_to_all(payload, "vocab", 0, 0, tiled=True)
    shard_max, shard_sums, shard_expected, shard_target, shard_root = (
        received[:, 0], received[:, 1], received[:, 2], received[:, 3], received[:, 4]
    )
    peak = jnp.max(shard_max, axis=0)
    scale = jnp.exp(shard_max - peak[None, :])
    totals = jnp.sum(shard_sums * scale, axis=0)
    own_expected = jnp.sum(shard_expected * scale, axis=0)
    own_target = jnp.sum(shard_target, axis=0)
    own_root = jnp.sum(shard_root, axis=0)
    source_block = source_of[vocab_index]
    length_own = jnp.sum(jnp.where(block_ids == source_block, lengths[0], 0))
    keep = (jnp.arange(count, dtype=jnp.int32) < length_own).astype(jnp.float32)
    log_total = jnp.log(totals)
    log_prob = (own_target - peak - log_total) * keep
    entropy = (peak + log_total - own_expected / totals) * keep
    return (log_prob[None], entropy[None], (own_root * keep)[None], (peak * keep)[None])


def solution(mesh):
    in_specs = (
        P("grp", "vocab", None),
        P("grp", "vocab"),
        P("grp", None),
        P(),
        P(),
        P(None, "vocab"),
    )
    out_specs = (P("grp", "vocab"), P("grp", "vocab"), P("grp", "vocab"), P("grp", "vocab"))
    return jax.shard_map(shards, mesh=mesh, in_specs=in_specs, out_specs=out_specs, check_vma=False)
```

time: 205 us -> 84 us (0.41)
  blocking collectives: 122 us -> 34.8 us
  waiting for transfers between devices: 26.3 us -> 4.8 us
  between operations: 14.8 us -> 0.8 us
  other arithmetic: 18.6 us -> 9.98 us
  matrix products: 15.8 us -> 23.5 us
  starting transfers between devices: 0.04 us -> 5.33 us
  local copies, waits for them, and re-layouts: 6.96 us -> 4.45 us
    unnamed x2 -> x0, blocking collectives: 82.2 us -> none
    pmax x1 -> x0, blocking collectives: 39.4 us -> none  [shards(): peak = lax.pmax(local_max, ('vocab', 'grp'))]
    all_gather x0 -> x1, blocking collectives: none -> 34.8 us  [shards(): lax.all_gather(jnp.concatenate([normed, coded], axis=1), 'vocab', axis=0,...]
    all_gather x1 -> x0, waiting for transfers between devices: 26.3 us -> none  [shards(): lax.all_gather(states, ('vocab', 'grp'), axis=1, tiled=True)]
    dot_general x2 -> x1, matrix products: 15.8 us -> 23.5 us  [partial_stats(): logits = jnp.dot(normed, columns, preferred_element_type=jnp.float32)]
    convert_element_type x1 -> x2, other arithmetic: 7.72 us -> 1.87 us  [the longest x1 1.01 us: normalize(): (values * lax.rsqrt(mean_square + EPSILON)[:, None] * gain).astype(jnp.bf...]
    all_to_all x0 -> x1, starting transfers between devices: none -> 5.33 us  [shards(): received = lax.all_to_all(payload, 'vocab', 0, 0, tiled=True)]
    all_to_all x0 -> x1, waiting for transfers between devices: none -> 4.8 us  [shards(): received = lax.all_to_all(payload, 'vocab', 0, 0, tiled=True)]
where the time goes in v1:
time: 84 us; the launch traced here: 83.7 us
  blocking collectives  34.8 us (41%)
  matrix products  23.5 us (28%)
  other arithmetic  9.98 us (12%)
  starting transfers between devices  5.33 us (6%)
  waiting for transfers between devices  4.8 us (6%)
  local copies, waits for them, and re-layouts  4.45 us (5%)
    all_gather x1, blocking collectives, shards(): lax.all_gather(jnp.concatenate([normed, coded], axis=1), 'vocab', axis=0,...  34.8 us
    dot_general x1, matrix products, partial_stats(): logits = jnp.dot(normed, columns, preferred_element_type=jnp.float32)  23.5 us
    all_to_all x1, starting transfers between devices, shards(): received = lax.all_to_all(payload, 'vocab', 0, 0, tiled=True)  5.33 us
    all_to_all x1, waiting for transfers between devices, shards(): received = lax.all_to_all(payload, 'vocab', 0, 0, tiled=True)  4.8 us
  transfers between devices with their start and end apart: 1, of which 1 were waited for; matrix products, arithmetic and copies ran while one was open for 2% of the time, Pallas kernels for 0%

profile of v1, /device:TPU:0, one launch (start us, length us, event | category | flops | bytes accessed | tf_op | source)
XLA Modules:
  0.0 83.7 jit_solution(1341524205917599960)
XLA Ops:
  0.6 0.0 copy-start.1
  0.7 0.7 bitcast_sign_fusion
  1.3 1.0 %fusion.4 = f32[12]{0:T(128)S(1)} fusion(bf16[1,12,4096]{2,1,0:T(8,128)(2,1)} %param.6), kind=kLoop, calls=%fused_computation.11 | loop fusion | flops 147444 | bytes 98352 | tf_op jit(solution)/shard_map/reduce_sum | solution.py:20
  2.4 1.0 %fusion.6 = bf16[12,4096]{1,0:T(8,128)(2,1)S(1)} fusion(bf16[1,12,4096]{2,1,0:T(8,128)(2,1)} %param.6, f32[4096]{0:T(1024)} %param.10, f32[12]{0:T(128)S(1)} %get-tuple-element.22), kind=kLoop, calls=%fused_computation.13 | loop fusion | flops 196608 | bytes 213040 | tf_op jit(solution)/shard_map/convert_element_type | solution.py:21
  3.4 0.9 %fusion.10 = bf16[12,2]{1,0:T(8,128)(2,1)S(1)} fusion(s32[2]{0:T(128)S(1)} %get-tuple-element.26, s32[12]{0:T(128)} %bitcast.68, s32[2]{0:T(128)S(1)} %get-tuple-element.27, s32[12]{0:T(128)S(1)} %bitcast_sign_fusion), kind=kLoop, calls=%fused_computation.27 | loop fusion | flops 456 | bytes 160 | tf_op jit(solution)/shard_map/convert_element_type | solution.py:53
  4.3 34.8 %all-gather = bf16[8,12,4224]{2,1,0:T(8,128)(2,1)S(1)} all-gather(bf16[1,12,4224]{2,1,0:T(8,128)(2,1)S(1)} %fusion.8), channel_id=1, replica_groups=mesh['vocab'=8,'grp'=4] {'vocab'}, dimensions={0}, use_global_device_ids=true | all-gather | bytes 912384 | tf_op jit(solution)/shard_map/all_gather | solution.py:55
  39.1 0.2 reshape.338
  39.3 0.0 copy-start
  39.3 0.1 multiply_reduce_fusion.1
  39.4 0.0 copy-done.1
  39.5 0.1 select_reduce_fusion
  39.6 0.5 copy-done
  40.2 23.5 %fusion.21 = (f32[96]{0:T(128)S(1)}, f32[96,8192]{1,0:T(8,128)S(1)}) fusion(bf16[4096,8192]{1,0:T(8,128)(2,1)} %param.11, bf16[96,4224]{1,0:T(8,128)(2,1)} %copy-done), kind=kOutput, calls=%fused_computation.78 | convolution fusion | flops 6443237376 | bytes 71041408 | tf_op jit(solution)/shard_map/dot_general | solution.py:26
  63.7 0.0 copy-start.2
  63.7 0.1 stack.13
  63.8 0.9 %fusion = (f32[96]{0:T(128)S(1)}, f32[96]{0:T(128)S(1)}) fusion(f32[96,8192]{1,0:T(8,128)S(1)} %get-tuple-element.25, f32[96]{0:T(128)S(1)} %get-tuple-element.24), kind=kLoop, calls=%fused_computation.4 | loop fusion | flops 3145536 | bytes 3146880 | tf_op jit(solution)/shard_map/reduce_sum | solution.py:35
  64.7 1.5 %gather_fusion.1 = f32[96]{0:T(128)S(1)} fusion(f32[96,8192]{1,0:T(8,128)S(1)} %get-tuple-element.25, s32[96]{0:T(128)S(1)} %or_bitcast_fusion), kind=kCustom, calls=%fused_computation.1 | custom fusion | bytes 1536 | tf_op jit(solution)/shard_map/jit(take_along_axis)/gather | solution.py:32
  66.2 0.1 gather.11
  66.3 0.1 min.16
  66.3 0.1 and.161
  66.4 0.1 stack.14
  66.5 0.1 stack.15
  66.6 0.6 dynamic_slice.12
  67.2 0.6 iota_compare_fusion.2
  67.9 0.6 gather_fusion
  68.5 0.1 select_bitcast_fusion
  68.6 0.1 broadcast_select_fusion
  68.7 0.6 maximum_bitcast_fusion
  69.3 5.3 %all-to-all-start = ((f32[8,5,12]{2,1,0:T(8,128)}), f32[8,5,12]{2,1,0:T(8,128)S(1)}, u32[]{:S(2)}, u32[]{:S(2)}) async-start(f32[8,5,12]{2,1,0:T(8,128)} %maximum_bitcast_fusion), calls=%async_computation | async-start | bytes 65536 | tf_op jit(solution)/shard_map/all_to_all | solution.py:69
  74.6 0.6 dynamic_slice.11
  75.2 0.0 copy-done.2
  75.2 1.3 %fusion.15 = s32[]{:T(128)} fusion(s32[1,8]{1,0:T(1,128)S(1)} %copy-done.2, s32[]{:T(128)} %bitcast.1), kind=kLoop, calls=%fused_computation.57 | loop fusion | flops 23 | bytes 40 | tf_op jit(solution)/shard_map/reduce_sum | solution.py:80
  76.5 4.8 %all-to-all-done = f32[8,5,12]{2,1,0:T(8,128)S(1)} async-done(((f32[8,5,12]{2,1,0:T(8,128)}), f32[8,5,12]{2,1,0:T(8,128)S(1)}, u32[]{:S(2)}, u32[]{:S(2)}) %all-to-all-start) | async-done | bytes 1952 | tf_op jit(solution)/shard_map/all_to_all | solution.py:69
  81.3 1.1 %bitcast_select_fusion = f32[1,12]{1,0:T(1,128)} fusion(f32[12]{0:T(128)S(1)} %get-tuple-element.18, s32[]{:T(128)} %fusion.15), kind=kLoop, calls=%fused_computation.59 | loop fusion | flops 24 | bytes 100 | tf_op jit(solution)/shard_map/mul | solution.py:85
  82.5 1.2 %fusion.17 = (f32[1,12]{1,0:T(1,128)}, f32[1,12]{1,0:T(1,128)}, f32[1,12]{1,0:T(1,128)}) fusion(f32[12]{0:T(128)S(1)} %get-tuple-element.17, f32[12]{0:T(128)S(1)} %get-tuple-element.9, f32[12]{0:T(128)S(1)} %get-tuple-element.10, s32[]{:T(128)} %fusion.15, f32[12]{0:T(128)S(1)} %get-tuple-element.16), kind=kLoop, calls=%fused_computation.61 | loop fusion | flops 108 | bytes 340 | tf_op jit(solution)/shard_map/mul | solution.py:84
  (16 shorter events, 0.2 us)
Async XLA Ops:
  0.6 38.8 %copy-start.1 = (s32[4,8]{1,0:T(4,128)S(1)}, s32[4,8]{1,0:T(4,128)}, u32[]{:S(2)}) copy-start(s32[4,8]{1,0:T(4,128)} %param.9) | copy-start | bytes 388
  39.3 0.9 %copy-start = (bf16[96,4224]{1,0:T(8,128)(2,1)}, bf16[96,4224]{1,0:T(8,128)(2,1)S(1)}, u32[]{:S(2)}) copy-start(bf16[96,4224]{1,0:T(8,128)(2,1)S(1)} %reshape.338) | copy-start | bytes 2433028
  63.7 11.5 %copy-start.2 = (s32[1,8]{1,0:T(1,128)S(1)}, s32[1,8]{1,0:T(1,128)}, u32[]{:S(2)}) copy-start(s32[1,8]{1,0:T(1,128)} %param.8) | copy-start | bytes 100
  69.3 12.0 %all-to-all-start = ((f32[8,5,12]{2,1,0:T(8,128)}), f32[8,5,12]{2,1,0:T(8,128)S(1)}, u32[]{:S(2)}, u32[]{:S(2)}) async-start(f32[8,5,12]{2,1,0:T(8,128)} %maximum_bitcast_fusion), calls=%async_computation | async-start | bytes 65536 | tf_op jit(solution)/shard_map/all_to_all | solution.py:69

commit v2 on v1

--- a/solution.py
+++ b/solution.py
@@ -6,6 +6,7 @@
 EPSILON = 1e-05
 RADIX = 256
 LANES = 128
+RING_LIMIT = 8
 
 
 def digit_count(total):
@@ -22,8 +23,15 @@
     return (normed, jnp.sqrt(mean_square))
 
 
-def partial_stats(normed, columns, token_ids, offset):
-    logits = jnp.dot(normed, columns, preferred_element_type=jnp.float32)
+def ring_gather(block, size):
+    pieces = [block]
+    for shift in range(1, size):
+        pieces.append(lax.ppermute(block, "vocab", [(i, (i + shift) % size) for i in range(size)]))
+    return jnp.concatenate(pieces, axis=0)
+
+
+def partial_stats(partial_logits, normed, columns, token_ids, offset):
+    logits = partial_logits + jnp.dot(normed, columns, preferred_element_type=jnp.float32)
     local_max = jnp.max(logits, axis=1)
     weights = jnp.exp(logits - local_max[:, None])
     width = columns.shape[1]
@@ -52,11 +60,27 @@
     place = RADIX ** jnp.arange(digits, dtype=jnp.int32)
     coded = ((target_ids[0][:, None] // place[None, :]) % RADIX).astype(jnp.bfloat16)
     coded = jnp.pad(coded, ((0, 0), (0, LANES - digits)))
-    packed = lax.all_gather(jnp.concatenate([normed, coded], axis=1), "vocab", axis=0, tiled=True)
-    group_normed = packed[:, :features]
-    group_ids = jnp.sum(packed[:, features : features + digits].astype(jnp.int32) * place[None, :], axis=1)
+    half = features // 2
+    first = jnp.concatenate([normed[:, :half], coded], axis=1)
+    second = normed[:, half:]
+    if vocab_size <= RING_LIMIT:
+        gathered_first = ring_gather(first, vocab_size)
+        gathered_second = ring_gather(second, vocab_size)
+        arrival = (vocab_index - block_ids) % vocab_size
+    else:
+        gathered_first = lax.all_gather(first, "vocab", axis=0, tiled=True)
+        gathered_second = lax.all_gather(second, "vocab", axis=0, tiled=True)
+        arrival = block_ids
+    group_ids = jnp.sum(
+        gathered_first[:, half : half + digits].astype(jnp.int32) * place[None, :], axis=1
+    )
     offset = vocab_index * width
-    local_max, sums, expected, target = partial_stats(group_normed, head, group_ids, offset)
+    partial_logits = jnp.dot(
+        gathered_first[:, :half], head[:half], preferred_element_type=jnp.float32
+    )
+    local_max, sums, expected, target = partial_stats(
+        partial_logits, gathered_second, head[half:], group_ids, offset
+    )
     rows = vocab_size * count
     home = own_order[vocab_index]
     root_rows = jnp.where(block_ids[:, None] == home, root_mean[None, :], 0.0)
@@ -64,7 +88,7 @@
     source_of = jnp.sum(
         jnp.where(own_order[None, :] == block_ids[:, None], block_ids[None, :], 0), axis=1
     )
-    routed = jnp.take(terms, source_of, axis=1)
+    routed = jnp.take(terms, arrival[source_of], axis=1)
     payload = jnp.concatenate([routed, root_rows[None]], axis=0).transpose(1, 0, 2)
     received = lax.all_to_all(payload, "vocab", 0, 0, tiled=True)
     shard_max, shard_sums, shard_expected, shard_target, shard_root = (

time: 84 us -> 86.3 us (1.027)
  blocking collectives: 34.8 us -> 0 us
  starting transfers between devices: 5.33 us -> 27.4 us
  matrix products: 23.5 us -> 29.5 us
  waiting for transfers between devices: 4.8 us -> 10.2 us
  local copies, waits for them, and re-layouts: 4.45 us -> 8.01 us
    all_gather x1 -> x0, blocking collectives: 34.8 us -> none  [shards(): lax.all_gather(jnp.concatenate([normed, coded], axis=1), 'vocab', axis=0,...]
    ppermute x0 -> x14, starting transfers between devices: none -> 21.8 us  [ring_gather(): lax.ppermute(block, 'vocab', [(i, (i + shift) % size) for i in range(size)])]
    dot_general x1 -> x2, matrix products: 23.5 us -> 29.5 us  [the longest x1 15.1 us: partial_stats(): jnp.dot(normed, columns, preferred_element_type=jnp.float32)]
    ppermute x0 -> x14, waiting for transfers between devices: none -> 4.83 us  [ring_gather(): lax.ppermute(block, 'vocab', [(i, (i + shift) % size) for i in range(size)])]
    concatenate x0 -> x2, local copies, waits for them, and re-layouts: none -> 1.67 us  [ring_gather(): return jnp.concatenate(pieces, axis=0)]
  transfers between devices with their start and end apart: 1 -> 15, of which waited for: 1 -> 3; matrix products, arithmetic and copies ran while one was open for 2% -> 26% of each run, Pallas kernels for 0% -> 0%
where the time goes in v2:
time: 86.3 us; the launch traced here: 86 us
  matrix products  29.5 us (34%)
  starting transfers between devices  27.4 us (32%)
  waiting for transfers between devices  10.2 us (12%)
  other arithmetic  9.99 us (12%)
  local copies, waits for them, and re-layouts  8.01 us (9%)
    ppermute x14, starting transfers between devices, ring_gather(): lax.ppermute(block, 'vocab', [(i, (i + shift) % size) for i in range(size)])  21.8 us
    dot_general x1, matrix products, partial_stats(): jnp.dot(normed, columns, preferred_element_type=jnp.float32)  15.1 us
    dot_general x1, matrix products, shards(): jnp.dot(gathered_first[:, :half], head[:half], preferred_element_type=jnp...  14.4 us
    all_to_all x1, starting transfers between devices, shards(): received = lax.all_to_all(payload, 'vocab', 0, 0, tiled=True)  5.64 us
    all_to_all x1, waiting for transfers between devices, shards(): received = lax.all_to_all(payload, 'vocab', 0, 0, tiled=True)  5.38 us
    ppermute x14, waiting for transfers between devices, ring_gather(): lax.ppermute(block, 'vocab', [(i, (i + shift) % size) for i in range(size)])  4.83 us
  transfers between devices with their start and end apart: 15, of which 3 were waited for; matrix products, arithmetic and copies ran while one was open for 26% of the time, Pallas kernels for 0%

profile of v2, /device:TPU:0, one launch (start us, length us, event | category | flops | bytes accessed | tf_op | source)
XLA Modules:
  0.0 86.0 jit_solution(6832421656974903303)
XLA Ops:
  0.6 1.1 %fusion.9 = f32[12]{0:T(128)S(1)} fusion(bf16[1,12,4096]{2,1,0:T(8,128)(2,1)} %param.6), kind=kLoop, calls=%fused_computation.14 | loop fusion | flops 147444 | bytes 98352 | tf_op jit(solution)/shard_map/reduce_sum | solution.py:21
  1.7 1.0 %fusion.11 = bf16[12,4096]{1,0:T(8,128)(2,1)S(1)} fusion(bf16[1,12,4096]{2,1,0:T(8,128)(2,1)} %param.6, f32[4096]{0:T(1024)} %param.10, f32[12]{0:T(128)S(1)} %get-tuple-element.24), kind=kLoop, calls=%fused_computation.16 | loop fusion | flops 196608 | bytes 213040 | tf_op jit(solution)/shard_map/convert_element_type | solution.py:22
  2.7 4.1 %collective-permute-start.10 = (bf16[12,2048]{1,0:T(8,128)(2,1)S(1)}, bf16[12,2048]{1,0:T(8,128)(2,1)S(1)}, u32[]{:S(2)}, u32[]{:S(2)}) collective-permute-start(bf16[12,2048]{1,0:T(8,128)(2,1)S(1)} %get-tuple-element.13), channel_id=1, source_target_pairs={{0,16},{4,20},{8,24},{12,28},{16,0},{20,4},{24,8},{28,12},{1,17},{... | collective-permute-start | bytes 147464 | tf_op jit(solution)/shard_map/ppermute | solution.py:29
  6.8 1.3 %collective-permute-start.11 = (bf16[12,2048]{1,0:T(8,128)(2,1)S(1)}, bf16[12,2048]{1,0:T(8,128)(2,1)S(1)}, u32[]{:S(2)}, u32[]{:S(2)}) collective-permute-start(bf16[12,2048]{1,0:T(8,128)(2,1)S(1)} %get-tuple-element.13), channel_id=1, source_target_pairs={{0,20},{4,24},{8,28},{12,0},{16,4},{20,8},{24,12},{28,16},{1,21},{... | collective-permute-start | bytes 147464 | tf_op jit(solution)/shard_map/ppermute | solution.py:29
  8.1 3.6 %collective-permute-start.12 = (bf16[12,2048]{1,0:T(8,128)(2,1)S(1)}, bf16[12,2048]{1,0:T(8,128)(2,1)S(1)}, u32[]{:S(2)}, u32[]{:S(2)}) collective-permute-start(bf16[12,2048]{1,0:T(8,128)(2,1)S(1)} %get-tuple-element.13), channel_id=1, source_target_pairs={{0,24},{4,28},{8,0},{12,4},{16,8},{20,12},{24,16},{28,20},{1,25},{... | collective-permute-start | bytes 147464 | tf_op jit(solution)/shard_map/ppermute | solution.py:29
  11.7 0.5 collective-permute-start.13
  12.2 0.7 bitcast_sign_fusion
  12.9 0.9 fusion.15
  13.8 1.6 %collective-permute-start = (bf16[12,2176]{1,0:T(8,128)(2,1)S(1)}, bf16[12,2176]{1,0:T(8,128)(2,1)S(1)}, u32[]{:S(2)}, u32[]{:S(2)}) collective-permute-start(bf16[12,2176]{1,0:T(8,128)(2,1)S(1)} %fusion.13), channel_id=1, source_target_pairs={{0,4},{4,8},{8,12},{12,16},{16,20},{20,24},{24,28},{28,0},{1,5},{5... | collective-permute-start | bytes 156680 | tf_op jit(solution)/shard_map/ppermute | solution.py:29
  15.4 0.7 dynamic-slice_bitcast_fusion
  16.0 0.1 select_reduce_fusion
  16.2 0.6 gather_fusion
  16.8 1.3 %dynamic_slice.12 = s32[1,1]{1,0:T(1,128)} dynamic-slice(s32[4,8]{1,0:T(4,128)} %param.9, s32[]{:T(128)S(6)} %select_n.262, s32[]{:T(128)S(6)} %select_n.263), dynamic_slice_sizes={1,1} | dynamic-slice | bytes 12 | tf_op jit(solution)/shard_map/dynamic_slice | solution.py:85
  18.1 0.6 iota_compare_fusion.2
  18.8 0.1 broadcast_select_fusion
  18.9 0.0 collective-permute-done.10
  18.9 0.1 collective-permute-start.1
  18.9 0.0 collective-permute-done.11
  18.9 0.8 collective-permute-start.7
  19.8 0.0 collective-permute-done.12
  19.8 0.7 collective-permute-start.8
  20.5 0.0 collective-permute-done.13
  20.5 4.3 %collective-permute-start.9 = (bf16[12,2048]{1,0:T(8,128)(2,1)S(1)}, bf16[12,2048]{1,0:T(8,128)(2,1)S(1)}, u32[]{:S(2)}, u32[]{:S(2)}) collective-permute-start(bf16[12,2048]{1,0:T(8,128)(2,1)S(1)} %get-tuple-element.13), channel_id=1, source_target_pairs={{0,12},{4,16},{8,20},{12,24},{16,28},{20,0},{24,4},{28,8},{1,13},{... | collective-permute-start | bytes 147464 | tf_op jit(solution)/shard_map/ppermute | solution.py:29
  24.8 0.6 dynamic_slice.11
  25.4 1.3 %collective-permute-done.7 = bf16[12,2048]{1,0:T(8,128)(2,1)S(1)} collective-permute-done((bf16[12,2048]{1,0:T(8,128)(2,1)S(1)}, bf16[12,2048]{1,0:T(8,128)(2,1)S(1)}, u32[]{:S(2)}, u32[]{:S(2)}) %collective-permute-start.7) | collective-permute-done | bytes 49184 | tf_op jit(solution)/shard_map/ppermute | solution.py:29
  26.7 0.0 collective-permute-start.2
  26.7 0.0 collective-permute-done.8
  26.7 1.6 %collective-permute-start.3 = (bf16[12,2176]{1,0:T(8,128)(2,1)S(1)}, bf16[12,2176]{1,0:T(8,128)(2,1)S(1)}, u32[]{:S(2)}, u32[]{:S(2)}) collective-permute-start(bf16[12,2176]{1,0:T(8,128)(2,1)S(1)} %fusion.13), channel_id=1, source_target_pairs={{0,16},{4,20},{8,24},{12,28},{16,0},{20,4},{24,8},{28,12},{1,17},{... | collective-permute-start | bytes 156680 | tf_op jit(solution)/shard_map/ppermute | solution.py:29
  28.3 3.5 %collective-permute-done.9 = bf16[12,2048]{1,0:T(8,128)(2,1)S(1)} collective-permute-done((bf16[12,2048]{1,0:T(8,128)(2,1)S(1)}, bf16[12,2048]{1,0:T(8,128)(2,1)S(1)}, u32[]{:S(2)}, u32[]{:S(2)}) %collective-permute-start.9) | collective-permute-done | bytes 49184 | tf_op jit(solution)/shard_map/ppermute | solution.py:29
  31.8 0.0 collective-permute-start.4
  31.8 0.7 concatenate.15
  32.5 0.0 collective-permute-done
  32.5 3.2 %collective-permute-start.5 = (bf16[12,2176]{1,0:T(8,128)(2,1)S(1)}, bf16[12,2176]{1,0:T(8,128)(2,1)S(1)}, u32[]{:S(2)}, u32[]{:S(2)}) collective-permute-start(bf16[12,2176]{1,0:T(8,128)(2,1)S(1)} %fusion.13), channel_id=1, source_target_pairs={{0,24},{4,28},{8,0},{12,4},{16,8},{20,12},{24,16},{28,20},{1,25},{... | collective-permute-start | bytes 156680 | tf_op jit(solution)/shard_map/ppermute | solution.py:29
  35.8 0.0 collective-permute-done.1
  35.8 0.0 collective-permute-start.6
  35.8 15.1 %fusion = f32[96,8192]{1,0:T(8,128)} fusion(bf16[96,2048]{1,0:T(8,128)(2,1)S(1)} %concatenate.15, bf16[4096,8192]{1,0:T(8,128)(2,1)} %param.11), kind=kOutput, calls=%fused_computation.3 | convolution fusion | flops 3221225472 | bytes 37093376 | tf_op jit(solution)/shard_map/dot_general | solution.py:34
  50.8 0.0 collective-permute-done.2
  50.8 0.0 collective-permute-done.3
  50.8 0.0 collective-permute-done.4
  50.9 0.0 collective-permute-done.5
  50.9 0.0 collective-permute-done.6
  50.9 0.9 %concatenate.14 = bf16[96,2176]{1,0:T(8,128)(2,1)S(1)} concatenate(bf16[12,2176]{1,0:T(8,128)(2,1)S(1)} %fusion.13, bf16[12,2176]{1,0:T(8,128)(2,1)S(1)} %collective-permute-done, bf16[12,2176]{1,0:T(8,128)(2,1)S(1)} %collective-permute-done.1, bf16[12,2176]{1,0:T(8,128)(2,1)S(1)} %collective-permute-done.2, bf16[12,2176]{1,0:T(8,128)(2,1)S(1)} %collective-permute-done.3, ...), dimensions={0} | concatenate | bytes 835584 | tf_op jit(solution)/shard_map/concatenate | solution.py:30
  51.8 0.0 copy-start
  51.8 0.1 multiply_reduce_fusion.1
  51.9 0.6 copy-done
  52.6 14.4 %fusion.29 = (f32[96]{0:T(128)S(1)}, f32[96,8192]{1,0:T(8,128)S(1)}) fusion(f32[96,8192]{1,0:T(8,128)} %fusion, bf16[4096,8192]{1,0:T(8,128)(2,1)} %param.11, bf16[96,2176]{1,0:T(8,128)(2,1)} %copy-done), kind=kOutput, calls=%fused_computation.90 | convolution fusion | flops 3222798336 | bytes 40239488 | tf_op jit(solution)/shard_map/dot_general | solution.py:78
  67.0 0.0 copy-start.1
  67.0 0.1 stack.13
  67.1 0.9 %fusion.7 = (f32[96]{0:T(128)S(1)}, f32[96]{0:T(128)S(1)}) fusion(f32[96,8192]{1,0:T(8,128)S(1)} %get-tuple-element.27, f32[96]{0:T(128)S(1)} %get-tuple-element.26), kind=kLoop, calls=%fused_computation.10 | loop fusion | flops 3145536 | bytes 3146880 | tf_op jit(solution)/shard_map/reduce_sum | solution.py:43
  68.0 0.1 stack.15
  68.1 0.1 stack.14
  68.2 1.5 %gather_fusion.2 = f32[96]{0:T(128)S(1)} fusion(f32[96,8192]{1,0:T(8,128)S(1)} %get-tuple-element.27, s32[96]{0:T(128)S(1)} %or_bitcast_fusion), kind=kCustom, calls=%fused_computation.2 | custom fusion | bytes 1536 | tf_op jit(solution)/shard_map/jit(take_along_axis)/gather | solution.py:40
  69.7 0.1 gather.17
  69.8 0.1 min.16
  69.9 0.1 and.167
  70.0 0.6 gather_fusion.1
  70.6 0.1 select_bitcast_fusion
  70.7 0.6 maximum_bitcast_fusion
  71.3 5.6 %all-to-all-start = ((f32[8,5,12]{2,1,0:T(8,128)}), f32[8,5,12]{2,1,0:T(8,128)S(1)}, u32[]{:S(2)}, u32[]{:S(2)}) async-start(f32[8,5,12]{2,1,0:T(8,128)} %maximum_bitcast_fusion), calls=%async_computation | async-start | bytes 65536 | tf_op jit(solution)/shard_map/all_to_all | solution.py:93
  76.9 0.0 copy-done.1
  76.9 1.3 %fusion.20 = s32[]{:T(128)} fusion(s32[1,8]{1,0:T(1,128)S(1)} %copy-done.1, s32[]{:T(128)} %bitcast.1), kind=kLoop, calls=%fused_computation.66 | loop fusion | flops 23 | bytes 40 | tf_op jit(solution)/shard_map/reduce_sum | solution.py:104
  78.2 5.4 %all-to-all-done = f32[8,5,12]{2,1,0:T(8,128)S(1)} async-done(((f32[8,5,12]{2,1,0:T(8,128)}), f32[8,5,12]{2,1,0:T(8,128)S(1)}, u32[]{:S(2)}, u32[]{:S(2)}) %all-to-all-start) | async-done | bytes 1952 | tf_op jit(solution)/shard_map/all_to_all | solution.py:93
  83.7 1.1 %bitcast_select_fusion = f32[1,12]{1,0:T(1,128)} fusion(f32[12]{0:T(128)S(1)} %get-tuple-element.20, s32[]{:T(128)} %fusion.20), kind=kLoop, calls=%fused_computation.70 | loop fusion | flops 24 | bytes 100 | tf_op jit(solution)/shard_map/mul | solution.py:109
  84.8 1.2 %fusion.24 = (f32[1,12]{1,0:T(1,128)}, f32[1,12]{1,0:T(1,128)}, f32[1,12]{1,0:T(1,128)}) fusion(f32[12]{0:T(128)S(1)} %get-tuple-element.19, f32[12]{0:T(128)S(1)} %get-tuple-element.9, f32[12]{0:T(128)S(1)} %get-tuple-element.10, s32[]{:T(128)} %fusion.20, f32[12]{0:T(128)S(1)} %get-tuple-element.18), kind=kLoop, calls=%fused_computation.72 | loop fusion | flops 108 | bytes 340 | tf_op jit(solution)/shard_map/mul | solution.py:108
  (19 shorter events, 0.2 us)
Async XLA Ops:
  2.7 16.1 %collective-permute-start.10 = (bf16[12,2048]{1,0:T(8,128)(2,1)S(1)}, bf16[12,2048]{1,0:T(8,128)(2,1)S(1)}, u32[]{:S(2)}, u32[]{:S(2)}) collective-permute-start(bf16[12,2048]{1,0:T(8,128)(2,1)S(1)} %get-tuple-element.13), channel_id=1, source_target_pairs={{0,16},{4,20},{8,24},{12,28},{16,0},{20,4},{24,8},{28,12},{1,17},{... | collective-permute-start | bytes 147464 | tf_op jit(solution)/shard_map/ppermute | solution.py:29
  6.8 12.1 %collective-permute-start.11 = (bf16[12,2048]{1,0:T(8,128)(2,1)S(1)}, bf16[12,2048]{1,0:T(8,128)(2,1)S(1)}, u32[]{:S(2)}, u32[]{:S(2)}) collective-permute-start(bf16[12,2048]{1,0:T(8,128)(2,1)S(1)} %get-tuple-element.13), channel_id=1, source_target_pairs={{0,20},{4,24},{8,28},{12,0},{16,4},{20,8},{24,12},{28,16},{1,21},{... | collective-permute-start | bytes 147464 | tf_op jit(solution)/shard_map/ppermute | solution.py:29
  8.1 11.7 %collective-permute-start.12 = (bf16[12,2048]{1,0:T(8,128)(2,1)S(1)}, bf16[12,2048]{1,0:T(8,128)(2,1)S(1)}, u32[]{:S(2)}, u32[]{:S(2)}) collective-permute-start(bf16[12,2048]{1,0:T(8,128)(2,1)S(1)} %get-tuple-element.13), channel_id=1, source_target_pairs={{0,24},{4,28},{8,0},{12,4},{16,8},{20,12},{24,16},{28,20},{1,25},{... | collective-permute-start | bytes 147464 | tf_op jit(solution)/shard_map/ppermute | solution.py:29
  11.7 8.7 %collective-permute-start.13 = (bf16[12,2048]{1,0:T(8,128)(2,1)S(1)}, bf16[12,2048]{1,0:T(8,128)(2,1)S(1)}, u32[]{:S(2)}, u32[]{:S(2)}) collective-permute-start(bf16[12,2048]{1,0:T(8,128)(2,1)S(1)} %get-tuple-element.13), channel_id=1, source_target_pairs={{0,28},{4,0},{8,4},{12,8},{16,12},{20,16},{24,20},{28,24},{1,29},{... | collective-permute-start | bytes 147464 | tf_op jit(solution)/shard_map/ppermute | solution.py:29
  13.8 18.7 %collective-permute-start = (bf16[12,2176]{1,0:T(8,128)(2,1)S(1)}, bf16[12,2176]{1,0:T(8,128)(2,1)S(1)}, u32[]{:S(2)}, u32[]{:S(2)}) collective-permute-start(bf16[12,2176]{1,0:T(8,128)(2,1)S(1)} %fusion.13), channel_id=1, source_target_pairs={{0,4},{4,8},{8,12},{12,16},{16,20},{20,24},{24,28},{28,0},{1,5},{5... | collective-permute-start | bytes 156680 | tf_op jit(solution)/shard_map/ppermute | solution.py:29
  18.9 16.9 %collective-permute-start.1 = (bf16[12,2176]{1,0:T(8,128)(2,1)S(1)}, bf16[12,2176]{1,0:T(8,128)(2,1)S(1)}, u32[]{:S(2)}, u32[]{:S(2)}) collective-permute-start(bf16[12,2176]{1,0:T(8,128)(2,1)S(1)} %fusion.13), channel_id=1, source_target_pairs={{0,8},{4,12},{8,16},{12,20},{16,24},{20,28},{24,0},{28,4},{1,9},{5... | collective-permute-start | bytes 156680 | tf_op jit(solution)/shard_map/ppermute | solution.py:29
  18.9 7.7 %collective-permute-start.7 = (bf16[12,2048]{1,0:T(8,128)(2,1)S(1)}, bf16[12,2048]{1,0:T(8,128)(2,1)S(1)}, u32[]{:S(2)}, u32[]{:S(2)}) collective-permute-start(bf16[12,2048]{1,0:T(8,128)(2,1)S(1)} %get-tuple-element.13), channel_id=1, source_target_pairs={{0,4},{4,8},{8,12},{12,16},{16,20},{20,24},{24,28},{28,0},{1,5},{5... | collective-permute-start | bytes 147464 | tf_op jit(solution)/shard_map/ppermute | solution.py:29
  19.8 6.9 %collective-permute-start.8 = (bf16[12,2048]{1,0:T(8,128)(2,1)S(1)}, bf16[12,2048]{1,0:T(8,128)(2,1)S(1)}, u32[]{:S(2)}, u32[]{:S(2)}) collective-permute-start(bf16[12,2048]{1,0:T(8,128)(2,1)S(1)} %get-tuple-element.13), channel_id=1, source_target_pairs={{0,8},{4,12},{8,16},{12,20},{16,24},{20,28},{24,0},{28,4},{1,9},{5... | collective-permute-start | bytes 147464 | tf_op jit(solution)/shard_map/ppermute | solution.py:29
  20.5 11.3 %collective-permute-start.9 = (bf16[12,2048]{1,0:T(8,128)(2,1)S(1)}, bf16[12,2048]{1,0:T(8,128)(2,1)S(1)}, u32[]{:S(2)}, u32[]{:S(2)}) collective-permute-start(bf16[12,2048]{1,0:T(8,128)(2,1)S(1)} %get-tuple-element.13), channel_id=1, source_target_pairs={{0,12},{4,16},{8,20},{12,24},{16,28},{20,0},{24,4},{28,8},{1,13},{... | collective-permute-start | bytes 147464 | tf_op jit(solution)/shard_map/ppermute | solution.py:29
  26.7 24.2 %collective-permute-start.2 = (bf16[12,2176]{1,0:T(8,128)(2,1)S(1)}, bf16[12,2176]{1,0:T(8,128)(2,1)S(1)}, u32[]{:S(2)}, u32[]{:S(2)}) collective-permute-start(bf16[12,2176]{1,0:T(8,128)(2,1)S(1)} %fusion.13), channel_id=1, source_target_pairs={{0,12},{4,16},{8,20},{12,24},{16,28},{20,0},{24,4},{28,8},{1,13},{... | collective-permute-start | bytes 156680 | tf_op jit(solution)/shard_map/ppermute | solution.py:29
  26.7 24.2 %collective-permute-start.3 = (bf16[12,2176]{1,0:T(8,128)(2,1)S(1)}, bf16[12,2176]{1,0:T(8,128)(2,1)S(1)}, u32[]{:S(2)}, u32[]{:S(2)}) collective-permute-start(bf16[12,2176]{1,0:T(8,128)(2,1)S(1)} %fusion.13), channel_id=1, source_target_pairs={{0,16},{4,20},{8,24},{12,28},{16,0},{20,4},{24,8},{28,12},{1,17},{... | collective-permute-start | bytes 156680 | tf_op jit(solution)/shard_map/ppermute | solution.py:29
  31.8 19.1 %collective-permute-start.4 = (bf16[12,2176]{1,0:T(8,128)(2,1)S(1)}, bf16[12,2176]{1,0:T(8,128)(2,1)S(1)}, u32[]{:S(2)}, u32[]{:S(2)}) collective-permute-start(bf16[12,2176]{1,0:T(8,128)(2,1)S(1)} %fusion.13), channel_id=1, source_target_pairs={{0,20},{4,24},{8,28},{12,0},{16,4},{20,8},{24,12},{28,16},{1,21},{... | collective-permute-start | bytes 156680 | tf_op jit(solution)/shard_map/ppermute | solution.py:29
  32.5 18.3 %collective-permute-start.5 = (bf16[12,2176]{1,0:T(8,128)(2,1)S(1)}, bf16[12,2176]{1,0:T(8,128)(2,1)S(1)}, u32[]{:S(2)}, u32[]{:S(2)}) collective-permute-start(bf16[12,2176]{1,0:T(8,128)(2,1)S(1)} %fusion.13), channel_id=1, source_target_pairs={{0,24},{4,28},{8,0},{12,4},{16,8},{20,12},{24,16},{28,20},{1,25},{... | collective-permute-start | bytes 156680 | tf_op jit(solution)/shard_map/ppermute | solution.py:29
  35.8 15.1 %collective-permute-start.6 = (bf16[12,2176]{1,0:T(8,128)(2,1)S(1)}, bf16[12,2176]{1,0:T(8,128)(2,1)S(1)}, u32[]{:S(2)}, u32[]{:S(2)}) collective-permute-start(bf16[12,2176]{1,0:T(8,128)(2,1)S(1)} %fusion.13), channel_id=1, source_target_pairs={{0,28},{4,0},{8,4},{12,8},{16,12},{20,16},{24,20},{28,24},{1,29},{... | collective-permute-start | bytes 156680 | tf_op jit(solution)/shard_map/ppermute | solution.py:29
  51.8 0.8 copy-start
  67.0 9.9 %copy-start.1 = (s32[1,8]{1,0:T(1,128)S(1)}, s32[1,8]{1,0:T(1,128)}, u32[]{:S(2)}) copy-start(s32[1,8]{1,0:T(1,128)} %param.8) | copy-start | bytes 100
  71.3 12.3 %all-to-all-start = ((f32[8,5,12]{2,1,0:T(8,128)}), f32[8,5,12]{2,1,0:T(8,128)S(1)}, u32[]{:S(2)}, u32[]{:S(2)}) async-start(f32[8,5,12]{2,1,0:T(8,128)} %maximum_bitcast_fusion), calls=%async_computation | async-start | bytes 65536 | tf_op jit(solution)/shard_map/all_to_all | solution.py:93

commit v3 on v1

--- a/solution.py
+++ b/solution.py
@@ -41,8 +41,11 @@
 def shards(states, target_ids, lengths, order, gain, head):
     count = states.shape[1]
     vocab_size = lax.axis_size("vocab")
+    group_size = lax.axis_size("grp")
     vocab_index = lax.axis_index("vocab")
     group_index = lax.axis_index("grp")
+    core = group_index % 2
+    pair_base = group_index - core
     own_order = lax.dynamic_index_in_dim(order, group_index, 0, keepdims=False)
     block_ids = jnp.arange(vocab_size, dtype=jnp.int32)
     normed, root_mean = normalize(states[0], gain)
@@ -53,20 +56,32 @@
     coded = ((target_ids[0][:, None] // place[None, :]) % RADIX).astype(jnp.bfloat16)
     coded = jnp.pad(coded, ((0, 0), (0, LANES - digits)))
     packed = lax.all_gather(jnp.concatenate([normed, coded], axis=1), "vocab", axis=0, tiled=True)
-    group_normed = packed[:, :features]
-    group_ids = jnp.sum(packed[:, features : features + digits].astype(jnp.int32) * place[None, :], axis=1)
-    offset = vocab_index * width
-    local_max, sums, expected, target = partial_stats(group_normed, head, group_ids, offset)
-    rows = vocab_size * count
+    partner = lax.ppermute(
+        packed, "grp", [(g, g ^ 1) for g in range(group_size)]
+    )
+    pair_rows = jnp.where(core == 0, jnp.concatenate([packed, partner]), jnp.concatenate([partner, packed]))
+    pair_normed = pair_rows[:, :features]
+    pair_ids = jnp.sum(pair_rows[:, features : features + digits].astype(jnp.int32) * place[None, :], axis=1)
+    span = width // 2
+    columns = lax.dynamic_slice_in_dim(head, core * span, span, 1)
+    offset = vocab_index * width + core * span
+    local_max, sums, expected, target = partial_stats(pair_normed, columns, pair_ids, offset)
+    terms = jnp.stack([local_max, sums, expected, target]).reshape(4, 2, vocab_size, count)
+    pair_order = lax.dynamic_slice_in_dim(order, pair_base, 2, 0)
+    route = (pair_order[:, None, :] == block_ids[None, :, None]).astype(jnp.float32)
+    routed = jnp.einsum("cjs,kcsr->jckr", route, terms, precision=lax.Precision.HIGHEST)
+    group_ids = jnp.arange(group_size, dtype=jnp.int32)
+    same_pair = (group_ids // 2 == pair_base // 2)[None, :, None, None]
+    routed = jnp.take(routed, group_ids % 2, axis=1)
+    stat_ids = jnp.arange(4, dtype=jnp.int32)[None, None, :, None]
+    fill = jnp.where(stat_ids == 0, jnp.finfo(jnp.float32).min, 0.0)
+    routed = jnp.where(same_pair, routed, fill)
     home = own_order[vocab_index]
-    root_rows = jnp.where(block_ids[:, None] == home, root_mean[None, :], 0.0)
-    terms = jnp.stack([local_max, sums, expected, target]).reshape(4, vocab_size, count)
-    source_of = jnp.sum(
-        jnp.where(own_order[None, :] == block_ids[:, None], block_ids[None, :], 0), axis=1
-    )
-    routed = jnp.take(terms, source_of, axis=1)
-    payload = jnp.concatenate([routed, root_rows[None]], axis=0).transpose(1, 0, 2)
-    received = lax.all_to_all(payload, "vocab", 0, 0, tiled=True)
+    root_slot = (block_ids[:, None] == home) & (group_ids[None, :] == group_index)
+    root_rows = jnp.where(root_slot[:, :, None], root_mean[None, None, :], 0.0)
+    payload = jnp.concatenate([routed, root_rows[:, :, None, :]], axis=2)
+    payload = payload.reshape(vocab_size * group_size, 5, count)
+    received = lax.all_to_all(payload, ("vocab", "grp"), 0, 0, tiled=True)
     shard_max, shard_sums, shard_expected, shard_target, shard_root = (
         received[:, 0], received[:, 1], received[:, 2], received[:, 3], received[:, 4]
     )
@@ -76,7 +91,7 @@
     own_expected = jnp.sum(shard_expected * scale, axis=0)
     own_target = jnp.sum(shard_target, axis=0)
     own_root = jnp.sum(shard_root, axis=0)
-    source_block = source_of[vocab_index]
+    source_block = jnp.sum(jnp.where(own_order == vocab_index, block_ids, 0))
     length_own = jnp.sum(jnp.where(block_ids == source_block, lengths[0], 0))
     keep = (jnp.arange(count, dtype=jnp.int32) < length_own).astype(jnp.float32)
     log_total = jnp.log(totals)

time: 84 us -> 79.2 us (0.943)
  matrix products: 23.5 us -> 14.7 us
  waiting for transfers between devices: 4.8 us -> 6.95 us
  local copies, waits for them, and re-layouts: 4.45 us -> 5.98 us
    dot_general x1, matrix products: 23.5 us -> 14.5 us  [partial_stats(): logits = jnp.dot(normed, columns, preferred_element_type=jnp.float32)]
    all_to_all x1, waiting for transfers between devices: 4.8 us -> 6.95 us  [shards(): received = lax.all_to_all(payload, ('vocab', 'grp'), 0, 0, tiled=True)]
  transfers between devices with their start and end apart: 1 -> 2, of which waited for: 1 -> 1; matrix products, arithmetic and copies ran while one was open for 2% -> 5% of each run, Pallas kernels for 0% -> 0%
where the time goes in v3:
time: 79.2 us; the launch traced here: 78.9 us
  blocking collectives  34.8 us (44%)
  matrix products  14.7 us (19%)
  other arithmetic  10 us (13%)
  waiting for transfers between devices  6.95 us (9%)
  local copies, waits for them, and re-layouts  5.98 us (8%)
  starting transfers between devices  5.46 us (7%)
  between operations  0.98 us (1%)
    all_gather x1, blocking collectives, shards(): lax.all_gather(jnp.concatenate([normed, coded], axis=1), 'vocab', axis=0,...  34.8 us
    dot_general x1, matrix products, partial_stats(): logits = jnp.dot(normed, columns, preferred_element_type=jnp.float32)  14.5 us
    all_to_all x1, waiting for transfers between devices, shards(): received = lax.all_to_all(payload, ('vocab', 'grp'), 0, 0, tiled=True)  6.95 us
    all_to_all x1, starting transfers between devices, shards(): received = lax.all_to_all(payload, ('vocab', 'grp'), 0, 0, tiled=True)  5.39 us
    gather x2, local copies, waits for them, and re-layouts, partial_stats(): jnp.take_along_axis(logits, jnp.clip(within, 0, width - 1)[:, None], axis=1)  1.99 us
  transfers between devices with their start and end apart: 2, of which 1 were waited for; matrix products, arithmetic and copies ran while one was open for 5% of the time, Pallas kernels for 0%

profile of v3, /device:TPU:0, one launch (start us, length us, event | category | flops | bytes accessed | tf_op | source)
XLA Modules:
  0.0 78.9 jit_solution(4403413902954407390)
XLA Ops:
  0.6 0.0 copy-start.1
  0.7 0.7 bitcast_sign_fusion
  1.3 1.0 %fusion.5 = f32[12]{0:T(128)S(1)} fusion(bf16[1,12,4096]{2,1,0:T(8,128)(2,1)} %param.6), kind=kLoop, calls=%fused_computation.14 | loop fusion | flops 147444 | bytes 98352 | tf_op jit(solution)/shard_map/reduce_sum | solution.py:20
  2.4 1.0 %fusion.7 = bf16[12,4096]{1,0:T(8,128)(2,1)S(1)} fusion(bf16[1,12,4096]{2,1,0:T(8,128)(2,1)} %param.6, f32[4096]{0:T(1024)} %param.10, f32[12]{0:T(128)S(1)} %get-tuple-element.18), kind=kLoop, calls=%fused_computation.16 | loop fusion | flops 196608 | bytes 213040 | tf_op jit(solution)/shard_map/convert_element_type | solution.py:21
  3.4 0.9 %fusion.18 = bf16[12,2]{1,0:T(8,128)(2,1)S(1)} fusion(s32[2]{0:T(128)S(1)} %get-tuple-element.22, s32[12]{0:T(128)} %bitcast.68, s32[2]{0:T(128)S(1)} %get-tuple-element.23, s32[12]{0:T(128)S(1)} %bitcast_sign_fusion), kind=kLoop, calls=%fused_computation.40 | loop fusion | flops 456 | bytes 160 | tf_op jit(solution)/shard_map/convert_element_type | solution.py:56
  4.3 34.8 %all-gather = bf16[8,12,4224]{2,1,0:T(8,128)(2,1)S(1)} all-gather(bf16[1,12,4224]{2,1,0:T(8,128)(2,1)S(1)} %fusion.9), channel_id=1, replica_groups=mesh['vocab'=8,'grp'=4] {'vocab'}, dimensions={0}, use_global_device_ids=true | all-gather | bytes 912384 | tf_op jit(solution)/shard_map/all_gather | solution.py:58
  39.1 0.2 reshape.400
  39.3 0.1 collective-permute-start
  39.4 0.0 copy-done.1
  39.4 0.6 dynamic_slice.16
  40.0 0.6 iota_compare_fusion.3
  40.7 0.1 broadcast_in_dim.101
  40.8 0.1 broadcast_in_dim.104
  40.9 0.1 and.229
  41.0 0.1 and.230
  41.1 0.1 and.232
  41.2 0.6 fusion.34
  41.8 0.1 broadcast_select_fusion
  41.9 0.0 collective-permute-done
  41.9 0.3 maximum_select_fusion
  42.2 0.0 copy-start
  42.2 0.1 multiply_reduce_fusion.1
  42.4 1.0 %copy-done = bf16[192,4224]{1,0:T(8,128)(2,1)} copy-done((bf16[192,4224]{1,0:T(8,128)(2,1)}, bf16[192,4224]{1,0:T(8,128)(2,1)S(1)}, u32[]{:S(2)}) %copy-start) | copy-done | bytes 1622040
  43.4 14.5 %fusion.38 = (f32[192]{0:T(256)S(1)}, f32[192,4096]{1,0:T(8,128)S(1)}) fusion(bf16[4096,8192]{1,0:T(8,128)(2,1)} %param.11, s32[]{:T(128)S(6)} %select_n.306, bf16[192,4224]{1,0:T(8,128)(2,1)} %copy-done), kind=kOutput, calls=%fused_computation.104 | convolution fusion | flops 6443237376 | bytes 38273796 | tf_op jit(solution)/shard_map/dot_general | solution.py:26
  58.0 0.0 copy-start.2
  58.0 0.1 stack.13
  58.1 0.9 %fusion.2 = (f32[192]{0:T(256)S(1)}, f32[192]{0:T(256)S(1)}) fusion(f32[192,4096]{1,0:T(8,128)S(1)} %get-tuple-element.21, f32[192]{0:T(256)S(1)} %get-tuple-element.20), kind=kLoop, calls=%fused_computation.6 | loop fusion | flops 3145344 | bytes 3148032 | tf_op jit(solution)/shard_map/reduce_sum | solution.py:35
  59.0 0.1 stack.14
  59.0 0.1 stack.15
  59.1 0.1 min.16
  59.3 1.9 %gather_fusion.1 = f32[192]{0:T(256)S(1)} fusion(f32[192,4096]{1,0:T(8,128)S(1)} %get-tuple-element.21, s32[192]{0:T(256)S(1)} %bitcast.60), kind=kCustom, calls=%fused_computation.1 | custom fusion | bytes 3072 | tf_op jit(solution)/shard_map/jit(take_along_axis)/gather | solution.py:32
  61.2 0.1 gather.13
  61.3 0.1 and.226
  61.4 0.1 convolution_bitcast_fusion
  61.5 0.6 gather_fusion
  62.2 0.1 select_select_fusion
  62.3 0.7 copy.14
  63.0 5.4 %all-to-all-start = ((f32[32,5,12]{2,1,0:T(8,128)}), f32[32,5,12]{2,1,0:T(8,128)S(1)}, u32[]{:S(2)}, u32[]{:S(2)}) async-start(f32[32,5,12]{2,1,0:T(8,128)} %copy.14), calls=%async_computation | async-start | bytes 262144 | tf_op jit(solution)/shard_map/all_to_all | solution.py:84
  68.3 0.0 copy-done.2
  68.4 1.3 %fusion.30 = s32[]{:T(128)} fusion(s32[1,8]{1,0:T(1,128)S(1)} %copy-done.2, s32[]{:T(128)} %fusion.34), kind=kLoop, calls=%fused_computation.84 | loop fusion | flops 23 | bytes 40 | tf_op jit(solution)/shard_map/reduce_sum | solution.py:95
  69.6 6.9 %all-to-all-done = f32[32,5,12]{2,1,0:T(8,128)S(1)} async-done(((f32[32,5,12]{2,1,0:T(8,128)}), f32[32,5,12]{2,1,0:T(8,128)S(1)}, u32[]{:S(2)}, u32[]{:S(2)}) %all-to-all-start) | async-done | bytes 7712 | tf_op jit(solution)/shard_map/all_to_all | solution.py:84
  76.6 0.1 fusion.37
  76.7 1.1 %bitcast_select_fusion.1 = f32[1,12]{1,0:T(1,128)} fusion(f32[12]{0:T(128)S(1)} %get-tuple-element.13, s32[]{:T(128)} %fusion.30), kind=kLoop, calls=%fused_computation.86 | loop fusion | flops 24 | bytes 100 | tf_op jit(solution)/shard_map/mul | solution.py:100
  77.8 1.1 %fusion.32 = (f32[1,12]{1,0:T(1,128)}, f32[1,12]{1,0:T(1,128)}, f32[1,12]{1,0:T(1,128)}) fusion(f32[12]{0:T(128)S(1)} %reduce_max.21, f32[12]{0:T(128)S(1)} %get-tuple-element.8, f32[12]{0:T(128)S(1)} %get-tuple-element.9, s32[]{:T(128)} %fusion.30, f32[12]{0:T(128)S(1)} %get-tuple-element.12), kind=kLoop, calls=%fused_computation.88 | loop fusion | flops 108 | bytes 340 | tf_op jit(solution)/shard_map/mul | solution.py:99
  (24 shorter events, 0.3 us)
Async XLA Ops:
  0.6 38.8 %copy-start.1 = (s32[4,8]{1,0:T(4,128)S(1)}, s32[4,8]{1,0:T(4,128)}, u32[]{:S(2)}) copy-start(s32[4,8]{1,0:T(4,128)} %param.9) | copy-start | bytes 388
  39.3 2.7 %collective-permute-start = (bf16[96,4224]{1,0:T(8,128)(2,1)S(1)}, bf16[96,4224]{1,0:T(8,128)(2,1)S(1)}, u32[]{:S(2)}, u32[]{:S(2)}) collective-permute-start(bf16[96,4224]{1,0:T(8,128)(2,1)S(1)} %reshape.400), channel_id=1, source_target_pairs={{0,1},{1,0},{2,3},{3,2},{4,5},{5,4},{6,7},{7,6},{8,9},{9,8},{10,11... | collective-permute-start | bytes 2433032 | tf_op jit(solution)/shard_map/ppermute | solution.py:59
  42.2 1.2 %copy-start = (bf16[192,4224]{1,0:T(8,128)(2,1)}, bf16[192,4224]{1,0:T(8,128)(2,1)S(1)}, u32[]{:S(2)}) copy-start(bf16[192,4224]{1,0:T(8,128)(2,1)S(1)} %maximum_select_fusion) | copy-start | bytes 4866052
  58.0 10.4 %copy-start.2 = (s32[1,8]{1,0:T(1,128)S(1)}, s32[1,8]{1,0:T(1,128)}, u32[]{:S(2)}) copy-start(s32[1,8]{1,0:T(1,128)} %param.8) | copy-start | bytes 100
  63.0 13.6 %all-to-all-start = ((f32[32,5,12]{2,1,0:T(8,128)}), f32[32,5,12]{2,1,0:T(8,128)S(1)}, u32[]{:S(2)}, u32[]{:S(2)}) async-start(f32[32,5,12]{2,1,0:T(8,128)} %copy.14), calls=%async_computation | async-start | bytes 262144 | tf_op jit(solution)/shard_map/all_to_all | solution.py:84

commit v4 on v3

--- a/solution.py
+++ b/solution.py
@@ -1,10 +1,11 @@
 import jax
 import jax.numpy as jnp
 from jax import lax
-from jax.sharding import PartitionSpec as P
+from jax.sharding import Mesh, PartitionSpec as P
 
 EPSILON = 1e-05
 RADIX = 256
+VOCAB = ("vocab_hi", "vocab_lo")
 LANES = 128
 
 
@@ -40,9 +41,9 @@
 
 def shards(states, target_ids, lengths, order, gain, head):
     count = states.shape[1]
-    vocab_size = lax.axis_size("vocab")
+    vocab_size = lax.axis_size(VOCAB)
     group_size = lax.axis_size("grp")
-    vocab_index = lax.axis_index("vocab")
+    vocab_index = lax.axis_index(VOCAB)
     group_index = lax.axis_index("grp")
     core = group_index % 2
     pair_base = group_index - core
@@ -55,7 +56,9 @@
     place = RADIX ** jnp.arange(digits, dtype=jnp.int32)
     coded = ((target_ids[0][:, None] // place[None, :]) % RADIX).astype(jnp.bfloat16)
     coded = jnp.pad(coded, ((0, 0), (0, LANES - digits)))
-    packed = lax.all_gather(jnp.concatenate([normed, coded], axis=1), "vocab", axis=0, tiled=True)
+    packed = jnp.concatenate([normed, coded], axis=1)
+    packed = lax.all_gather(packed, "vocab_lo", axis=0, tiled=True)
+    packed = lax.all_gather(packed, "vocab_hi", axis=0, tiled=True)
     partner = lax.ppermute(
         packed, "grp", [(g, g ^ 1) for g in range(group_size)]
     )
@@ -81,7 +84,7 @@
     root_rows = jnp.where(root_slot[:, :, None], root_mean[None, None, :], 0.0)
     payload = jnp.concatenate([routed, root_rows[:, :, None, :]], axis=2)
     payload = payload.reshape(vocab_size * group_size, 5, count)
-    received = lax.all_to_all(payload, ("vocab", "grp"), 0, 0, tiled=True)
+    received = lax.all_to_all(payload, VOCAB + ("grp",), 0, 0, tiled=True)
     shard_max, shard_sums, shard_expected, shard_target, shard_root = (
         received[:, 0], received[:, 1], received[:, 2], received[:, 3], received[:, 4]
     )
@@ -101,13 +104,16 @@
 
 
 def solution(mesh):
+    vocab_size, group_size = mesh.devices.shape
+    low = 2 if vocab_size % 2 == 0 else 1
+    split = Mesh(mesh.devices.reshape(vocab_size // low, low, group_size), VOCAB + ("grp",))
     in_specs = (
-        P("grp", "vocab", None),
-        P("grp", "vocab"),
+        P("grp", VOCAB, None),
+        P("grp", VOCAB),
         P("grp", None),
         P(),
         P(),
-        P(None, "vocab"),
+        P(None, VOCAB),
     )
-    out_specs = (P("grp", "vocab"), P("grp", "vocab"), P("grp", "vocab"), P("grp", "vocab"))
-    return jax.shard_map(shards, mesh=mesh, in_specs=in_specs, out_specs=out_specs, check_vma=False)
+    out_specs = (P("grp", VOCAB),) * 4
+    return jax.shard_map(shards, mesh=split, in_specs=in_specs, out_specs=out_specs, check_vma=False)

time: 79.2 us -> 72.4 us (0.914)
  blocking collectives: 34.8 us -> 27.7 us
  starting transfers between devices: 5.46 us -> 3.94 us
  local copies, waits for them, and re-layouts: 5.98 us -> 7.21 us
    all_gather x1 -> x2, blocking collectives: 34.8 us -> 27.7 us  [the longest x1 20.4 us: shards(): packed = lax.all_gather(packed, 'vocab_hi', axis=0, tiled=True)]
    all_to_all x1, starting transfers between devices: 5.39 us -> 3.94 us  [shards(): received = lax.all_to_all(payload, VOCAB + ('grp',), 0, 0, tiled=True)]
  transfers between devices with their start and end apart: 2 -> 2, of which waited for: 1 -> 1; matrix products, arithmetic and copies ran while one was open for 5% -> 8% of each run, Pallas kernels for 0% -> 0%
where the time goes in v4:
time: 72.4 us; the launch traced here: 72 us
  blocking collectives  27.7 us (38%)
  matrix products  14.7 us (20%)
  other arithmetic  10.7 us (15%)
  local copies, waits for them, and re-layouts  7.21 us (10%)
  waiting for transfers between devices  6.95 us (10%)
  starting transfers between devices  3.94 us (5%)
  between operations  0.9 us (1%)
    all_gather x1, blocking collectives, shards(): packed = lax.all_gather(packed, 'vocab_hi', axis=0, tiled=True)  20.4 us
    dot_general x1, matrix products, partial_stats(): logits = jnp.dot(normed, columns, preferred_element_type=jnp.float32)  14.5 us
    all_gather x1, blocking collectives, shards(): packed = lax.all_gather(packed, 'vocab_lo', axis=0, tiled=True)  7.21 us
    all_to_all x1, waiting for transfers between devices, shards(): received = lax.all_to_all(payload, VOCAB + ('grp',), 0, 0, tiled=True)  6.95 us
    all_to_all x1, starting transfers between devices, shards(): received = lax.all_to_all(payload, VOCAB + ('grp',), 0, 0, tiled=True)  3.94 us
    gather x2, local copies, waits for them, and re-layouts, partial_stats(): jnp.take_along_axis(logits, jnp.clip(within, 0, width - 1)[:, None], axis=1)  1.99 us
  transfers between devices with their start and end apart: 2, of which 1 were waited for; matrix products, arithmetic and copies ran while one was open for 8% of the time, Pallas kernels for 0%

profile of v4, /device:TPU:0, one launch (start us, length us, event | category | flops | bytes accessed | tf_op | source)
XLA Modules:
  0.0 72.0 jit_solution(15203203441792066629)
XLA Ops:
  0.6 0.7 bitcast_sign_fusion
  1.3 1.0 %fusion.5 = f32[12]{0:T(128)S(1)} fusion(bf16[1,12,4096]{2,1,0:T(8,128)(2,1)} %param.6), kind=kLoop, calls=%fused_computation.14 | loop fusion | flops 147444 | bytes 98352 | tf_op jit(solution)/shard_map/reduce_sum | solution.py:21
  2.4 1.0 %fusion.7 = bf16[12,4096]{1,0:T(8,128)(2,1)S(1)} fusion(bf16[1,12,4096]{2,1,0:T(8,128)(2,1)} %param.6, f32[4096]{0:T(1024)} %param.10, f32[12]{0:T(128)S(1)} %get-tuple-element.18), kind=kLoop, calls=%fused_computation.16 | loop fusion | flops 196608 | bytes 213040 | tf_op jit(solution)/shard_map/convert_element_type | solution.py:22
  3.4 0.9 %fusion.18 = bf16[12,2]{1,0:T(8,128)(2,1)S(1)} fusion(s32[2]{0:T(128)S(1)} %get-tuple-element.22, s32[12]{0:T(128)} %bitcast.68, s32[2]{0:T(128)S(1)} %get-tuple-element.23, s32[12]{0:T(128)S(1)} %bitcast_sign_fusion), kind=kLoop, calls=%fused_computation.40 | loop fusion | flops 456 | bytes 160 | tf_op jit(solution)/shard_map/convert_element_type | solution.py:57
  4.3 7.2 %all-gather = bf16[2,12,4224]{2,1,0:T(8,128)(2,1)S(1)} all-gather(bf16[1,12,4224]{2,1,0:T(8,128)(2,1)S(1)} %fusion.9), channel_id=1, replica_groups=mesh['vocab_hi'=4,'vocab_lo'=2,'grp'=4] {'vocab_lo'}, dimensions={0}, use_global_device_ids=true | all-gather | bytes 304128 | tf_op jit(solution)/shard_map/all_gather | solution.py:60
  11.5 0.1 reshape.400
  11.5 20.4 %all_gather.7 = bf16[96,4224]{1,0:T(8,128)(2,1)S(1)} all-gather(bf16[24,4224]{1,0:T(8,128)(2,1)S(1)} %reshape.400), channel_id=1, replica_groups=mesh['vocab_hi'=4,'vocab_lo'=2,'grp'=4] {'vocab_hi'}, dimensions={0}, use_global_device_ids=true | all-gather | bytes 1013760 | tf_op jit(solution)/shard_map/all_gather | solution.py:61
  32.0 0.0 collective-permute-start
  32.0 1.3 %dynamic_slice.16 = s32[1,1]{1,0:T(1,128)} dynamic-slice(s32[4,8]{1,0:T(4,128)} %param.9, s32[]{:T(128)S(6)} %select_n.317, s32[]{:T(128)S(6)} %select_n.319), dynamic_slice_sizes={1,1} | dynamic-slice | bytes 12 | tf_op jit(solution)/shard_map/dynamic_slice | solution.py:82
  33.3 0.6 iota_compare_fusion.3
  34.0 0.1 broadcast_in_dim.101
  34.1 0.1 broadcast_in_dim.104
  34.1 0.1 and.230
  34.2 0.1 and.231
  34.3 0.1 and.233
  34.4 1.3 %fusion.34 = s32[]{:T(128)} fusion(s32[4,8]{1,0:T(4,128)} %param.9, s32[]{:T(128)S(6)} %select_n.288, s32[]{:T(128)S(6)} %add.129), kind=kLoop, calls=%fused_computation.98 | loop fusion | flops 23 | bytes 44 | tf_op jit(solution)/shard_map/reduce_sum | solution.py:97
  35.8 0.7 constant_dynamic-slice_fusion
  36.5 0.1 broadcast_select_fusion
  36.5 0.0 collective-permute-done
  36.5 0.3 maximum_select_fusion
  36.8 0.0 copy-start
  36.8 0.1 multiply_reduce_fusion.1
  37.0 1.0 %copy-done = bf16[192,4224]{1,0:T(8,128)(2,1)} copy-done((bf16[192,4224]{1,0:T(8,128)(2,1)}, bf16[192,4224]{1,0:T(8,128)(2,1)S(1)}, u32[]{:S(2)}) %copy-start) | copy-done | bytes 1622040
  38.0 14.5 %fusion.38 = (f32[192]{0:T(256)S(1)}, f32[192,4096]{1,0:T(8,128)S(1)}) fusion(bf16[4096,8192]{1,0:T(8,128)(2,1)} %param.11, s32[]{:T(128)S(6)} %select_n.306, bf16[192,4224]{1,0:T(8,128)(2,1)} %copy-done), kind=kOutput, calls=%fused_computation.104 | convolution fusion | flops 6443237376 | bytes 38273796 | tf_op jit(solution)/shard_map/dot_general | solution.py:27
  52.6 0.0 copy-start.1
  52.6 0.1 stack.13
  52.7 0.9 %fusion.2 = (f32[192]{0:T(256)S(1)}, f32[192]{0:T(256)S(1)}) fusion(f32[192,4096]{1,0:T(8,128)S(1)} %get-tuple-element.21, f32[192]{0:T(256)S(1)} %get-tuple-element.20), kind=kLoop, calls=%fused_computation.6 | loop fusion | flops 3145344 | bytes 3148032 | tf_op jit(solution)/shard_map/reduce_sum | solution.py:36
  53.6 0.1 stack.14
  53.7 0.1 stack.15
  53.8 0.1 min.16
  53.9 1.9 %gather_fusion.1 = f32[192]{0:T(256)S(1)} fusion(f32[192,4096]{1,0:T(8,128)S(1)} %get-tuple-element.21, s32[192]{0:T(256)S(1)} %bitcast.60), kind=kCustom, calls=%fused_computation.1 | custom fusion | bytes 3072 | tf_op jit(solution)/shard_map/jit(take_along_axis)/gather | solution.py:33
  55.8 0.1 gather.13
  55.9 0.1 and.227
  56.0 0.1 convolution_bitcast_fusion
  56.2 0.6 gather_fusion
  56.8 0.1 select_select_fusion
  56.9 0.7 copy.14
  57.6 3.9 %all-to-all-start = ((f32[32,5,12]{2,1,0:T(8,128)}), f32[32,5,12]{2,1,0:T(8,128)S(1)}, u32[]{:S(2)}, u32[]{:S(2)}) async-start(f32[32,5,12]{2,1,0:T(8,128)} %copy.14), calls=%async_computation | async-start | bytes 262144 | tf_op jit(solution)/shard_map/all_to_all | solution.py:87
  61.5 0.0 copy-done.1
  61.5 1.3 %fusion.30 = s32[]{:T(128)} fusion(s32[1,8]{1,0:T(1,128)S(1)} %copy-done.1, s32[]{:T(128)} %fusion.34), kind=kLoop, calls=%fused_computation.84 | loop fusion | flops 23 | bytes 40 | tf_op jit(solution)/shard_map/reduce_sum | solution.py:98
  62.8 6.9 %all-to-all-done = f32[32,5,12]{2,1,0:T(8,128)S(1)} async-done(((f32[32,5,12]{2,1,0:T(8,128)}), f32[32,5,12]{2,1,0:T(8,128)S(1)}, u32[]{:S(2)}, u32[]{:S(2)}) %all-to-all-start) | async-done | bytes 7712 | tf_op jit(solution)/shard_map/all_to_all | solution.py:87
  69.7 0.1 fusion.37
  69.8 1.1 %bitcast_select_fusion.1 = f32[1,12]{1,0:T(1,128)} fusion(f32[12]{0:T(128)S(1)} %get-tuple-element.13, s32[]{:T(128)} %fusion.30), kind=kLoop, calls=%fused_computation.86 | loop fusion | flops 24 | bytes 100 | tf_op jit(solution)/shard_map/mul | solution.py:103
  71.0 1.1 %fusion.32 = (f32[1,12]{1,0:T(1,128)}, f32[1,12]{1,0:T(1,128)}, f32[1,12]{1,0:T(1,128)}) fusion(f32[12]{0:T(128)S(1)} %reduce_max.21, f32[12]{0:T(128)S(1)} %get-tuple-element.8, f32[12]{0:T(128)S(1)} %get-tuple-element.9, s32[]{:T(128)} %fusion.30, f32[12]{0:T(128)S(1)} %get-tuple-element.12), kind=kLoop, calls=%fused_computation.88 | loop fusion | flops 108 | bytes 340 | tf_op jit(solution)/shard_map/mul | solution.py:102
  (23 shorter events, 0.3 us)
Async XLA Ops:
  32.0 4.6 %collective-permute-start = (bf16[96,4224]{1,0:T(8,128)(2,1)S(1)}, bf16[96,4224]{1,0:T(8,128)(2,1)S(1)}, u32[]{:S(2)}, u32[]{:S(2)}) collective-permute-start(bf16[96,4224]{1,0:T(8,128)(2,1)S(1)} %all_gather.7), channel_id=1, source_target_pairs={{0,1},{1,0},{2,3},{3,2},{4,5},{5,4},{6,7},{7,6},{8,9},{9,8},{10,11... | collective-permute-start | bytes 2433032 | tf_op jit(solution)/shard_map/ppermute | solution.py:62
  36.8 1.2 %copy-start = (bf16[192,4224]{1,0:T(8,128)(2,1)}, bf16[192,4224]{1,0:T(8,128)(2,1)S(1)}, u32[]{:S(2)}) copy-start(bf16[192,4224]{1,0:T(8,128)(2,1)S(1)} %maximum_select_fusion) | copy-start | bytes 4866052
  52.6 8.9 %copy-start.1 = (s32[1,8]{1,0:T(1,128)S(1)}, s32[1,8]{1,0:T(1,128)}, u32[]{:S(2)}) copy-start(s32[1,8]{1,0:T(1,128)} %param.8) | copy-start | bytes 100
  57.6 12.2 %all-to-all-start = ((f32[32,5,12]{2,1,0:T(8,128)}), f32[32,5,12]{2,1,0:T(8,128)S(1)}, u32[]{:S(2)}, u32[]{:S(2)}) async-start(f32[32,5,12]{2,1,0:T(8,128)} %copy.14), calls=%async_computation | async-start | bytes 262144 | tf_op jit(solution)/shard_map/all_to_all | solution.py:87

commit v5 on v4

--- a/solution.py
+++ b/solution.py
@@ -1,12 +1,18 @@
+from functools import partial
+
 import jax
 import jax.numpy as jnp
 from jax import lax
+from jax.experimental import pallas as pl
+from jax.experimental.pallas import tpu as pltpu
 from jax.sharding import Mesh, PartitionSpec as P
 
 EPSILON = 1e-05
 RADIX = 256
 VOCAB = ("vocab_hi", "vocab_lo")
 LANES = 128
+TILE = 512
+ROW_TILE = 256
 
 
 def digit_count(total):
@@ -39,6 +45,62 @@
     )
 
 
+def stats_kernel(scalars, rows_ref, codes_ref, head_ref, max_ref, sum_ref, exp_ref, tgt_ref, *, tile, digits):
+    step = pl.program_id(1)
+
+    @pl.when(step == 0)
+    def _():
+        max_ref[...] = jnp.full(max_ref.shape, -jnp.inf, jnp.float32)
+        sum_ref[...] = jnp.zeros(sum_ref.shape, jnp.float32)
+        exp_ref[...] = jnp.zeros(exp_ref.shape, jnp.float32)
+        tgt_ref[...] = jnp.zeros(tgt_ref.shape, jnp.float32)
+
+    logits = jnp.dot(rows_ref[...], head_ref[...], preferred_element_type=jnp.float32)
+    old_max = max_ref[...]
+    new_max = jnp.maximum(old_max, jnp.max(logits, axis=1, keepdims=True))
+    rescale = jnp.exp(old_max - new_max)
+    weights = jnp.exp(logits - new_max)
+    sum_ref[...] = sum_ref[...] * rescale + jnp.sum(weights, axis=1, keepdims=True)
+    exp_ref[...] = exp_ref[...] * rescale + jnp.sum(weights * logits, axis=1, keepdims=True)
+    max_ref[...] = new_max
+    codes = codes_ref[...].astype(jnp.float32)
+    lane = lax.broadcasted_iota(jnp.int32, codes.shape, 1)
+    place = jnp.zeros(codes.shape, jnp.float32)
+    for k in range(digits):
+        place = jnp.where(lane == k, float(RADIX**k), place)
+    token = jnp.sum(codes * place, axis=1, keepdims=True)
+    column = scalars[1] + step * tile + lax.broadcasted_iota(jnp.int32, logits.shape, 1)
+    hit = column.astype(jnp.float32) == token
+    tgt_ref[...] += jnp.sum(jnp.where(hit, logits, 0.0), axis=1, keepdims=True)
+
+
+def fused_stats(packed, head, first_block, first_column, features, span, digits):
+    rows = packed.shape[0]
+    tile = min(TILE, span)
+    row_tile = rows
+    while row_tile > ROW_TILE and row_tile % 2 == 0:
+        row_tile //= 2
+    grid = (rows // row_tile, span // tile)
+    scalars = jnp.stack([first_block, first_column]).astype(jnp.int32)
+    stat = jax.ShapeDtypeStruct((rows, 1), jnp.float32)
+    stat_spec = pl.BlockSpec((row_tile, 1), lambda i, j, s: (i, 0))
+    return pl.pallas_call(
+        partial(stats_kernel, tile=tile, digits=digits),
+        out_shape=(stat,) * 4,
+        grid_spec=pltpu.PrefetchScalarGridSpec(
+            num_scalar_prefetch=1,
+            grid=grid,
+            in_specs=[
+                pl.BlockSpec((row_tile, features), lambda i, j, s: (i, 0)),
+                pl.BlockSpec((row_tile, LANES), lambda i, j, s: (i, features // LANES)),
+                pl.BlockSpec((features, tile), lambda i, j, s: (0, s[0] + j)),
+            ],
+            out_specs=[stat_spec] * 4,
+        ),
+        compiler_params=pltpu.CompilerParams(dimension_semantics=("arbitrary", "arbitrary")),
+    )(scalars, packed, packed, head)
+
+
 def shards(states, target_ids, lengths, order, gain, head):
     count = states.shape[1]
     vocab_size = lax.axis_size(VOCAB)
@@ -63,12 +125,14 @@
         packed, "grp", [(g, g ^ 1) for g in range(group_size)]
     )
     pair_rows = jnp.where(core == 0, jnp.concatenate([packed, partner]), jnp.concatenate([partner, packed]))
-    pair_normed = pair_rows[:, :features]
-    pair_ids = jnp.sum(pair_rows[:, features : features + digits].astype(jnp.int32) * place[None, :], axis=1)
     span = width // 2
-    columns = lax.dynamic_slice_in_dim(head, core * span, span, 1)
-    offset = vocab_index * width + core * span
-    local_max, sums, expected, target = partial_stats(pair_normed, columns, pair_ids, offset)
+    first_column = vocab_index * width + core * span
+    local_max, sums, expected, target = (
+        stat[:, 0]
+        for stat in fused_stats(
+            pair_rows, head, core * (span // min(TILE, span)), first_column, features, span, digits
+        )
+    )
     terms = jnp.stack([local_max, sums, expected, target]).reshape(4, 2, vocab_size, count)
     pair_order = lax.dynamic_slice_in_dim(order, pair_base, 2, 0)
     route = (pair_order[:, None, :] == block_ids[None, :, None]).astype(jnp.float32)

time: 72.4 us -> 75.4 us (1.041)
  Pallas kernels: 0 us -> 17.8 us
  matrix products: 14.7 us -> 0.15 us
  local copies, waits for them, and re-layouts: 7.21 us -> 2.71 us
  other arithmetic: 10.7 us -> 14.8 us
    pallas_call x0 -> x1, Pallas kernels: none -> 17.8 us  [fused_stats(): pl.pallas_call(partial(stats_kernel, tile=tile, digits=digits), out_shape...]
    dot_general x1 -> x0, matrix products: 14.5 us -> none  [partial_stats(): logits = jnp.dot(normed, columns, preferred_element_type=jnp.float32)]
    pallas_call x0 -> x4, other arithmetic: none -> 4.01 us  [fused_stats(): pl.pallas_call(partial(stats_kernel, tile=tile, digits=digits), out_shape...]
    gather x2 -> x0, local copies, waits for them, and re-layouts: 1.99 us -> none  [partial_stats(): jnp.take_along_axis(logits, jnp.clip(within, 0, width - 1)[:, None], axis=1)]
    select_n x1, other arithmetic: 0.28 us -> 1.48 us  [shards(): jnp.where(core == 0, jnp.concatenate([packed, partner]), jnp.concatenate(...]
    unnamed x6 -> x5, local copies, waits for them, and re-layouts: 1.11 us -> 0.06 us
    reduce_sum x2 -> x0, other arithmetic: 1.02 us -> none  [the longest x1 0.9 us: partial_stats(): jnp.sum(weights, axis=1)]
  transfers between devices with their start and end apart: 2 -> 2, of which waited for: 1 -> 1; matrix products, arithmetic and copies ran while one was open for 8% -> 6% of each run, Pallas kernels for 0% -> 0%
where the time goes in v5:
time: 75.4 us; the launch traced here: 74.9 us
  blocking collectives  27.7 us (37%)
  Pallas kernels  17.8 us (24%)
  other arithmetic  14.8 us (20%)
  waiting for transfers between devices  6.95 us (9%)
  starting transfers between devices  3.92 us (5%)
  local copies, waits for them, and re-layouts  2.71 us (4%)
  between operations  0.9 us (1%)
    all_gather x1, blocking collectives, shards(): packed = lax.all_gather(packed, 'vocab_hi', axis=0, tiled=True)  20.4 us
    pallas_call x1, Pallas kernels, fused_stats(): pl.pallas_call(partial(stats_kernel, tile=tile, digits=digits), out_shape...  17.8 us
    all_gather x1, blocking collectives, shards(): packed = lax.all_gather(packed, 'vocab_lo', axis=0, tiled=True)  7.21 us
    all_to_all x1, waiting for transfers between devices, shards(): received = lax.all_to_all(payload, VOCAB + ('grp',), 0, 0, tiled=True)  6.95 us
    pallas_call x4, other arithmetic, fused_stats(): pl.pallas_call(partial(stats_kernel, tile=tile, digits=digits), out_shape...  4.01 us
    all_to_all x1, starting transfers between devices, shards(): received = lax.all_to_all(payload, VOCAB + ('grp',), 0, 0, tiled=True)  3.92 us
  transfers between devices with their start and end apart: 2, of which 1 were waited for; matrix products, arithmetic and copies ran while one was open for 6% of the time, Pallas kernels for 0%

profile of v5, /device:TPU:0, one launch (start us, length us, event | category | flops | bytes accessed | tf_op | source)
XLA Modules:
  0.0 74.9 jit_solution(10222144577693053216)
XLA Ops:
  0.6 0.0 copy-start
  0.7 0.7 bitcast_sign_fusion
  1.3 1.0 %fusion.1 = f32[12]{0:T(128)S(1)} fusion(bf16[1,12,4096]{2,1,0:T(8,128)(2,1)} %param.6), kind=kLoop, calls=%fused_computation.7 | loop fusion | flops 147444 | bytes 98352 | tf_op jit(solution)/shard_map/reduce_sum | solution.py:27
  2.4 1.0 %fusion.3 = bf16[12,4096]{1,0:T(8,128)(2,1)S(1)} fusion(bf16[1,12,4096]{2,1,0:T(8,128)(2,1)} %param.6, f32[4096]{0:T(1024)} %param.10, f32[12]{0:T(128)S(1)} %get-tuple-element.24), kind=kLoop, calls=%fused_computation.9 | loop fusion | flops 196608 | bytes 213040 | tf_op jit(solution)/shard_map/convert_element_type | solution.py:28
  3.4 0.9 %fusion.14 = bf16[12,2]{1,0:T(8,128)(2,1)S(1)} fusion(s32[2]{0:T(128)S(1)} %get-tuple-element.26, s32[12]{0:T(128)} %bitcast.72, s32[2]{0:T(128)S(1)} %get-tuple-element.27, s32[12]{0:T(128)S(1)} %bitcast_sign_fusion), kind=kLoop, calls=%fused_computation.31 | loop fusion | flops 456 | bytes 160 | tf_op jit(solution)/shard_map/convert_element_type | solution.py:119
  4.3 7.2 %all-gather = bf16[2,12,4224]{2,1,0:T(8,128)(2,1)S(1)} all-gather(bf16[1,12,4224]{2,1,0:T(8,128)(2,1)S(1)} %fusion.5), channel_id=1, replica_groups=mesh['vocab_hi'=4,'vocab_lo'=2,'grp'=4] {'vocab_lo'}, dimensions={0}, use_global_device_ids=true | all-gather | bytes 304128 | tf_op jit(solution)/shard_map/all_gather | solution.py:122
  11.5 0.1 reshape.284
  11.5 20.4 %all_gather.7 = bf16[96,4224]{1,0:T(8,128)(2,1)S(1)} all-gather(bf16[24,4224]{1,0:T(8,128)(2,1)S(1)} %reshape.284), channel_id=1, replica_groups=mesh['vocab_hi'=4,'vocab_lo'=2,'grp'=4] {'vocab_hi'}, dimensions={0}, use_global_device_ids=true | all-gather | bytes 1013760 | tf_op jit(solution)/shard_map/all_gather | solution.py:123
  32.0 0.0 collective-permute-start
  32.1 0.0 copy-done
  32.1 0.6 dynamic_slice.12
  32.7 0.6 iota_compare_fusion.3
  33.3 0.1 broadcast_in_dim.90
  33.4 0.1 broadcast_in_dim.93
  33.5 0.1 and.184
  33.6 0.1 and.185
  33.7 0.1 and.187
  33.8 0.6 fusion.23
  34.4 0.6 pad_add_fusion.scalars
  35.0 0.1 broadcast_select_fusion
  35.1 0.0 collective-permute-done
  35.1 1.5 %maximum_select_fusion.rows_ref.codes_ref = bf16[192,4224]{1,0:T(8,128)(2,1)} fusion(bf16[96,4224]{1,0:T(8,128)(2,1)S(1)} %collective-permute-done, bf16[96,4224]{1,0:T(8,128)(2,1)S(1)} %all_gather.7, pred[]{:T(512)S(6)} %eq.84), kind=kLoop, calls=%fused_computation.1 | loop fusion | flops 7299072 | bytes 3244033 | tf_op jit(solution)/shard_map/jit(_where)/select_n | solution.py:127
  36.6 0.0 copy-start.1
  36.6 17.8 %shard_map.93 = (f32[192,1]{1,0:T(8,128)}, f32[192,1]{1,0:T(8,128)}, f32[192,1]{1,0:T(8,128)}, f32[192,1]{1,0:T(8,128)}) custom-call(s32[2]{0:T(128)} %pad_add_fusion.scalars, bf16[192,4224]{1,0:T(8,128)(2,1)} %maximum_select_fusion.rows_ref.codes_ref, bf16[192,4224]{1,0:T(8,128)(2,1)} %maximum_select_fusion.rows_ref.codes_ref, bf16[4096,8192]{1,0:T(8,128)(2,1)} %head_ref.1), custom_call_target="tpu_custom_call" | custom-call | tf_op jit(solution)/shard_map/pallas_call | solution.py:87
  54.5 1.0 %reduce.5 = f32[192]{0:T(256)S(1)} reduce(f32[192,1]{1,0:T(8,128)} %get-tuple-element.10, f32[]{:T(128)} %constant.154), dimensions={1}, to_apply=%get-tuple-element.10.reduce_sub_computation | reduce | bytes 1540 | tf_op jit(solution)/shard_map/pallas_call | solution.py:87
  55.5 0.1 stack.25
  55.5 1.0 %reduce.6 = f32[192]{0:T(256)S(1)} reduce(f32[192,1]{1,0:T(8,128)} %get-tuple-element.11, f32[]{:T(128)} %constant.154), dimensions={1}, to_apply=%get-tuple-element.11.reduce_sub_computation | reduce | bytes 1540 | tf_op jit(solution)/shard_map/pallas_call | solution.py:87
  56.6 0.1 stack.26
  56.6 1.0 %reduce.3 = f32[192]{0:T(256)S(1)} reduce(f32[192,1]{1,0:T(8,128)} %get-tuple-element.8, f32[]{:T(128)} %constant.154), dimensions={1}, to_apply=%get-tuple-element.8.reduce_sub_computation | reduce | bytes 1540 | tf_op jit(solution)/shard_map/pallas_call | solution.py:87
  57.7 0.1 stack.23
  57.7 1.0 %reduce.4 = f32[192]{0:T(256)S(1)} reduce(f32[192,1]{1,0:T(8,128)} %get-tuple-element.9, f32[]{:T(128)} %constant.154), dimensions={1}, to_apply=%get-tuple-element.9.reduce_sub_computation | reduce | bytes 1540 | tf_op jit(solution)/shard_map/pallas_call | solution.py:87
  58.8 0.1 stack.24
  58.9 0.1 convolution_bitcast_fusion
  59.0 0.6 gather_fusion
  59.6 0.1 select_select_fusion
  59.7 0.7 copy.26
  60.4 3.9 %all-to-all-start = ((f32[32,5,12]{2,1,0:T(8,128)}), f32[32,5,12]{2,1,0:T(8,128)S(1)}, u32[]{:S(2)}, u32[]{:S(2)}) async-start(f32[32,5,12]{2,1,0:T(8,128)} %copy.26), calls=%async_computation | async-start | bytes 262144 | tf_op jit(solution)/shard_map/all_to_all | solution.py:151
  64.3 0.0 copy-done.1
  64.3 1.3 %fusion.22 = s32[]{:T(128)} fusion(s32[1,8]{1,0:T(1,128)S(1)} %copy-done.1, s32[]{:T(128)} %fusion.23), kind=kLoop, calls=%fused_computation.62 | loop fusion | flops 23 | bytes 40 | tf_op jit(solution)/shard_map/reduce_sum | solution.py:162
  65.6 6.9 %all-to-all-done = f32[32,5,12]{2,1,0:T(8,128)S(1)} async-done(((f32[32,5,12]{2,1,0:T(8,128)}), f32[32,5,12]{2,1,0:T(8,128)S(1)}, u32[]{:S(2)}, u32[]{:S(2)}) %all-to-all-start) | async-done | bytes 7712 | tf_op jit(solution)/shard_map/all_to_all | solution.py:151
  72.6 0.1 fusion.29
  72.7 1.1 %bitcast_select_fusion.1 = f32[1,12]{1,0:T(1,128)} fusion(f32[12]{0:T(128)S(1)} %get-tuple-element.19, s32[]{:T(128)} %fusion.22), kind=kLoop, calls=%fused_computation.66 | loop fusion | flops 24 | bytes 100 | tf_op jit(solution)/shard_map/mul | solution.py:167
  73.8 1.1 %fusion.25 = (f32[1,12]{1,0:T(1,128)}, f32[1,12]{1,0:T(1,128)}, f32[1,12]{1,0:T(1,128)}) fusion(f32[12]{0:T(128)S(1)} %reduce_max.11, f32[12]{0:T(128)S(1)} %get-tuple-element.14, f32[12]{0:T(128)S(1)} %get-tuple-element.15, s32[]{:T(128)} %fusion.22, f32[12]{0:T(128)S(1)} %get-tuple-element.18), kind=kLoop, calls=%fused_computation.68 | loop fusion | flops 108 | bytes 340 | tf_op jit(solution)/shard_map/mul | solution.py:166
  (17 shorter events, 0.2 us)
Async XLA Ops:
  0.6 31.4 %copy-start = (s32[4,8]{1,0:T(4,128)S(1)}, s32[4,8]{1,0:T(4,128)}, u32[]{:S(2)}) copy-start(s32[4,8]{1,0:T(4,128)} %param.9) | copy-start | bytes 388
  32.0 3.1 %collective-permute-start = (bf16[96,4224]{1,0:T(8,128)(2,1)S(1)}, bf16[96,4224]{1,0:T(8,128)(2,1)S(1)}, u32[]{:S(2)}, u32[]{:S(2)}) collective-permute-start(bf16[96,4224]{1,0:T(8,128)(2,1)S(1)} %all_gather.7), channel_id=1, source_target_pairs={{0,1},{1,0},{2,3},{3,2},{4,5},{5,4},{6,7},{7,6},{8,9},{9,8},{10,11... | collective-permute-start | bytes 2433032 | tf_op jit(solution)/shard_map/ppermute | solution.py:124
  36.6 27.7 %copy-start.1 = (s32[1,8]{1,0:T(1,128)S(1)}, s32[1,8]{1,0:T(1,128)}, u32[]{:S(2)}) copy-start(s32[1,8]{1,0:T(1,128)} %param.8) | copy-start | bytes 100
  60.4 12.2 %all-to-all-start = ((f32[32,5,12]{2,1,0:T(8,128)}), f32[32,5,12]{2,1,0:T(8,128)S(1)}, u32[]{:S(2)}, u32[]{:S(2)}) async-start(f32[32,5,12]{2,1,0:T(8,128)} %copy.26), calls=%async_computation | async-start | bytes 262144 | tf_op jit(solution)/shard_map/all_to_all | solution.py:151

commit v6 on v4

--- a/solution.py
+++ b/solution.py
@@ -4,8 +4,10 @@
 from jax.sharding import Mesh, PartitionSpec as P
 
 EPSILON = 1e-05
-RADIX = 256
+RADIX_BITS = 8
+RADIX = 1 << RADIX_BITS
 VOCAB = ("vocab_hi", "vocab_lo")
+GROUP = ("grp_hi", "grp_lo")
 LANES = 128
 
 
@@ -27,24 +29,22 @@
     logits = jnp.dot(normed, columns, preferred_element_type=jnp.float32)
     local_max = jnp.max(logits, axis=1)
     weights = jnp.exp(logits - local_max[:, None])
-    width = columns.shape[1]
     within = token_ids - offset
-    inside = (within >= 0) & (within < width)
-    picked = jnp.take_along_axis(logits, jnp.clip(within, 0, width - 1)[:, None], axis=1)[:, 0]
+    column = lax.broadcasted_iota(jnp.int32, logits.shape, 1)
     return (
         local_max,
         jnp.sum(weights, axis=1),
         jnp.sum(weights * logits, axis=1),
-        jnp.where(inside, picked, 0.0),
+        jnp.sum(jnp.where(column == within[:, None], logits, 0.0), axis=1),
     )
 
 
 def shards(states, target_ids, lengths, order, gain, head):
     count = states.shape[1]
     vocab_size = lax.axis_size(VOCAB)
-    group_size = lax.axis_size("grp")
+    group_size = lax.axis_size(GROUP)
     vocab_index = lax.axis_index(VOCAB)
-    group_index = lax.axis_index("grp")
+    group_index = lax.axis_index(GROUP)
     core = group_index % 2
     pair_base = group_index - core
     own_order = lax.dynamic_index_in_dim(order, group_index, 0, keepdims=False)
@@ -54,14 +54,13 @@
     features = normed.shape[1]
     digits = digit_count(width * vocab_size)
     place = RADIX ** jnp.arange(digits, dtype=jnp.int32)
-    coded = ((target_ids[0][:, None] // place[None, :]) % RADIX).astype(jnp.bfloat16)
+    shifts = RADIX_BITS * jnp.arange(digits, dtype=jnp.int32)
+    coded = ((target_ids[0][:, None] >> shifts[None, :]) & (RADIX - 1)).astype(jnp.bfloat16)
     coded = jnp.pad(coded, ((0, 0), (0, LANES - digits)))
     packed = jnp.concatenate([normed, coded], axis=1)
     packed = lax.all_gather(packed, "vocab_lo", axis=0, tiled=True)
     packed = lax.all_gather(packed, "vocab_hi", axis=0, tiled=True)
-    partner = lax.ppermute(
-        packed, "grp", [(g, g ^ 1) for g in range(group_size)]
-    )
+    partner = lax.ppermute(packed, "grp_lo", [(0, 1), (1, 0)])
     pair_rows = jnp.where(core == 0, jnp.concatenate([packed, partner]), jnp.concatenate([partner, packed]))
     pair_normed = pair_rows[:, :features]
     pair_ids = jnp.sum(pair_rows[:, features : features + digits].astype(jnp.int32) * place[None, :], axis=1)
@@ -73,18 +72,13 @@
     pair_order = lax.dynamic_slice_in_dim(order, pair_base, 2, 0)
     route = (pair_order[:, None, :] == block_ids[None, :, None]).astype(jnp.float32)
     routed = jnp.einsum("cjs,kcsr->jckr", route, terms, precision=lax.Precision.HIGHEST)
-    group_ids = jnp.arange(group_size, dtype=jnp.int32)
-    same_pair = (group_ids // 2 == pair_base // 2)[None, :, None, None]
-    routed = jnp.take(routed, group_ids % 2, axis=1)
-    stat_ids = jnp.arange(4, dtype=jnp.int32)[None, None, :, None]
-    fill = jnp.where(stat_ids == 0, jnp.finfo(jnp.float32).min, 0.0)
-    routed = jnp.where(same_pair, routed, fill)
+    group_ids = jnp.arange(2, dtype=jnp.int32)
     home = own_order[vocab_index]
-    root_slot = (block_ids[:, None] == home) & (group_ids[None, :] == group_index)
+    root_slot = (block_ids[:, None] == home) & (group_ids[None, :] == core)
     root_rows = jnp.where(root_slot[:, :, None], root_mean[None, None, :], 0.0)
     payload = jnp.concatenate([routed, root_rows[:, :, None, :]], axis=2)
-    payload = payload.reshape(vocab_size * group_size, 5, count)
-    received = lax.all_to_all(payload, VOCAB + ("grp",), 0, 0, tiled=True)
+    payload = payload.reshape(vocab_size * 2, 5, count)
+    received = lax.all_to_all(payload, VOCAB + ("grp_lo",), 0, 0, tiled=True)
     shard_max, shard_sums, shard_expected, shard_target, shard_root = (
         received[:, 0], received[:, 1], received[:, 2], received[:, 3], received[:, 4]
     )
@@ -105,15 +99,15 @@
 
 def solution(mesh):
     vocab_size, group_size = mesh.devices.shape
-    low = 2 if vocab_size % 2 == 0 else 1
-    split = Mesh(mesh.devices.reshape(vocab_size // low, low, group_size), VOCAB + ("grp",))
+    assert vocab_size % 2 == 0 and group_size % 2 == 0
+    split = Mesh(mesh.devices.reshape(vocab_size // 2, 2, group_size // 2, 2), VOCAB + GROUP)
     in_specs = (
-        P("grp", VOCAB, None),
-        P("grp", VOCAB),
-        P("grp", None),
+        P(GROUP, VOCAB, None),
+        P(GROUP, VOCAB),
+        P(GROUP, None),
         P(),
         P(),
         P(None, VOCAB),
     )
-    out_specs = (P("grp", VOCAB),) * 4
+    out_specs = (P(GROUP, VOCAB),) * 4
     return jax.shard_map(shards, mesh=split, in_specs=in_specs, out_specs=out_specs, check_vma=False)

time: 72.4 us -> 66.5 us (0.919)
  local copies, waits for them, and re-layouts: 7.21 us -> 4.44 us
  other arithmetic: 10.7 us -> 8.99 us
  waiting for transfers between devices: 6.95 us -> 5.58 us
    gather x4 -> x0, local copies, waits for them, and re-layouts: 2.59 us -> none  [the longest x2 1.99 us: partial_stats(): jnp.take_along_axis(logits, jnp.clip(within, 0, width - 1)[:, None], axis=1)]
    all_to_all x1, waiting for transfers between devices: 6.95 us -> 5.58 us  [shards(): received = lax.all_to_all(payload, VOCAB + ('grp_lo',), 0, 0, tiled=True)]
    mul x1, other arithmetic: 1.07 us -> 0.01 us  [shards(): shifts = RADIX_BITS * jnp.arange(digits, dtype=jnp.int32)]
where the time goes in v6:
time: 66.5 us; the launch traced here: 66.2 us
  blocking collectives  27.7 us (42%)
  matrix products  14.7 us (22%)
  other arithmetic  8.99 us (14%)
  waiting for transfers between devices  5.58 us (8%)
  local copies, waits for them, and re-layouts  4.44 us (7%)
  starting transfers between devices  4.04 us (6%)
  between operations  0.78 us (1%)
    all_gather x1, blocking collectives, shards(): packed = lax.all_gather(packed, 'vocab_hi', axis=0, tiled=True)  20.4 us
    dot_general x1, matrix products, partial_stats(): logits = jnp.dot(normed, columns, preferred_element_type=jnp.float32)  14.6 us
    all_gather x1, blocking collectives, shards(): packed = lax.all_gather(packed, 'vocab_lo', axis=0, tiled=True)  7.21 us
    all_to_all x1, waiting for transfers between devices, shards(): received = lax.all_to_all(payload, VOCAB + ('grp_lo',), 0, 0, tiled=True)  5.58 us
    all_to_all x1, starting transfers between devices, shards(): received = lax.all_to_all(payload, VOCAB + ('grp_lo',), 0, 0, tiled=True)  4.04 us
  transfers between devices with their start and end apart: 2, of which 1 were waited for; matrix products, arithmetic and copies ran while one was open for 8% of the time, Pallas kernels for 0%

profile of v6, /device:TPU:0, one launch (start us, length us, event | category | flops | bytes accessed | tf_op | source)
XLA Modules:
  0.0 66.2 jit_solution(14688936223897566983)
XLA Ops:
  0.6 1.1 %fusion.5 = f32[12]{0:T(128)S(1)} fusion(bf16[1,12,4096]{2,1,0:T(8,128)(2,1)} %param.6), kind=kLoop, calls=%fused_computation.14 | loop fusion | flops 147444 | bytes 98352 | tf_op jit(solution)/shard_map/reduce_sum | solution.py:23
  1.7 1.0 %fusion.7 = bf16[12,4096]{1,0:T(8,128)(2,1)S(1)} fusion(bf16[1,12,4096]{2,1,0:T(8,128)(2,1)} %param.6, f32[4096]{0:T(1024)} %param.10, f32[12]{0:T(128)S(1)} %get-tuple-element.19), kind=kLoop, calls=%fused_computation.16 | loop fusion | flops 196608 | bytes 213040 | tf_op jit(solution)/shard_map/convert_element_type | solution.py:24
  2.7 0.7 %and_convert_fusion = bf16[12,2]{1,0:T(8,128)(2,1)S(1)} fusion(s32[2]{0:T(128)S(1)} %iota_multiply_fusion, s32[12]{0:T(128)} %bitcast.57), kind=kLoop, calls=%fused_computation.34 | loop fusion | flops 72 | bytes 104 | tf_op jit(solution)/shard_map/convert_element_type | solution.py:58
  3.5 7.2 %all-gather = bf16[2,12,4224]{2,1,0:T(8,128)(2,1)S(1)} all-gather(bf16[1,12,4224]{2,1,0:T(8,128)(2,1)S(1)} %fusion.9), channel_id=1, replica_groups=mesh['vocab_hi'=4,'vocab_lo'=2,'grp_hi'=2,'grp_lo'=2] {'vocab_lo'}, dimensions={0}, use_global_device_ids=true | all-gather | bytes 304128 | tf_op jit(solution)/shard_map/all_gather | solution.py:61
  10.7 0.1 reshape.213
  10.7 20.4 %all_gather.7 = bf16[96,4224]{1,0:T(8,128)(2,1)S(1)} all-gather(bf16[24,4224]{1,0:T(8,128)(2,1)S(1)} %reshape.213), channel_id=1, replica_groups=mesh['vocab_hi'=4,'vocab_lo'=2,'grp_hi'=2,'grp_lo'=2] {'vocab_hi'}, dimensions={0}, use_global_device_ids=true | all-gather | bytes 1013760 | tf_op jit(solution)/shard_map/all_gather | solution.py:62
  31.2 0.0 collective-permute-start
  31.2 0.1 and.86
  31.3 1.3 %dynamic_slice.16 = s32[1,1]{1,0:T(1,128)} dynamic-slice(s32[4,8]{1,0:T(4,128)} %param.9, s32[]{:T(128)S(6)} %select_n.116, s32[]{:T(128)S(6)} %select_n.118), dynamic_slice_sizes={1,1} | dynamic-slice | bytes 12 | tf_op jit(solution)/shard_map/dynamic_slice | solution.py:76
  32.6 0.6 iota_compare_fusion.4
  33.2 0.1 and.83
  33.3 0.1 and.84
  33.4 1.3 %fusion.26 = s32[]{:T(128)} fusion(s32[4,8]{1,0:T(4,128)} %param.9, s32[]{:T(128)S(6)} %select_n.101, s32[]{:T(128)S(6)} %add.49), kind=kLoop, calls=%fused_computation.68 | loop fusion | flops 23 | bytes 44 | tf_op jit(solution)/shard_map/reduce_sum | solution.py:91
  34.7 0.7 %constant_dynamic-slice_fusion = s32[2,8]{1,0:T(2,128)S(1)} fusion(s32[4,8]{1,0:T(4,128)} %param.9, s32[]{:T(128)S(6)} %select_n.115), kind=kLoop, calls=%fused_computation.48 | loop fusion | bytes 132 | tf_op jit(solution)/shard_map/dynamic_slice | solution.py:72
  35.4 0.1 broadcast_select_fusion
  35.5 0.0 collective-permute-done
  35.5 0.3 maximum_select_fusion
  35.8 0.0 copy-start
  35.8 1.2 %copy-done = bf16[192,4224]{1,0:T(8,128)(2,1)} copy-done((bf16[192,4224]{1,0:T(8,128)(2,1)}, bf16[192,4224]{1,0:T(8,128)(2,1)S(1)}, u32[]{:S(2)}) %copy-start) | copy-done | bytes 1622040
  37.0 0.1 multiply_reduce_fusion.1
  37.1 14.6 %fusion.29 = (f32[192]{0:T(256)S(1)}, f32[192,4096]{1,0:T(8,128)S(1)}) fusion(bf16[4096,8192]{1,0:T(8,128)(2,1)} %param.11, s32[]{:T(128)S(6)} %select_n.107, bf16[192,4224]{1,0:T(8,128)(2,1)} %copy-done), kind=kOutput, calls=%fused_computation.72 | convolution fusion | flops 6443237376 | bytes 38273796 | tf_op jit(solution)/shard_map/dot_general | solution.py:29
  51.6 0.0 copy-start.1
  51.7 0.1 stack.15
  51.8 1.1 %fusion.2 = (f32[192]{0:T(256)S(1)}, f32[192]{0:T(256)S(1)}, f32[192]{0:T(256)S(1)}) fusion(f32[192,4096]{1,0:T(8,128)S(1)} %get-tuple-element.22, f32[192]{0:T(256)S(1)} %get-tuple-element.21, s32[192]{0:T(256)S(1)} %broadcast_subtract_fusion), kind=kLoop, calls=%fused_computation.6 | loop fusion | flops 5504448 | bytes 3149568 | tf_op jit(solution)/shard_map/reduce_sum | solution.py:36
  52.9 0.1 stack.16
  53.0 0.1 stack.17
  53.1 0.1 stack.18
  53.2 0.1 convolution_bitcast_fusion
  53.4 0.6 copy.14
  54.0 4.0 %all-to-all-start = ((f32[16,5,12]{2,1,0:T(8,128)}), f32[16,5,12]{2,1,0:T(8,128)S(1)}, u32[]{:S(2)}, u32[]{:S(2)}) async-start(f32[16,5,12]{2,1,0:T(8,128)} %copy.14), calls=%async_computation | async-start | bytes 131072 | tf_op jit(solution)/shard_map/all_to_all | solution.py:81
  58.0 0.0 copy-done.1
  58.1 1.3 %fusion.23 = s32[]{:T(128)} fusion(s32[1,8]{1,0:T(1,128)S(1)} %copy-done.1, s32[]{:T(128)} %fusion.26), kind=kLoop, calls=%fused_computation.53 | loop fusion | flops 23 | bytes 40 | tf_op jit(solution)/shard_map/reduce_sum | solution.py:92
  59.4 5.6 %all-to-all-done = f32[16,5,12]{2,1,0:T(8,128)S(1)} async-done(((f32[16,5,12]{2,1,0:T(8,128)}), f32[16,5,12]{2,1,0:T(8,128)S(1)}, u32[]{:S(2)}, u32[]{:S(2)}) %all-to-all-start) | async-done | bytes 3872 | tf_op jit(solution)/shard_map/all_to_all | solution.py:81
  64.9 0.1 fusion.28
  65.0 1.1 %fusion.24 = (f32[1,12]{1,0:T(1,128)}, f32[1,12]{1,0:T(1,128)}, f32[1,12]{1,0:T(1,128)}, f32[1,12]{1,0:T(1,128)}) fusion(f32[12]{0:T(128)S(1)} %reduce_max.21, f32[12]{0:T(128)S(1)} %get-tuple-element.9, f32[12]{0:T(128)S(1)} %get-tuple-element.10, s32[]{:T(128)} %fusion.23, f32[12]{0:T(128)S(1)} %get-tuple-element.13, f32[12]{0:T(128)S(1)} %get-tuple-element.14), kind=kLoop, calls=%fused_computation.56 | loop fusion | flops 120 | bytes 436 | tf_op jit(solution)/shard_map/mul | solution.py:96
  (12 shorter events, 0.2 us)
Async XLA Ops:
  31.2 4.3 %collective-permute-start = (bf16[96,4224]{1,0:T(8,128)(2,1)S(1)}, bf16[96,4224]{1,0:T(8,128)(2,1)S(1)}, u32[]{:S(2)}, u32[]{:S(2)}) collective-permute-start(bf16[96,4224]{1,0:T(8,128)(2,1)S(1)} %all_gather.7), channel_id=1, source_target_pairs={{0,1},{1,0},{2,3},{3,2},{4,5},{5,4},{6,7},{7,6},{8,9},{9,8},{10,11... | collective-permute-start | bytes 2433032 | tf_op jit(solution)/shard_map/ppermute | solution.py:63
  35.8 1.2 %copy-start = (bf16[192,4224]{1,0:T(8,128)(2,1)}, bf16[192,4224]{1,0:T(8,128)(2,1)S(1)}, u32[]{:S(2)}) copy-start(bf16[192,4224]{1,0:T(8,128)(2,1)S(1)} %maximum_select_fusion) | copy-start | bytes 4866052
  51.6 6.4 %copy-start.1 = (s32[1,8]{1,0:T(1,128)S(1)}, s32[1,8]{1,0:T(1,128)}, u32[]{:S(2)}) copy-start(s32[1,8]{1,0:T(1,128)} %param.8) | copy-start | bytes 100
  54.0 10.9 %all-to-all-start = ((f32[16,5,12]{2,1,0:T(8,128)}), f32[16,5,12]{2,1,0:T(8,128)S(1)}, u32[]{:S(2)}, u32[]{:S(2)}) async-start(f32[16,5,12]{2,1,0:T(8,128)} %copy.14), calls=%async_computation | async-start | bytes 131072 | tf_op jit(solution)/shard_map/all_to_all | solution.py:81

commit v7 on v6

--- a/solution.py
+++ b/solution.py
@@ -1,6 +1,9 @@
+from functools import partial
+
 import jax
 import jax.numpy as jnp
 from jax import lax
+from jax.experimental import pallas as pl
 from jax.sharding import Mesh, PartitionSpec as P
 
 EPSILON = 1e-05
@@ -39,6 +42,31 @@
     )
 
 
+def pack_kernel(states_ref, gain_ref, ids_ref, out_ref, *, features, digits):
+    values = states_ref[...].astype(jnp.float32)
+    mean_square = jnp.mean(values * values, axis=1, keepdims=True)
+    normed = (values * lax.rsqrt(mean_square + EPSILON) * gain_ref[...]).astype(jnp.bfloat16)
+    out_ref[:, :features] = normed
+    ids = ids_ref[...]
+    count = ids.shape[1]
+    row = lax.broadcasted_iota(jnp.int32, (count, count), 0)
+    col = lax.broadcasted_iota(jnp.int32, (count, count), 1)
+    token = jnp.sum(jnp.where(row == col, jnp.broadcast_to(ids, (count, count)), 0), axis=1, keepdims=True)
+    lane = lax.broadcasted_iota(jnp.int32, (count, LANES), 1)
+    code = jnp.zeros((count, LANES), jnp.int32)
+    for k in range(digits):
+        code = jnp.where(lane == k, (token >> (RADIX_BITS * k)) & (RADIX - 1), code)
+    out_ref[:, features:] = code.astype(jnp.float32).astype(jnp.bfloat16)
+
+
+def pack_rows(block_states, gain, token_ids, digits):
+    count, features = block_states.shape
+    return pl.pallas_call(
+        partial(pack_kernel, features=features, digits=digits),
+        out_shape=jax.ShapeDtypeStruct((count, features + LANES), jnp.bfloat16),
+    )(block_states, gain.reshape(1, features), token_ids)
+
+
 def shards(states, target_ids, lengths, order, gain, head):
     count = states.shape[1]
     vocab_size = lax.axis_size(VOCAB)
@@ -49,19 +77,16 @@
     pair_base = group_index - core
     own_order = lax.dynamic_index_in_dim(order, group_index, 0, keepdims=False)
     block_ids = jnp.arange(vocab_size, dtype=jnp.int32)
-    normed, root_mean = normalize(states[0], gain)
+    root_mean = jnp.sqrt(jnp.mean(jnp.square(states[0].astype(jnp.float32)), axis=-1))
     width = head.shape[1]
-    features = normed.shape[1]
+    features = states.shape[2]
     digits = digit_count(width * vocab_size)
     place = RADIX ** jnp.arange(digits, dtype=jnp.int32)
-    shifts = RADIX_BITS * jnp.arange(digits, dtype=jnp.int32)
-    coded = ((target_ids[0][:, None] >> shifts[None, :]) & (RADIX - 1)).astype(jnp.bfloat16)
-    coded = jnp.pad(coded, ((0, 0), (0, LANES - digits)))
-    packed = jnp.concatenate([normed, coded], axis=1)
+    packed = pack_rows(states[0], gain, target_ids, digits)
     packed = lax.all_gather(packed, "vocab_lo", axis=0, tiled=True)
     packed = lax.all_gather(packed, "vocab_hi", axis=0, tiled=True)
     partner = lax.ppermute(packed, "grp_lo", [(0, 1), (1, 0)])
-    pair_rows = jnp.where(core == 0, jnp.concatenate([packed, partner]), jnp.concatenate([partner, packed]))
+    pair_rows = jnp.concatenate([packed, partner])
     pair_normed = pair_rows[:, :features]
     pair_ids = jnp.sum(pair_rows[:, features : features + digits].astype(jnp.int32) * place[None, :], axis=1)
     span = width // 2
@@ -70,8 +95,10 @@
     local_max, sums, expected, target = partial_stats(pair_normed, columns, pair_ids, offset)
     terms = jnp.stack([local_max, sums, expected, target]).reshape(4, 2, vocab_size, count)
     pair_order = lax.dynamic_slice_in_dim(order, pair_base, 2, 0)
+    pair_order = jnp.where(core == 0, pair_order, pair_order[::-1])
     route = (pair_order[:, None, :] == block_ids[None, :, None]).astype(jnp.float32)
     routed = jnp.einsum("cjs,kcsr->jckr", route, terms, precision=lax.Precision.HIGHEST)
+    routed = jnp.where(core == 0, routed, routed[:, ::-1])
     group_ids = jnp.arange(2, dtype=jnp.int32)
     home = own_order[vocab_index]
     root_slot = (block_ids[:, None] == home) & (group_ids[None, :] == core)

time: 66.5 us -> 68.7 us (1.033)
  Pallas kernels: 0 us -> 1.72 us
  local copies, waits for them, and re-layouts: 4.44 us -> 5.19 us
    convert_element_type x2 -> x0, other arithmetic: 1.74 us -> none  [the longest x1 1.01 us: normalize(): (values * lax.rsqrt(mean_square + EPSILON)[:, None] * gain).astype(jnp.bf...]
    pallas_call x0 -> x1, Pallas kernels: none -> 1.72 us  [pack_rows(): pl.pallas_call(partial(pack_kernel, features=features, digits=digits), ou...]
    concatenate x0 -> x1, local copies, waits for them, and re-layouts: none -> 0.96 us  [shards(): pair_rows = jnp.concatenate([packed, partner])]
    reduce_sum x1, other arithmetic: 0.11 us -> 0.91 us  [shards(): jnp.sum(pair_rows[:, features:features + digits].astype(jnp.int32) * plac...]
  transfers between devices with their start and end apart: 2 -> 2, of which waited for: 1 -> 1; matrix products, arithmetic and copies ran while one was open for 8% -> 12% of each run, Pallas kernels for 0% -> 0%
where the time goes in v7:
time: 68.7 us; the launch traced here: 68.3 us
  blocking collectives  27.9 us (41%)
  matrix products  14.7 us (21%)
  other arithmetic  8.44 us (12%)
  waiting for transfers between devices  5.58 us (8%)
  local copies, waits for them, and re-layouts  5.19 us (8%)
  starting transfers between devices  4.05 us (6%)
  Pallas kernels  1.72 us (3%)
  between operations  0.81 us (1%)
    all_gather x1, blocking collectives, shards(): packed = lax.all_gather(packed, 'vocab_hi', axis=0, tiled=True)  20.4 us
    dot_general x1, matrix products, partial_stats(): logits = jnp.dot(normed, columns, preferred_element_type=jnp.float32)  14.6 us
    all_gather x1, blocking collectives, shards(): packed = lax.all_gather(packed, 'vocab_lo', axis=0, tiled=True)  7.47 us
    all_to_all x1, waiting for transfers between devices, shards(): received = lax.all_to_all(payload, VOCAB + ('grp_lo',), 0, 0, tiled=True)  5.58 us
    all_to_all x1, starting transfers between devices, shards(): received = lax.all_to_all(payload, VOCAB + ('grp_lo',), 0, 0, tiled=True)  4.04 us
    pallas_call x1, Pallas kernels, pack_rows(): pl.pallas_call(partial(pack_kernel, features=features, digits=digits), ou...  1.72 us
  transfers between devices with their start and end apart: 2, of which 1 were waited for; matrix products, arithmetic and copies ran while one was open for 12% of the time, Pallas kernels for 0%

profile of v7, /device:TPU:0, one launch (start us, length us, event | category | flops | bytes accessed | tf_op | source)
XLA Modules:
  0.0 68.3 jit_solution(5981690104711435524)
XLA Ops:
  0.6 1.7 %shard_map.93 = bf16[12,4224]{1,0:T(8,128)(2,1)} custom-call(bf16[12,4096]{1,0:T(8,128)(2,1)} %bitcast.50, f32[1,4096]{1,0:T(1,128)} %bitcast.56, s32[1,12]{1,0:T(1,128)} %ids_ref.1), custom_call_target="tpu_custom_call" | custom-call | tf_op jit(solution)/shard_map/pallas_call | solution.py:64
  2.3 7.5 %all-gather = bf16[2,12,4224]{2,1,0:T(8,128)(2,1)S(1)} all-gather(bf16[1,12,4224]{2,1,0:T(8,128)(2,1)} %bitcast.49), channel_id=1, replica_groups=mesh['vocab_hi'=4,'vocab_lo'=2,'grp_hi'=2,'grp_lo'=2] {'vocab_lo'}, dimensions={0}, use_global_device_ids=true | all-gather | bytes 304128 | tf_op jit(solution)/shard_map/all_gather | solution.py:86
  9.8 0.1 reshape.203
  9.9 20.4 %all_gather.7 = bf16[96,4224]{1,0:T(8,128)(2,1)S(1)} all-gather(bf16[24,4224]{1,0:T(8,128)(2,1)S(1)} %reshape.203), channel_id=1, replica_groups=mesh['vocab_hi'=4,'vocab_lo'=2,'grp_hi'=2,'grp_lo'=2] {'vocab_hi'}, dimensions={0}, use_global_device_ids=true | all-gather | bytes 1013760 | tf_op jit(solution)/shard_map/all_gather | solution.py:87
  30.3 0.0 collective-permute-start
  30.3 1.1 %multiply_reduce_fusion.1 = f32[12]{0:T(128)S(1)} fusion(bf16[1,12,4096]{2,1,0:T(8,128)(2,1)} %param.6), kind=kLoop, calls=%fused_computation.9 | loop fusion | flops 147444 | bytes 98352 | tf_op jit(solution)/shard_map/reduce_sum | solution.py:80
  31.4 0.7 %constant_dynamic-slice_fusion = s32[2,8]{1,0:T(2,128)S(1)} fusion(s32[4,8]{1,0:T(4,128)} %param.9, s32[]{:T(128)S(6)} %select_n.123), kind=kLoop, calls=%fused_computation.42 | loop fusion | bytes 132 | tf_op jit(solution)/shard_map/dynamic_slice | solution.py:97
  32.1 0.7 %broadcast_select_fusion.1 = s32[2,8]{1,0:T(2,128)S(1)} fusion(s32[2,8]{1,0:T(2,128)S(1)} %rev.6, pred[]{:T(512)S(6)} %eq.69, s32[4,8]{1,0:T(4,128)} %param.9, s32[]{:T(128)S(6)} %select_n.123), kind=kLoop, calls=%fused_computation.39 | loop fusion | flops 16 | bytes 197 | tf_op jit(solution)/shard_map/jit(_where)/select_n | solution.py:98
  32.8 1.3 %dynamic_slice.16 = s32[1,1]{1,0:T(1,128)} dynamic-slice(s32[4,8]{1,0:T(4,128)} %param.9, s32[]{:T(128)S(6)} %select_n.126, s32[]{:T(128)S(6)} %select_n.128), dynamic_slice_sizes={1,1} | dynamic-slice | bytes 12 | tf_op jit(solution)/shard_map/dynamic_slice | solution.py:103
  34.0 0.6 iota_compare_fusion.3
  34.7 0.1 and.82
  34.8 0.1 and.79
  34.9 0.1 and.80
  35.0 1.3 %fusion.20 = s32[]{:T(128)} fusion(s32[4,8]{1,0:T(4,128)} %param.9, s32[]{:T(128)S(6)} %select_n.109, s32[]{:T(128)S(6)} %add.40), kind=kLoop, calls=%fused_computation.61 | loop fusion | flops 23 | bytes 44 | tf_op jit(solution)/shard_map/reduce_sum | solution.py:118
  36.3 0.1 broadcast_select_fusion
  36.4 0.9 %constant_dynamic-update-slice_fusion.1 = bf16[192,4224]{1,0:T(8,128)(2,1)} fusion(bf16[96,4224]{1,0:T(8,128)(2,1)S(1)} %all_gather.7), kind=kLoop, calls=%fused_computation.28 | loop fusion | bytes 1622016
  37.3 0.0 collective-permute-done
  37.3 1.0 %constant_dynamic-update-slice_fusion = bf16[192,4224]{1,0:T(8,128)(2,1)} fusion(bf16[192,4224]{1,0:T(8,128)(2,1)} %constant_dynamic-update-slice_fusion.1, bf16[96,4224]{1,0:T(8,128)(2,1)S(1)} %collective-permute-done), kind=kLoop, calls=%fused_computation.27 | loop fusion | bytes 1622016 | tf_op jit(solution)/shard_map/concatenate | solution.py:89
  38.3 0.9 %multiply_reduce_fusion.2 = s32[192]{0:T(256)S(1)} fusion(bf16[192,4224]{1,0:T(8,128)(2,1)} %constant_dynamic-update-slice_fusion, s32[2]{0:T(128)S(1)} %compare_select_fusion.5), kind=kLoop, calls=%fused_computation.10 | loop fusion | flops 960 | bytes 1544 | tf_op jit(solution)/shard_map/reduce_sum | solution.py:91
  39.2 14.6 %fusion.23 = (f32[192]{0:T(256)S(1)}, f32[192,4096]{1,0:T(8,128)S(1)}) fusion(bf16[4096,8192]{1,0:T(8,128)(2,1)} %param.11, s32[]{:T(128)S(6)} %select_n.114, bf16[192,4224]{1,0:T(8,128)(2,1)} %constant_dynamic-update-slice_fusion), kind=kOutput, calls=%fused_computation.64 | convolution fusion | flops 6443237376 | bytes 38273796 | tf_op jit(solution)/shard_map/dot_general | solution.py:32
  53.8 0.0 copy-start
  53.8 0.1 stack.15
  53.9 1.1 %fusion.2 = (f32[192]{0:T(256)S(1)}, f32[192]{0:T(256)S(1)}, f32[192]{0:T(256)S(1)}) fusion(f32[192,4096]{1,0:T(8,128)S(1)} %get-tuple-element.20, f32[192]{0:T(256)S(1)} %get-tuple-element.19, s32[192]{0:T(256)S(1)} %broadcast_subtract_fusion), kind=kLoop, calls=%fused_computation.6 | loop fusion | flops 5504448 | bytes 3149568 | tf_op jit(solution)/shard_map/reduce_sum | solution.py:39
  55.0 0.1 stack.16
  55.1 0.1 stack.17
  55.2 0.1 stack.18
  55.3 0.1 convolution_bitcast_fusion
  55.5 0.6 copy.14
  56.1 4.0 %all-to-all-start = ((f32[16,5,12]{2,1,0:T(8,128)}), f32[16,5,12]{2,1,0:T(8,128)S(1)}, u32[]{:S(2)}, u32[]{:S(2)}) async-start(f32[16,5,12]{2,1,0:T(8,128)} %copy.14), calls=%async_computation | async-start | bytes 131072 | tf_op jit(solution)/shard_map/all_to_all | solution.py:108
  60.2 0.0 copy-done
  60.2 1.3 %fusion.17 = s32[]{:T(128)} fusion(s32[1,8]{1,0:T(1,128)S(1)} %copy-done, s32[]{:T(128)} %fusion.20), kind=kLoop, calls=%fused_computation.47 | loop fusion | flops 23 | bytes 40 | tf_op jit(solution)/shard_map/reduce_sum | solution.py:119
  61.5 5.6 %all-to-all-done = f32[16,5,12]{2,1,0:T(8,128)S(1)} async-done(((f32[16,5,12]{2,1,0:T(8,128)}), f32[16,5,12]{2,1,0:T(8,128)S(1)}, u32[]{:S(2)}, u32[]{:S(2)}) %all-to-all-start) | async-done | bytes 3872 | tf_op jit(solution)/shard_map/all_to_all | solution.py:108
  67.1 0.1 fusion.22
  67.2 1.1 %fusion.18 = (f32[1,12]{1,0:T(1,128)}, f32[1,12]{1,0:T(1,128)}, f32[1,12]{1,0:T(1,128)}, f32[1,12]{1,0:T(1,128)}) fusion(f32[12]{0:T(128)S(1)} %reduce_max.21, f32[12]{0:T(128)S(1)} %get-tuple-element.9, f32[12]{0:T(128)S(1)} %get-tuple-element.10, s32[]{:T(128)} %fusion.17, f32[12]{0:T(128)S(1)} %get-tuple-element.13, f32[12]{0:T(128)S(1)} %get-tuple-element.14), kind=kLoop, calls=%fused_computation.50 | loop fusion | flops 120 | bytes 436 | tf_op jit(solution)/shard_map/mul | solution.py:123
  (12 shorter events, 0.2 us)
Async XLA Ops:
  30.3 7.1 %collective-permute-start = (bf16[96,4224]{1,0:T(8,128)(2,1)S(1)}, bf16[96,4224]{1,0:T(8,128)(2,1)S(1)}, u32[]{:S(2)}, u32[]{:S(2)}) collective-permute-start(bf16[96,4224]{1,0:T(8,128)(2,1)S(1)} %all_gather.7), channel_id=1, source_target_pairs={{0,1},{1,0},{2,3},{3,2},{4,5},{5,4},{6,7},{7,6},{8,9},{9,8},{10,11... | collective-permute-start | bytes 2433032 | tf_op jit(solution)/shard_map/ppermute | solution.py:88
  53.8 6.4 %copy-start = (s32[1,8]{1,0:T(1,128)S(1)}, s32[1,8]{1,0:T(1,128)}, u32[]{:S(2)}) copy-start(s32[1,8]{1,0:T(1,128)} %param.8) | copy-start | bytes 100
  56.1 10.9 %all-to-all-start = ((f32[16,5,12]{2,1,0:T(8,128)}), f32[16,5,12]{2,1,0:T(8,128)S(1)}, u32[]{:S(2)}, u32[]{:S(2)}) async-start(f32[16,5,12]{2,1,0:T(8,128)} %copy.14), calls=%async_computation | async-start | bytes 131072 | tf_op jit(solution)/shard_map/all_to_all | solution.py:108

commit v8 on v7

--- a/solution.py
+++ b/solution.py
@@ -86,7 +86,7 @@
     packed = lax.all_gather(packed, "vocab_lo", axis=0, tiled=True)
     packed = lax.all_gather(packed, "vocab_hi", axis=0, tiled=True)
     partner = lax.ppermute(packed, "grp_lo", [(0, 1), (1, 0)])
-    pair_rows = jnp.concatenate([packed, partner])
+    pair_rows = jnp.where(core == 0, jnp.concatenate([packed, partner]), jnp.concatenate([partner, packed]))
     pair_normed = pair_rows[:, :features]
     pair_ids = jnp.sum(pair_rows[:, features : features + digits].astype(jnp.int32) * place[None, :], axis=1)
     span = width // 2
@@ -95,10 +95,8 @@
     local_max, sums, expected, target = partial_stats(pair_normed, columns, pair_ids, offset)
     terms = jnp.stack([local_max, sums, expected, target]).reshape(4, 2, vocab_size, count)
     pair_order = lax.dynamic_slice_in_dim(order, pair_base, 2, 0)
-    pair_order = jnp.where(core == 0, pair_order, pair_order[::-1])
     route = (pair_order[:, None, :] == block_ids[None, :, None]).astype(jnp.float32)
     routed = jnp.einsum("cjs,kcsr->jckr", route, terms, precision=lax.Precision.HIGHEST)
-    routed = jnp.where(core == 0, routed, routed[:, ::-1])
     group_ids = jnp.arange(2, dtype=jnp.int32)
     home = own_order[vocab_index]
     root_slot = (block_ids[:, None] == home) & (group_ids[None, :] == core)

time: 68.7 us -> 67.5 us (0.983)
  local copies, waits for them, and re-layouts: 5.19 us -> 3.26 us
  other arithmetic: 8.44 us -> 9.23 us
    concatenate x1 -> x0, local copies, waits for them, and re-layouts: 0.96 us -> none  [shards(): pair_rows = jnp.concatenate([packed, partner])]
    unnamed x4 -> x3, local copies, waits for them, and re-layouts: 1 us -> 0.06 us
    select_n x2 -> x1, other arithmetic: 0.7 us -> 1.49 us  [shards(): jnp.where(core == 0, jnp.concatenate([packed, partner]), jnp.concatenate(...]
  transfers between devices with their start and end apart: 2 -> 2, of which waited for: 1 -> 1; matrix products, arithmetic and copies ran while one was open for 12% -> 10% of each run, Pallas kernels for 0% -> 0%
where the time goes in v8:
time: 67.5 us; the launch traced here: 67.2 us
  blocking collectives  27.9 us (41%)
  matrix products  14.7 us (22%)
  other arithmetic  9.23 us (14%)
  waiting for transfers between devices  5.58 us (8%)
  starting transfers between devices  4.03 us (6%)
  local copies, waits for them, and re-layouts  3.26 us (5%)
  Pallas kernels  1.72 us (3%)
  between operations  0.79 us (1%)
    all_gather x1, blocking collectives, shards(): packed = lax.all_gather(packed, 'vocab_hi', axis=0, tiled=True)  20.4 us
    dot_general x1, matrix products, partial_stats(): logits = jnp.dot(normed, columns, preferred_element_type=jnp.float32)  14.6 us
    all_gather x1, blocking collectives, shards(): packed = lax.all_gather(packed, 'vocab_lo', axis=0, tiled=True)  7.47 us
    all_to_all x1, waiting for transfers between devices, shards(): received = lax.all_to_all(payload, VOCAB + ('grp_lo',), 0, 0, tiled=True)  5.58 us
    all_to_all x1, starting transfers between devices, shards(): received = lax.all_to_all(payload, VOCAB + ('grp_lo',), 0, 0, tiled=True)  4.03 us
    pallas_call x1, Pallas kernels, pack_rows(): pl.pallas_call(partial(pack_kernel, features=features, digits=digits), ou...  1.72 us
    select_n x1, other arithmetic, shards(): jnp.where(core == 0, jnp.concatenate([packed, partner]), jnp.concatenate(...  1.49 us
  transfers between devices with their start and end apart: 2, of which 1 were waited for; matrix products, arithmetic and copies ran while one was open for 10% of the time, Pallas kernels for 0%

profile of v8, /device:TPU:0, one launch (start us, length us, event | category | flops | bytes accessed | tf_op | source)
XLA Modules:
  0.0 67.2 jit_solution(9727285599272672927)
XLA Ops:
  0.6 1.7 %shard_map.93 = bf16[12,4224]{1,0:T(8,128)(2,1)} custom-call(bf16[12,4096]{1,0:T(8,128)(2,1)} %bitcast.50, f32[1,4096]{1,0:T(1,128)} %bitcast.56, s32[1,12]{1,0:T(1,128)} %ids_ref.1), custom_call_target="tpu_custom_call" | custom-call | tf_op jit(solution)/shard_map/pallas_call | solution.py:64
  2.3 7.5 %all-gather = bf16[2,12,4224]{2,1,0:T(8,128)(2,1)S(1)} all-gather(bf16[1,12,4224]{2,1,0:T(8,128)(2,1)} %bitcast.49), channel_id=1, replica_groups=mesh['vocab_hi'=4,'vocab_lo'=2,'grp_hi'=2,'grp_lo'=2] {'vocab_lo'}, dimensions={0}, use_global_device_ids=true | all-gather | bytes 304128 | tf_op jit(solution)/shard_map/all_gather | solution.py:86
  9.8 0.1 reshape.203
  9.9 20.4 %all_gather.7 = bf16[96,4224]{1,0:T(8,128)(2,1)S(1)} all-gather(bf16[24,4224]{1,0:T(8,128)(2,1)S(1)} %reshape.203), channel_id=1, replica_groups=mesh['vocab_hi'=4,'vocab_lo'=2,'grp_hi'=2,'grp_lo'=2] {'vocab_hi'}, dimensions={0}, use_global_device_ids=true | all-gather | bytes 1013760 | tf_op jit(solution)/shard_map/all_gather | solution.py:87
  30.3 0.0 collective-permute-start
  30.3 1.3 %dynamic_slice.16 = s32[1,1]{1,0:T(1,128)} dynamic-slice(s32[4,8]{1,0:T(4,128)} %param.9, s32[]{:T(128)S(6)} %select_n.116, s32[]{:T(128)S(6)} %select_n.118), dynamic_slice_sizes={1,1} | dynamic-slice | bytes 12 | tf_op jit(solution)/shard_map/dynamic_slice | solution.py:101
  31.6 0.6 iota_compare_fusion.3
  32.2 0.1 and.82
  32.3 0.1 and.79
  32.4 0.1 and.80
  32.5 1.3 %fusion.20 = s32[]{:T(128)} fusion(s32[4,8]{1,0:T(4,128)} %param.9, s32[]{:T(128)S(6)} %select_n.101, s32[]{:T(128)S(6)} %add.40), kind=kLoop, calls=%fused_computation.58 | loop fusion | flops 23 | bytes 44 | tf_op jit(solution)/shard_map/reduce_sum | solution.py:116
  33.8 0.7 %constant_dynamic-slice_fusion = s32[2,8]{1,0:T(2,128)S(1)} fusion(s32[4,8]{1,0:T(4,128)} %param.9, s32[]{:T(128)S(6)} %select_n.115), kind=kLoop, calls=%fused_computation.39 | loop fusion | bytes 132 | tf_op jit(solution)/shard_map/dynamic_slice | solution.py:97
  34.5 1.0 %multiply_reduce_fusion.1 = f32[12]{0:T(128)S(1)} fusion(bf16[1,12,4096]{2,1,0:T(8,128)(2,1)} %param.6), kind=kLoop, calls=%fused_computation.10 | loop fusion | flops 147444 | bytes 98352 | tf_op jit(solution)/shard_map/reduce_sum | solution.py:80
  35.6 0.1 broadcast_select_fusion
  35.7 0.0 collective-permute-done
  35.7 1.5 %maximum_select_fusion = bf16[192,4224]{1,0:T(8,128)(2,1)} fusion(bf16[96,4224]{1,0:T(8,128)(2,1)S(1)} %collective-permute-done, bf16[96,4224]{1,0:T(8,128)(2,1)S(1)} %all_gather.7, pred[]{:T(512)S(6)} %eq.68), kind=kLoop, calls=%fused_computation.7 | loop fusion | flops 7299072 | bytes 3244033 | tf_op jit(solution)/shard_map/jit(_where)/select_n | solution.py:89
  37.2 0.9 %multiply_reduce_fusion.2 = s32[192]{0:T(256)S(1)} fusion(bf16[192,4224]{1,0:T(8,128)(2,1)} %maximum_select_fusion, s32[2]{0:T(128)S(1)} %compare_select_fusion.5), kind=kLoop, calls=%fused_computation.11 | loop fusion | flops 960 | bytes 1544 | tf_op jit(solution)/shard_map/reduce_sum | solution.py:91
  38.1 14.6 %fusion.23 = (f32[192]{0:T(256)S(1)}, f32[192,4096]{1,0:T(8,128)S(1)}) fusion(bf16[4096,8192]{1,0:T(8,128)(2,1)} %param.11, s32[]{:T(128)S(6)} %select_n.107, bf16[192,4224]{1,0:T(8,128)(2,1)} %maximum_select_fusion), kind=kOutput, calls=%fused_computation.61 | convolution fusion | flops 6443237376 | bytes 38273796 | tf_op jit(solution)/shard_map/dot_general | solution.py:32
  52.6 0.0 copy-start
  52.6 0.1 stack.15
  52.7 1.1 %fusion.2 = (f32[192]{0:T(256)S(1)}, f32[192]{0:T(256)S(1)}, f32[192]{0:T(256)S(1)}) fusion(f32[192,4096]{1,0:T(8,128)S(1)} %get-tuple-element.20, f32[192]{0:T(256)S(1)} %get-tuple-element.19, s32[192]{0:T(256)S(1)} %broadcast_subtract_fusion), kind=kLoop, calls=%fused_computation.6 | loop fusion | flops 5504448 | bytes 3149568 | tf_op jit(solution)/shard_map/reduce_sum | solution.py:39
  53.9 0.1 stack.16
  54.0 0.1 stack.17
  54.1 0.1 stack.18
  54.1 0.1 convolution_bitcast_fusion
  54.3 0.6 copy.14
  55.0 4.0 %all-to-all-start = ((f32[16,5,12]{2,1,0:T(8,128)}), f32[16,5,12]{2,1,0:T(8,128)S(1)}, u32[]{:S(2)}, u32[]{:S(2)}) async-start(f32[16,5,12]{2,1,0:T(8,128)} %copy.14), calls=%async_computation | async-start | bytes 131072 | tf_op jit(solution)/shard_map/all_to_all | solution.py:106
  59.0 0.0 copy-done
  59.0 1.3 %fusion.17 = s32[]{:T(128)} fusion(s32[1,8]{1,0:T(1,128)S(1)} %copy-done, s32[]{:T(128)} %fusion.20), kind=kLoop, calls=%fused_computation.44 | loop fusion | flops 23 | bytes 40 | tf_op jit(solution)/shard_map/reduce_sum | solution.py:117
  60.3 5.6 %all-to-all-done = f32[16,5,12]{2,1,0:T(8,128)S(1)} async-done(((f32[16,5,12]{2,1,0:T(8,128)}), f32[16,5,12]{2,1,0:T(8,128)S(1)}, u32[]{:S(2)}, u32[]{:S(2)}) %all-to-all-start) | async-done | bytes 3872 | tf_op jit(solution)/shard_map/all_to_all | solution.py:106
  65.9 0.1 fusion.22
  66.0 1.1 %fusion.18 = (f32[1,12]{1,0:T(1,128)}, f32[1,12]{1,0:T(1,128)}, f32[1,12]{1,0:T(1,128)}, f32[1,12]{1,0:T(1,128)}) fusion(f32[12]{0:T(128)S(1)} %reduce_max.21, f32[12]{0:T(128)S(1)} %get-tuple-element.9, f32[12]{0:T(128)S(1)} %get-tuple-element.10, s32[]{:T(128)} %fusion.17, f32[12]{0:T(128)S(1)} %get-tuple-element.13, f32[12]{0:T(128)S(1)} %get-tuple-element.14), kind=kLoop, calls=%fused_computation.47 | loop fusion | flops 120 | bytes 436 | tf_op jit(solution)/shard_map/mul | solution.py:121
  (10 shorter events, 0.1 us)
Async XLA Ops:
  30.3 5.4 %collective-permute-start = (bf16[96,4224]{1,0:T(8,128)(2,1)S(1)}, bf16[96,4224]{1,0:T(8,128)(2,1)S(1)}, u32[]{:S(2)}, u32[]{:S(2)}) collective-permute-start(bf16[96,4224]{1,0:T(8,128)(2,1)S(1)} %all_gather.7), channel_id=1, source_target_pairs={{0,1},{1,0},{2,3},{3,2},{4,5},{5,4},{6,7},{7,6},{8,9},{9,8},{10,11... | collective-permute-start | bytes 2433032 | tf_op jit(solution)/shard_map/ppermute | solution.py:88
  52.6 6.4 %copy-start = (s32[1,8]{1,0:T(1,128)S(1)}, s32[1,8]{1,0:T(1,128)}, u32[]{:S(2)}) copy-start(s32[1,8]{1,0:T(1,128)} %param.8) | copy-start | bytes 100
  55.0 10.9 %all-to-all-start = ((f32[16,5,12]{2,1,0:T(8,128)}), f32[16,5,12]{2,1,0:T(8,128)S(1)}, u32[]{:S(2)}, u32[]{:S(2)}) async-start(f32[16,5,12]{2,1,0:T(8,128)} %copy.14), calls=%async_computation | async-start | bytes 131072 | tf_op jit(solution)/shard_map/all_to_all | solution.py:106

commit v9 on v6

--- a/solution.py
+++ b/solution.py
@@ -9,6 +9,7 @@
 VOCAB = ("vocab_hi", "vocab_lo")
 GROUP = ("grp_hi", "grp_lo")
 LANES = 128
+PIPELINE_LIMIT = 4
 
 
 def digit_count(total):
@@ -25,8 +26,9 @@
     return (normed, jnp.sqrt(mean_square))
 
 
-def partial_stats(normed, columns, token_ids, offset):
-    logits = jnp.dot(normed, columns, preferred_element_type=jnp.float32)
+def partial_stats(rows, columns, features, digits, place, offset):
+    token_ids = jnp.sum(rows[:, features : features + digits].astype(jnp.int32) * place[None, :], axis=1)
+    logits = jnp.dot(rows[:, :features], columns, preferred_element_type=jnp.float32)
     local_max = jnp.max(logits, axis=1)
     weights = jnp.exp(logits - local_max[:, None])
     within = token_ids - offset
@@ -37,7 +39,6 @@
         jnp.sum(weights * logits, axis=1),
         jnp.sum(jnp.where(column == within[:, None], logits, 0.0), axis=1),
     )
-
 
 def shards(states, target_ids, lengths, order, gain, head):
     count = states.shape[1]
@@ -58,20 +59,51 @@
     coded = ((target_ids[0][:, None] >> shifts[None, :]) & (RADIX - 1)).astype(jnp.bfloat16)
     coded = jnp.pad(coded, ((0, 0), (0, LANES - digits)))
     packed = jnp.concatenate([normed, coded], axis=1)
-    packed = lax.all_gather(packed, "vocab_lo", axis=0, tiled=True)
-    packed = lax.all_gather(packed, "vocab_hi", axis=0, tiled=True)
-    partner = lax.ppermute(packed, "grp_lo", [(0, 1), (1, 0)])
-    pair_rows = jnp.where(core == 0, jnp.concatenate([packed, partner]), jnp.concatenate([partner, packed]))
-    pair_normed = pair_rows[:, :features]
-    pair_ids = jnp.sum(pair_rows[:, features : features + digits].astype(jnp.int32) * place[None, :], axis=1)
     span = width // 2
     columns = lax.dynamic_slice_in_dim(head, core * span, span, 1)
     offset = vocab_index * width + core * span
-    local_max, sums, expected, target = partial_stats(pair_normed, columns, pair_ids, offset)
-    terms = jnp.stack([local_max, sums, expected, target]).reshape(4, 2, vocab_size, count)
+    low_size = lax.axis_size("vocab_lo")
+    high_size = lax.axis_size("vocab_hi")
+    high_index = lax.axis_index("vocab_hi")
+    near = lax.all_gather(packed, "vocab_lo", axis=0, tiled=True)
+    swap = [(0, 1), (1, 0)]
+    if high_size <= PIPELINE_LIMIT:
+        far = [
+            lax.ppermute(near, "vocab_hi", [(i, (i + shift) % high_size) for i in range(high_size)])
+            for shift in range(1, high_size)
+        ]
+        near_rows = jnp.concatenate([near, lax.ppermute(near, "grp_lo", swap)])
+        near_stats = partial_stats(near_rows, columns, features, digits, place, offset)
+        far_own = jnp.concatenate(far)
+        far_rows = jnp.concatenate([far_own, lax.ppermute(far_own, "grp_lo", swap)])
+        far_stats = partial_stats(far_rows, columns, features, digits, place, offset)
+        near_count = near.shape[0]
+        far_count = far_own.shape[0]
+        positions = jnp.arange(vocab_size, dtype=jnp.int32)
+        block_of = ((high_index - positions // low_size) % high_size) * low_size + positions % low_size
+        terms = jnp.stack(
+            [
+                jnp.concatenate(
+                    [
+                        jnp.concatenate([near_stat[:near_count], far_stat[:far_count]]),
+                        jnp.concatenate([near_stat[near_count:], far_stat[far_count:]]),
+                    ]
+                )
+                for near_stat, far_stat in zip(near_stats, far_stats)
+            ]
+        ).reshape(4, 2, vocab_size, count)
+    else:
+        own_rows = lax.all_gather(near, "vocab_hi", axis=0, tiled=True)
+        pair_rows = jnp.concatenate([own_rows, lax.ppermute(own_rows, "grp_lo", swap)])
+        terms = jnp.stack(partial_stats(pair_rows, columns, features, digits, place, offset))
+        terms = terms.reshape(4, 2, vocab_size, count)
+        block_of = block_ids
     pair_order = lax.dynamic_slice_in_dim(order, pair_base, 2, 0)
+    pair_order = jnp.where(core == 0, pair_order, pair_order[::-1])
+    pair_order = jnp.take(pair_order, block_of, axis=1)
     route = (pair_order[:, None, :] == block_ids[None, :, None]).astype(jnp.float32)
     routed = jnp.einsum("cjs,kcsr->jckr", route, terms, precision=lax.Precision.HIGHEST)
+    routed = jnp.where(core == 0, routed, routed[:, ::-1])
     group_ids = jnp.arange(2, dtype=jnp.int32)
     home = own_order[vocab_index]
     root_slot = (block_ids[:, None] == home) & (group_ids[None, :] == core)

time: 66.5 us -> 67.4 us (1.014)
  blocking collectives: 27.7 us -> 7.21 us
  matrix products: 14.7 us -> 27.6 us
  starting transfers between devices: 4.04 us -> 10.7 us
  waiting for transfers between devices: 5.58 us -> 6.61 us
  other arithmetic: 8.99 us -> 9.9 us
    all_gather x2 -> x1, blocking collectives: 27.7 us -> 7.21 us  [shards(): near = lax.all_gather(packed, 'vocab_lo', axis=0, tiled=True)]
    dot_general x1 -> x2, matrix products: 14.6 us -> 27.4 us  [partial_stats(): jnp.dot(rows[:, :features], columns, preferred_element_type=jnp.float32)]
    ppermute x1 -> x5, starting transfers between devices: 0.01 us -> 5.48 us  [the longest x3 4.91 us: shards(): lax.ppermute(near, 'vocab_hi', [(i, (i + shift) % high_size) for i in ran...]
    all_to_all x1, starting transfers between devices: 4.04 us -> 5.17 us  [shards(): received = lax.all_to_all(payload, VOCAB + ('grp_lo',), 0, 0, tiled=True)]
    mul x0 -> x1, other arithmetic: none -> 1.12 us  [shards(): own_root * keep]
    ppermute x1 -> x5, waiting for transfers between devices: 0.01 us -> 1.04 us  [the longest x1 1.02 us: shards(): far_rows = jnp.concatenate([far_own, lax.ppermute(far_own, 'grp_lo', swap)])]
    reduce_sum x1, other arithmetic: 1.33 us -> 0.64 us  [shards(): source_block = jnp.sum(jnp.where(own_order == vocab_index, block_ids, 0))]
    dynamic_slice x1, local copies, waits for them, and re-layouts: 1.27 us -> 0.58 us  [shards(): home = own_order[vocab_index]]
  transfers between devices with their start and end apart: 2 -> 6, of which waited for: 1 -> 2; matrix products, arithmetic and copies ran while one was open for 8% -> 28% of each run, Pallas kernels for 0% -> 0%
where the time goes in v9:
time: 67.4 us; the launch traced here: 67.1 us
  matrix products  27.6 us (41%)
  starting transfers between devices  10.7 us (16%)
  other arithmetic  9.9 us (15%)
  blocking collectives  7.21 us (11%)
  waiting for transfers between devices  6.61 us (10%)
  local copies, waits for them, and re-layouts  4.31 us (6%)
  between operations  0.88 us (1%)
    dot_general x2, matrix products, partial_stats(): jnp.dot(rows[:, :features], columns, preferred_element_type=jnp.float32)  27.4 us
    all_gather x1, blocking collectives, shards(): near = lax.all_gather(packed, 'vocab_lo', axis=0, tiled=True)  7.21 us
    all_to_all x1, waiting for transfers between devices, shards(): received = lax.all_to_all(payload, VOCAB + ('grp_lo',), 0, 0, tiled=True)  5.58 us
    all_to_all x1, starting transfers between devices, shards(): received = lax.all_to_all(payload, VOCAB + ('grp_lo',), 0, 0, tiled=True)  5.17 us
    ppermute x3, starting transfers between devices, shards(): lax.ppermute(near, 'vocab_hi', [(i, (i + shift) % high_size) for i in ran...  4.91 us
  transfers between devices with their start and end apart: 6, of which 2 were waited for; matrix products, arithmetic and copies ran while one was open for 28% of the time, Pallas kernels for 0%

profile of v9, /device:TPU:0, one launch (start us, length us, event | category | flops | bytes accessed | tf_op | source)
XLA Modules:
  0.0 67.1 jit_solution(11750708471200411875)
XLA Ops:
  0.6 0.0 copy-start.1
  0.7 1.1 %fusion.9 = f32[12]{0:T(128)S(1)} fusion(bf16[1,12,4096]{2,1,0:T(8,128)(2,1)} %param.6), kind=kLoop, calls=%fused_computation.23 | loop fusion | flops 147444 | bytes 98352 | tf_op jit(solution)/shard_map/reduce_sum | solution.py:24
  1.7 0.7 %and_convert_fusion = bf16[12,2]{1,0:T(8,128)(2,1)S(1)} fusion(s32[2]{0:T(128)S(1)} %iota_multiply_fusion, s32[12]{0:T(128)} %bitcast.61), kind=kLoop, calls=%fused_computation.51 | loop fusion | flops 72 | bytes 104 | tf_op jit(solution)/shard_map/convert_element_type | solution.py:59
  2.4 1.0 %fusion.11 = bf16[12,4096]{1,0:T(8,128)(2,1)S(1)} fusion(bf16[1,12,4096]{2,1,0:T(8,128)(2,1)} %param.6, f32[4096]{0:T(1024)} %param.10, f32[12]{0:T(128)S(1)} %get-tuple-element.38), kind=kLoop, calls=%fused_computation.25 | loop fusion | flops 196608 | bytes 213040 | tf_op jit(solution)/shard_map/convert_element_type | solution.py:25
  3.5 7.2 %all-gather = bf16[2,12,4224]{2,1,0:T(8,128)(2,1)S(1)} all-gather(bf16[1,12,4224]{2,1,0:T(8,128)(2,1)S(1)} %fusion.13), channel_id=1, replica_groups=mesh['vocab_hi'=4,'vocab_lo'=2,'grp_hi'=2,'grp_lo'=2] {'vocab_lo'}, dimensions={0}, use_global_device_ids=true | all-gather | bytes 304128 | tf_op jit(solution)/shard_map/all_gather | solution.py:68
  10.7 0.1 reshape.341
  10.7 3.9 %collective-permute-start.3 = (bf16[24,4224]{1,0:T(8,128)(2,1)S(1)}, bf16[24,4224]{1,0:T(8,128)(2,1)S(1)}, u32[]{:S(2)}, u32[]{:S(2)}) collective-permute-start(bf16[24,4224]{1,0:T(8,128)(2,1)S(1)} %reshape.341), channel_id=1, source_target_pairs={{0,24},{8,0},{16,8},{24,16},{1,25},{9,1},{17,9},{25,17},{2,26},{10... | collective-permute-start | bytes 608264 | tf_op jit(solution)/shard_map/ppermute | solution.py:72
  14.6 0.0 collective-permute-start.2
  14.6 1.0 %collective-permute-start.1 = (bf16[24,4224]{1,0:T(8,128)(2,1)S(1)}, bf16[24,4224]{1,0:T(8,128)(2,1)S(1)}, u32[]{:S(2)}, u32[]{:S(2)}) collective-permute-start(bf16[24,4224]{1,0:T(8,128)(2,1)S(1)} %reshape.341), channel_id=1, source_target_pairs={{0,8},{8,16},{16,24},{24,0},{1,9},{9,17},{17,25},{25,1},{2,10},{10... | collective-permute-start | bytes 608264 | tf_op jit(solution)/shard_map/ppermute | solution.py:72
  15.7 0.0 collective-permute-start
  15.8 0.0 copy-done.1
  15.8 0.6 fusion.40
  16.4 0.6 dynamic_slice.16
  17.0 0.6 iota_compare_fusion.5
  17.6 0.1 and.178
  17.7 0.1 and.175
  17.8 0.1 and.176
  17.9 0.1 copy.24
  18.0 0.1 rev.6
  18.1 0.6 gather_fusion
  18.6 0.1 select_bitcast_fusion
  18.7 0.1 copy.18
  18.8 0.1 broadcast_select_fusion
  18.9 0.0 collective-permute-done
  18.9 0.1 multiply_reduce_fusion.3
  19.0 13.8 %fusion.52 = (f32[48]{0:T(128)S(1)}, f32[48,4096]{1,0:T(8,128)S(1)}) fusion(bf16[4096,8192]{1,0:T(8,128)(2,1)} %param.11, s32[]{:T(128)S(6)} %select_n.201, bf16[48,4224]{1,0:T(8,128)(2,1)S(1)} %constant_dynamic-update-slice_fusion), kind=kOutput, calls=%fused_computation.135 | convolution fusion | flops 1610809344 | bytes 34734276 | tf_op jit(solution)/shard_map/dot_general | solution.py:31
  32.8 0.1 fusion.47
  32.9 0.0 collective-permute-done.3
  32.9 0.0 collective-permute-done.2
  32.9 0.0 collective-permute-done.1
  33.0 0.6 collective-permute-start.4
  33.5 0.4 fusion.6
  34.0 0.1 fusion.48
  34.1 0.1 fusion.50
  34.2 1.0 %collective-permute-done.4 = bf16[72,4224]{1,0:T(8,128)(2,1)S(1)} collective-permute-done((bf16[72,4224]{1,0:T(8,128)(2,1)S(1)}, bf16[72,4224]{1,0:T(8,128)(2,1)S(1)}, u32[]{:S(2)}, u32[]{:S(2)}) %collective-permute-start.4) | collective-permute-done | bytes 608288 | tf_op jit(solution)/shard_map/ppermute | solution.py:78
  35.2 0.1 constant_dynamic-update-slice_fusion.2
  35.3 0.0 copy-start
  35.3 1.0 %copy-done = bf16[144,4224]{1,0:T(8,128)(2,1)} copy-done((bf16[144,4224]{1,0:T(8,128)(2,1)}, bf16[144,4224]{1,0:T(8,128)(2,1)S(1)}, u32[]{:S(2)}) %copy-start) | copy-done | bytes 1216536
  36.3 0.1 multiply_reduce_fusion.2
  36.4 13.6 %fusion.51 = (f32[144]{0:T(256)S(1)}, f32[144,4096]{1,0:T(8,128)S(1)}) fusion(bf16[4096,8192]{1,0:T(8,128)(2,1)} %param.11, s32[]{:T(128)S(6)} %select_n.201, bf16[144,4224]{1,0:T(8,128)(2,1)} %copy-done), kind=kOutput, calls=%fused_computation.134 | convolution fusion | flops 4832428032 | bytes 37093956 | tf_op jit(solution)/shard_map/dot_general | solution.py:31
  50.1 0.1 fusion.43
  50.1 0.0 copy-start.2
  50.1 0.9 %fusion.4 = (f32[144]{0:T(256)S(1)}, f32[144]{0:T(256)S(1)}, f32[144]{0:T(256)S(1)}) fusion(f32[144,4096]{1,0:T(8,128)S(1)} %get-tuple-element.41, f32[144]{0:T(256)S(1)} %get-tuple-element.40, s32[144]{0:T(256)S(1)} %broadcast_subtract_fusion), kind=kLoop, calls=%fused_computation.9 | loop fusion | flops 4128336 | bytes 2362176 | tf_op jit(solution)/shard_map/reduce_sum | solution.py:38
  51.0 0.1 fusion.46
  51.1 0.1 pad_maximum_fusion.5
  51.2 0.1 stack.18
  51.3 0.1 pad_maximum_fusion.2
  51.4 0.1 stack.15
  51.5 0.1 fusion.44
  51.5 0.1 pad_maximum_fusion.3
  51.6 0.1 stack.16
  51.7 0.1 pad_maximum_fusion.4
  51.8 0.1 stack.17
  51.9 0.1 convolution_bitcast_fusion
  52.1 0.6 copy.20
  52.7 5.2 %all-to-all-start = ((f32[16,5,12]{2,1,0:T(8,128)}), f32[16,5,12]{2,1,0:T(8,128)S(1)}, u32[]{:S(2)}, u32[]{:S(2)}) async-start(f32[16,5,12]{2,1,0:T(8,128)} %copy.20), calls=%async_computation | async-start | bytes 131072 | tf_op jit(solution)/shard_map/all_to_all | solution.py:113
  57.9 0.0 copy-done.2
  57.9 1.3 %fusion.32 = s32[]{:T(128)} fusion(s32[1,8]{1,0:T(1,128)S(1)} %copy-done.2, s32[]{:T(128)} %fusion.40), kind=kLoop, calls=%fused_computation.101 | loop fusion | flops 23 | bytes 40 | tf_op jit(solution)/shard_map/reduce_sum | solution.py:124
  59.2 5.6 %all-to-all-done = f32[16,5,12]{2,1,0:T(8,128)S(1)} async-done(((f32[16,5,12]{2,1,0:T(8,128)}), f32[16,5,12]{2,1,0:T(8,128)S(1)}, u32[]{:S(2)}, u32[]{:S(2)}) %all-to-all-start) | async-done | bytes 3872 | tf_op jit(solution)/shard_map/all_to_all | solution.py:113
  64.8 0.1 fusion.42
  64.9 1.1 %bitcast_select_fusion.1 = f32[1,12]{1,0:T(1,128)} fusion(f32[12]{0:T(128)S(1)} %get-tuple-element.17, s32[]{:T(128)} %fusion.32), kind=kLoop, calls=%fused_computation.107 | loop fusion | flops 24 | bytes 100 | tf_op jit(solution)/shard_map/mul | solution.py:129
  66.0 1.1 %fusion.38 = (f32[1,12]{1,0:T(1,128)}, f32[1,12]{1,0:T(1,128)}, f32[1,12]{1,0:T(1,128)}) fusion(f32[12]{0:T(128)S(1)} %reduce_max.31, f32[12]{0:T(128)S(1)} %get-tuple-element.12, f32[12]{0:T(128)S(1)} %get-tuple-element.13, s32[]{:T(128)} %fusion.32, f32[12]{0:T(128)S(1)} %get-tuple-element.16), kind=kLoop, calls=%fused_computation.109 | loop fusion | flops 108 | bytes 340 | tf_op jit(solution)/shard_map/mul | solution.py:128
  (25 shorter events, 0.4 us)
Async XLA Ops:
  0.6 15.1 %copy-start.1 = (s32[4,8]{1,0:T(4,128)S(1)}, s32[4,8]{1,0:T(4,128)}, u32[]{:S(2)}) copy-start(s32[4,8]{1,0:T(4,128)} %param.9) | copy-start | bytes 388
  10.7 22.1 %collective-permute-start.3 = (bf16[24,4224]{1,0:T(8,128)(2,1)S(1)}, bf16[24,4224]{1,0:T(8,128)(2,1)S(1)}, u32[]{:S(2)}, u32[]{:S(2)}) collective-permute-start(bf16[24,4224]{1,0:T(8,128)(2,1)S(1)} %reshape.341), channel_id=1, source_target_pairs={{0,24},{8,0},{16,8},{24,16},{1,25},{9,1},{17,9},{25,17},{2,26},{10... | collective-permute-start | bytes 608264 | tf_op jit(solution)/shard_map/ppermute | solution.py:72
  14.6 18.3 %collective-permute-start.2 = (bf16[24,4224]{1,0:T(8,128)(2,1)S(1)}, bf16[24,4224]{1,0:T(8,128)(2,1)S(1)}, u32[]{:S(2)}, u32[]{:S(2)}) collective-permute-start(bf16[24,4224]{1,0:T(8,128)(2,1)S(1)} %reshape.341), channel_id=1, source_target_pairs={{0,16},{8,24},{16,0},{24,8},{1,17},{9,25},{17,1},{25,9},{2,18},{10... | collective-permute-start | bytes 608264 | tf_op jit(solution)/shard_map/ppermute | solution.py:72
  14.6 18.3 %collective-permute-start.1 = (bf16[24,4224]{1,0:T(8,128)(2,1)S(1)}, bf16[24,4224]{1,0:T(8,128)(2,1)S(1)}, u32[]{:S(2)}, u32[]{:S(2)}) collective-permute-start(bf16[24,4224]{1,0:T(8,128)(2,1)S(1)} %reshape.341), channel_id=1, source_target_pairs={{0,8},{8,16},{16,24},{24,0},{1,9},{9,17},{17,25},{25,1},{2,10},{10... | collective-permute-start | bytes 608264 | tf_op jit(solution)/shard_map/ppermute | solution.py:72
  15.7 3.2 %collective-permute-start = (bf16[24,4224]{1,0:T(8,128)(2,1)S(1)}, bf16[24,4224]{1,0:T(8,128)(2,1)S(1)}, u32[]{:S(2)}, u32[]{:S(2)}) collective-permute-start(bf16[24,4224]{1,0:T(8,128)(2,1)S(1)} %reshape.341), channel_id=1, source_target_pairs={{0,1},{1,0},{2,3},{3,2},{4,5},{5,4},{6,7},{7,6},{8,9},{9,8},{10,11... | collective-permute-start | bytes 608264 | tf_op jit(solution)/shard_map/ppermute | solution.py:75
  33.0 2.2 %collective-permute-start.4 = (bf16[72,4224]{1,0:T(8,128)(2,1)S(1)}, bf16[72,4224]{1,0:T(8,128)(2,1)S(1)}, u32[]{:S(2)}, u32[]{:S(2)}) collective-permute-start(bf16[72,4224]{1,0:T(8,128)(2,1)S(1)} %pad_maximum_fusion), channel_id=1, source_target_pairs={{0,1},{1,0},{2,3},{3,2},{4,5},{5,4},{6,7},{7,6},{8,9},{9,8},{10,11... | collective-permute-start | bytes 1824776 | tf_op jit(solution)/shard_map/ppermute | solution.py:78
  35.3 1.0 %copy-start = (bf16[144,4224]{1,0:T(8,128)(2,1)}, bf16[144,4224]{1,0:T(8,128)(2,1)S(1)}, u32[]{:S(2)}) copy-start(bf16[144,4224]{1,0:T(8,128)(2,1)S(1)} %constant_dynamic-update-slice_fusion.2) | copy-start | bytes 3649540
  50.1 7.8 %copy-start.2 = (s32[1,8]{1,0:T(1,128)S(1)}, s32[1,8]{1,0:T(1,128)}, u32[]{:S(2)}) copy-start(s32[1,8]{1,0:T(1,128)} %param.8) | copy-start | bytes 100
  52.7 12.1 %all-to-all-start = ((f32[16,5,12]{2,1,0:T(8,128)}), f32[16,5,12]{2,1,0:T(8,128)S(1)}, u32[]{:S(2)}, u32[]{:S(2)}) async-start(f32[16,5,12]{2,1,0:T(8,128)} %copy.20), calls=%async_computation | async-start | bytes 131072 | tf_op jit(solution)/shard_map/all_to_all | solution.py:113

commit v10 on v6

--- a/solution.py
+++ b/solution.py
@@ -60,8 +60,7 @@
     packed = jnp.concatenate([normed, coded], axis=1)
     packed = lax.all_gather(packed, "vocab_lo", axis=0, tiled=True)
     packed = lax.all_gather(packed, "vocab_hi", axis=0, tiled=True)
-    partner = lax.ppermute(packed, "grp_lo", [(0, 1), (1, 0)])
-    pair_rows = jnp.where(core == 0, jnp.concatenate([packed, partner]), jnp.concatenate([partner, packed]))
+    pair_rows = lax.all_gather(packed, "grp_lo", axis=0, tiled=True)
     pair_normed = pair_rows[:, :features]
     pair_ids = jnp.sum(pair_rows[:, features : features + digits].astype(jnp.int32) * place[None, :], axis=1)
     span = width // 2

time: 66.5 us -> 86.8 us (1.31)
  between operations: 0.78 us -> 14.2 us
  waiting for transfers between devices: 5.58 us -> 13.2 us
  local copies, waits for them, and re-layouts: 4.44 us -> 1.9 us
  starting transfers between devices: 4.04 us -> 5.91 us
    all_gather x0 -> x1, waiting for transfers between devices: none -> 7.63 us  [shards(): pair_rows = lax.all_gather(packed, 'grp_lo', axis=0, tiled=True)]
    all_to_all x1, starting transfers between devices: 4.04 us -> 5.88 us  [shards(): received = lax.all_to_all(payload, VOCAB + ('grp_lo',), 0, 0, tiled=True)]
    unnamed x5, local copies, waits for them, and re-layouts: 1.24 us -> 0.06 us
  transfers between devices with their start and end apart: 2 -> 2, of which waited for: 1 -> 2; matrix products, arithmetic and copies ran while one was open for 8% -> 4% of each run, Pallas kernels for 0% -> 0%
where the time goes in v10:
time: 86.8 us; the launch traced here: 86.5 us
  blocking collectives  27.7 us (32%)
  matrix products  14.7 us (17%)
  between operations  14.2 us (16%)
  waiting for transfers between devices  13.2 us (15%)
  other arithmetic  8.83 us (10%)
  starting transfers between devices  5.91 us (7%)
  local copies, waits for them, and re-layouts  1.9 us (2%)
    all_gather x1, blocking collectives, shards(): packed = lax.all_gather(packed, 'vocab_hi', axis=0, tiled=True)  20.5 us
    dot_general x1, matrix products, partial_stats(): logits = jnp.dot(normed, columns, preferred_element_type=jnp.float32)  14.5 us
    all_gather x1, waiting for transfers between devices, shards(): pair_rows = lax.all_gather(packed, 'grp_lo', axis=0, tiled=True)  7.63 us
    all_gather x1, blocking collectives, shards(): packed = lax.all_gather(packed, 'vocab_lo', axis=0, tiled=True)  7.21 us
    all_to_all x1, starting transfers between devices, shards(): received = lax.all_to_all(payload, VOCAB + ('grp_lo',), 0, 0, tiled=True)  5.88 us
    all_to_all x1, waiting for transfers between devices, shards(): received = lax.all_to_all(payload, VOCAB + ('grp_lo',), 0, 0, tiled=True)  5.58 us
  transfers between devices with their start and end apart: 2, of which 2 were waited for; matrix products, arithmetic and copies ran while one was open for 4% of the time, Pallas kernels for 0%

profile of v10, /device:TPU:0, one launch (start us, length us, event | category | flops | bytes accessed | tf_op | source)
XLA Modules:
  0.0 86.5 jit_solution(3649383240217678616)
XLA Ops:
  7.2 0.0 copy-start
  7.2 0.0 all-gather.3.cloned.1.call-start
  7.2 1.1 %fusion.5 = f32[12]{0:T(128)S(1)} fusion(bf16[1,12,4096]{2,1,0:T(8,128)(2,1)} %param.6), kind=kLoop, calls=%fused_computation.13 | loop fusion | flops 147444 | bytes 98352 | tf_op jit(solution)/shard_map/reduce_sum | solution.py:23
  8.3 1.0 %fusion.7 = bf16[12,4096]{1,0:T(8,128)(2,1)S(1)} fusion(bf16[1,12,4096]{2,1,0:T(8,128)(2,1)} %param.6, f32[4096]{0:T(1024)} %param.10, f32[12]{0:T(128)S(1)} %get-tuple-element.19), kind=kLoop, calls=%fused_computation.15 | loop fusion | flops 196608 | bytes 213040 | tf_op jit(solution)/shard_map/convert_element_type | solution.py:24
  9.3 0.7 and_convert_fusion
  10.1 7.2 %all-gather = bf16[2,12,4224]{2,1,0:T(8,128)(2,1)S(1)} all-gather(bf16[1,12,4224]{2,1,0:T(8,128)(2,1)S(1)} %fusion.9), channel_id=1, replica_groups=mesh['vocab_hi'=4,'vocab_lo'=2,'grp_hi'=2,'grp_lo'=2] {'vocab_lo'}, dimensions={0}, use_global_device_ids=true | all-gather | bytes 304128 | tf_op jit(solution)/shard_map/all_gather | solution.py:61
  17.3 0.1 reshape.213
  17.3 20.5 %all_gather.10 = bf16[96,4224]{1,0:T(8,128)(2,1)} all-gather(bf16[24,4224]{1,0:T(8,128)(2,1)S(1)} %reshape.213), channel_id=1, replica_groups=mesh['vocab_hi'=4,'vocab_lo'=2,'grp_hi'=2,'grp_lo'=2] {'vocab_hi'}, dimensions={0}, use_global_device_ids=true | all-gather | bytes 1013760 | tf_op jit(solution)/shard_map/all_gather | solution.py:62
  37.9 0.0 all-gather.3.cloned.1.call-update
  37.9 0.1 and.86
  38.0 0.0 copy-done
  38.0 0.6 dynamic_slice.16
  38.6 0.6 iota_compare_fusion.4
  39.3 0.1 and.83
  39.3 0.1 and.84
  39.4 0.6 fusion.26
  40.1 0.1 broadcast_select_fusion
  40.2 7.6 %all-gather.3.cloned.1.call-done = bf16[192,4224]{1,0:T(8,128)(2,1)} async-done(((bf16[96,4224]{1,0:T(8,128)(2,1)}), bf16[192,4224]{1,0:T(8,128)(2,1)}) %all-gather.3.cloned.1.call-update) | async-done | bytes 1622032 | tf_op jit(solution)/shard_map/all_gather | solution.py:63
  47.8 14.5 %fusion.29 = (f32[192]{0:T(256)S(1)}, f32[192,4096]{1,0:T(8,128)S(1)}) fusion(bf16[4096,8192]{1,0:T(8,128)(2,1)} %param.11, s32[]{:T(128)S(6)} %select_n.97, bf16[192,4224]{1,0:T(8,128)(2,1)} %all-gather.3.cloned.1.call-done), kind=kOutput, calls=%fused_computation.71 | convolution fusion | flops 6443237376 | bytes 38273796 | tf_op jit(solution)/shard_map/dot_general | solution.py:29
  62.4 0.0 copy-start.1
  62.4 0.1 stack.15
  62.5 0.9 %multiply_reduce_fusion.1 = s32[192]{0:T(256)S(1)} fusion(bf16[192,4224]{1,0:T(8,128)(2,1)} %all-gather.3.cloned.1.call-done, s32[2]{0:T(128)S(1)} %compare_select_fusion.5), kind=kLoop, calls=%fused_computation.18 | loop fusion | flops 960 | bytes 1544 | tf_op jit(solution)/shard_map/reduce_sum | solution.py:65
  63.4 1.1 %fusion.2 = (f32[192]{0:T(256)S(1)}, f32[192]{0:T(256)S(1)}, f32[192]{0:T(256)S(1)}) fusion(f32[192,4096]{1,0:T(8,128)S(1)} %get-tuple-element.22, f32[192]{0:T(256)S(1)} %get-tuple-element.21, s32[192]{0:T(256)S(1)} %broadcast_subtract_fusion), kind=kLoop, calls=%fused_computation.6 | loop fusion | flops 5504448 | bytes 3149568 | tf_op jit(solution)/shard_map/reduce_sum | solution.py:36
  64.5 0.1 stack.16
  64.6 0.1 stack.17
  64.7 0.1 stack.18
  64.8 0.1 convolution_bitcast_fusion
  65.0 0.6 copy.14
  65.6 5.9 %all-to-all-start = ((f32[16,5,12]{2,1,0:T(8,128)}), f32[16,5,12]{2,1,0:T(8,128)S(1)}, u32[]{:S(2)}, u32[]{:S(2)}) async-start(f32[16,5,12]{2,1,0:T(8,128)} %copy.14), calls=%async_computation | async-start | bytes 131072 | tf_op jit(solution)/shard_map/all_to_all | solution.py:80
  71.5 0.0 copy-done.1
  71.5 1.3 %fusion.23 = s32[]{:T(128)} fusion(s32[1,8]{1,0:T(1,128)S(1)} %copy-done.1, s32[]{:T(128)} %fusion.26), kind=kLoop, calls=%fused_computation.52 | loop fusion | flops 23 | bytes 40 | tf_op jit(solution)/shard_map/reduce_sum | solution.py:91
  72.8 5.6 %all-to-all-done = f32[16,5,12]{2,1,0:T(8,128)S(1)} async-done(((f32[16,5,12]{2,1,0:T(8,128)}), f32[16,5,12]{2,1,0:T(8,128)S(1)}, u32[]{:S(2)}, u32[]{:S(2)}) %all-to-all-start) | async-done | bytes 3872 | tf_op jit(solution)/shard_map/all_to_all | solution.py:80
  78.4 0.1 fusion.28
  78.5 1.1 %fusion.24 = (f32[1,12]{1,0:T(1,128)}, f32[1,12]{1,0:T(1,128)}, f32[1,12]{1,0:T(1,128)}, f32[1,12]{1,0:T(1,128)}) fusion(f32[12]{0:T(128)S(1)} %reduce_max.21, f32[12]{0:T(128)S(1)} %get-tuple-element.9, f32[12]{0:T(128)S(1)} %get-tuple-element.10, s32[]{:T(128)} %fusion.23, f32[12]{0:T(128)S(1)} %get-tuple-element.13, f32[12]{0:T(128)S(1)} %get-tuple-element.14), kind=kLoop, calls=%fused_computation.55 | loop fusion | flops 120 | bytes 436 | tf_op jit(solution)/shard_map/mul | solution.py:95
  (13 shorter events, 0.2 us)
Async XLA Ops:
  7.2 30.9 %copy-start = (s32[4,8]{1,0:T(4,128)S(1)}, s32[4,8]{1,0:T(4,128)}, u32[]{:S(2)}) copy-start(s32[4,8]{1,0:T(4,128)} %param.9) | copy-start | bytes 388
  7.2 40.6 %all-gather.3.cloned.1.call-start = ((), (), s32[]{:S(2)}) async-start(), calls=%async_computation.1 | async-start | bytes 2433024 | tf_op jit(solution)/shard_map/all_gather | solution.py:63
  62.4 9.2 %copy-start.1 = (s32[1,8]{1,0:T(1,128)S(1)}, s32[1,8]{1,0:T(1,128)}, u32[]{:S(2)}) copy-start(s32[1,8]{1,0:T(1,128)} %param.8) | copy-start | bytes 100
  65.6 12.8 %all-to-all-start = ((f32[16,5,12]{2,1,0:T(8,128)}), f32[16,5,12]{2,1,0:T(8,128)S(1)}, u32[]{:S(2)}, u32[]{:S(2)}) async-start(f32[16,5,12]{2,1,0:T(8,128)} %copy.14), calls=%async_computation | async-start | bytes 131072 | tf_op jit(solution)/shard_map/all_to_all | solution.py:80
Sparse Core Ops, SparseCore 0:
  38.0 9.7 all-gather.2

commit v11 on v6

--- a/solution.py
+++ b/solution.py
@@ -58,7 +58,14 @@
     coded = ((target_ids[0][:, None] >> shifts[None, :]) & (RADIX - 1)).astype(jnp.bfloat16)
     coded = jnp.pad(coded, ((0, 0), (0, LANES - digits)))
     packed = jnp.concatenate([normed, coded], axis=1)
-    packed = lax.all_gather(packed, "vocab_lo", axis=0, tiled=True)
+    low_index = lax.axis_index("vocab_lo")
+    if lax.axis_size("vocab_lo") == 2:
+        packed = jnp.concatenate([packed, lax.ppermute(packed, "vocab_lo", [(0, 1), (1, 0)])])
+        positions = jnp.arange(vocab_size, dtype=jnp.int32)
+        block_of = (positions // 2) * 2 + ((positions % 2) ^ low_index)
+    else:
+        packed = lax.all_gather(packed, "vocab_lo", axis=0, tiled=True)
+        block_of = block_ids
     packed = lax.all_gather(packed, "vocab_hi", axis=0, tiled=True)
     partner = lax.ppermute(packed, "grp_lo", [(0, 1), (1, 0)])
     pair_rows = jnp.where(core == 0, jnp.concatenate([packed, partner]), jnp.concatenate([partner, packed]))
@@ -70,6 +77,7 @@
     local_max, sums, expected, target = partial_stats(pair_normed, columns, pair_ids, offset)
     terms = jnp.stack([local_max, sums, expected, target]).reshape(4, 2, vocab_size, count)
     pair_order = lax.dynamic_slice_in_dim(order, pair_base, 2, 0)
+    pair_order = jnp.take(pair_order, block_of, axis=1)
     route = (pair_order[:, None, :] == block_ids[None, :, None]).astype(jnp.float32)
     routed = jnp.einsum("cjs,kcsr->jckr", route, terms, precision=lax.Precision.HIGHEST)
     group_ids = jnp.arange(2, dtype=jnp.int32)

time: 66.5 us -> 66 us (level)
  blocking collectives: 27.7 us -> 20.4 us
  starting transfers between devices: 4.04 us -> 7.06 us
  waiting for transfers between devices: 5.58 us -> 8.44 us
  local copies, waits for them, and re-layouts: 4.44 us -> 5.13 us
    all_gather x1 -> x0, blocking collectives: 7.21 us -> none  [shards(): packed = lax.all_gather(packed, 'vocab_lo', axis=0, tiled=True)]
    ppermute x0 -> x1, starting transfers between devices: none -> 3.03 us  [shards(): lax.ppermute(packed, 'vocab_lo', [(0, 1), (1, 0)])]
    ppermute x0 -> x1, waiting for transfers between devices: none -> 2.86 us  [shards(): lax.ppermute(packed, 'vocab_lo', [(0, 1), (1, 0)])]
  transfers between devices with their start and end apart: 2 -> 3, of which waited for: 1 -> 2; matrix products, arithmetic and copies ran while one was open for 8% -> 10% of each run, Pallas kernels for 0% -> 0%
where the time goes in v11:
time: 66 us; the launch traced here: 65.7 us
  blocking collectives  20.4 us (31%)
  matrix products  14.7 us (22%)
  other arithmetic  9.15 us (14%)
  waiting for transfers between devices  8.44 us (13%)
  starting transfers between devices  7.06 us (11%)
  local copies, waits for them, and re-layouts  5.13 us (8%)
  between operations  0.81 us (1%)
    all_gather x1, blocking collectives, shards(): packed = lax.all_gather(packed, 'vocab_hi', axis=0, tiled=True)  20.4 us
    dot_general x1, matrix products, partial_stats(): logits = jnp.dot(normed, columns, preferred_element_type=jnp.float32)  14.6 us
    all_to_all x1, waiting for transfers between devices, shards(): received = lax.all_to_all(payload, VOCAB + ('grp_lo',), 0, 0, tiled=True)  5.58 us
    all_to_all x1, starting transfers between devices, shards(): received = lax.all_to_all(payload, VOCAB + ('grp_lo',), 0, 0, tiled=True)  4.03 us
    ppermute x1, starting transfers between devices, shards(): lax.ppermute(packed, 'vocab_lo', [(0, 1), (1, 0)])  3.03 us
    ppermute x1, waiting for transfers between devices, shards(): lax.ppermute(packed, 'vocab_lo', [(0, 1), (1, 0)])  2.86 us
    reduce_sum x1, other arithmetic, shards(): source_block = jnp.sum(jnp.where(own_order == vocab_index, block_ids, 0))  1.33 us
  transfers between devices with their start and end apart: 3, of which 2 were waited for; matrix products, arithmetic and copies ran while one was open for 10% of the time, Pallas kernels for 0%

profile of v11, /device:TPU:0, one launch (start us, length us, event | category | flops | bytes accessed | tf_op | source)
XLA Modules:
  0.0 65.7 jit_solution(3738324747463158690)
XLA Ops:
  0.6 1.1 %fusion.4 = f32[12]{0:T(128)S(1)} fusion(bf16[1,12,4096]{2,1,0:T(8,128)(2,1)} %param.6), kind=kLoop, calls=%fused_computation.13 | loop fusion | flops 147444 | bytes 98352 | tf_op jit(solution)/shard_map/reduce_sum | solution.py:23
  1.7 1.0 %fusion.6 = bf16[12,4096]{1,0:T(8,128)(2,1)S(1)} fusion(bf16[1,12,4096]{2,1,0:T(8,128)(2,1)} %param.6, f32[4096]{0:T(1024)} %param.10, f32[12]{0:T(128)S(1)} %get-tuple-element.19), kind=kLoop, calls=%fused_computation.15 | loop fusion | flops 196608 | bytes 213040 | tf_op jit(solution)/shard_map/convert_element_type | solution.py:24
  2.7 0.7 %and_convert_fusion = bf16[12,2]{1,0:T(8,128)(2,1)S(1)} fusion(s32[2]{0:T(128)S(1)} %iota_multiply_fusion, s32[12]{0:T(128)} %bitcast.59), kind=kLoop, calls=%fused_computation.33 | loop fusion | flops 72 | bytes 104 | tf_op jit(solution)/shard_map/convert_element_type | solution.py:58
  3.5 3.0 %collective-permute-start = (bf16[12,4224]{1,0:T(8,128)(2,1)S(1)}, bf16[12,4224]{1,0:T(8,128)(2,1)S(1)}, u32[]{:S(2)}, u32[]{:S(2)}) collective-permute-start(bf16[12,4224]{1,0:T(8,128)(2,1)S(1)} %pad_maximum_fusion.1), channel_id=1, source_target_pairs={{0,4},{4,0},{1,5},{5,1},{2,6},{6,2},{3,7},{7,3},{8,12},{12,8},{9,1... | collective-permute-start | bytes 304136 | tf_op jit(solution)/shard_map/ppermute | solution.py:63
  6.5 0.7 %constant_dynamic-slice_fusion = s32[2,8]{1,0:T(2,128)S(1)} fusion(s32[4,8]{1,0:T(4,128)} %param.9, s32[]{:T(128)S(6)} %select_n.174), kind=kLoop, calls=%fused_computation.62 | loop fusion | bytes 132 | tf_op jit(solution)/shard_map/dynamic_slice | solution.py:79
  7.2 2.9 %collective-permute-done = bf16[12,4224]{1,0:T(8,128)(2,1)S(1)} collective-permute-done((bf16[12,4224]{1,0:T(8,128)(2,1)S(1)}, bf16[12,4224]{1,0:T(8,128)(2,1)S(1)}, u32[]{:S(2)}, u32[]{:S(2)}) %collective-permute-start) | collective-permute-done | bytes 101408 | tf_op jit(solution)/shard_map/ppermute | solution.py:63
  10.1 0.1 pad_maximum_fusion
  10.2 20.4 %all_gather.3 = bf16[96,4224]{1,0:T(8,128)(2,1)S(1)} all-gather(bf16[24,4224]{1,0:T(8,128)(2,1)S(1)} %pad_maximum_fusion), channel_id=1, replica_groups=mesh['vocab_hi'=4,'vocab_lo'=2,'grp_hi'=2,'grp_lo'=2] {'vocab_hi'}, dimensions={0}, use_global_device_ids=true | all-gather | bytes 1013760 | tf_op jit(solution)/shard_map/all_gather | solution.py:69
  30.6 0.0 collective-permute-start.1
  30.6 0.1 copy.24
  30.7 0.6 gather_fusion
  31.3 0.1 select_bitcast_fusion
  31.3 0.1 copy.18
  31.4 0.1 and.142
  31.5 1.3 %dynamic_slice.16 = s32[1,1]{1,0:T(1,128)} dynamic-slice(s32[4,8]{1,0:T(4,128)} %param.9, s32[]{:T(128)S(6)} %select_n.179, s32[]{:T(128)S(6)} %select_n.181), dynamic_slice_sizes={1,1} | dynamic-slice | bytes 12 | tf_op jit(solution)/shard_map/dynamic_slice | solution.py:84
  32.8 0.6 iota_compare_fusion.3
  33.4 0.1 and.139
  33.5 0.1 and.140
  33.6 1.3 %fusion.30 = s32[]{:T(128)} fusion(s32[4,8]{1,0:T(4,128)} %param.9, s32[]{:T(128)S(6)} %select_n.157, s32[]{:T(128)S(6)} %add.105), kind=kLoop, calls=%fused_computation.89 | loop fusion | flops 23 | bytes 44 | tf_op jit(solution)/shard_map/reduce_sum | solution.py:99
  35.0 0.1 broadcast_select_fusion
  35.0 0.0 collective-permute-done.1
  35.0 0.3 maximum_select_fusion
  35.3 0.0 copy-start
  35.3 1.2 %copy-done = bf16[192,4224]{1,0:T(8,128)(2,1)} copy-done((bf16[192,4224]{1,0:T(8,128)(2,1)}, bf16[192,4224]{1,0:T(8,128)(2,1)S(1)}, u32[]{:S(2)}) %copy-start) | copy-done | bytes 1622040
  36.5 0.1 multiply_reduce_fusion.1
  36.6 14.6 %fusion.33 = (f32[192]{0:T(256)S(1)}, f32[192,4096]{1,0:T(8,128)S(1)}) fusion(bf16[4096,8192]{1,0:T(8,128)(2,1)} %param.11, s32[]{:T(128)S(6)} %select_n.163, bf16[192,4224]{1,0:T(8,128)(2,1)} %copy-done), kind=kOutput, calls=%fused_computation.93 | convolution fusion | flops 6443237376 | bytes 38273796 | tf_op jit(solution)/shard_map/dot_general | solution.py:29
  51.2 0.0 copy-start.1
  51.2 0.1 stack.15
  51.3 1.1 %fusion.2 = (f32[192]{0:T(256)S(1)}, f32[192]{0:T(256)S(1)}, f32[192]{0:T(256)S(1)}) fusion(f32[192,4096]{1,0:T(8,128)S(1)} %get-tuple-element.22, f32[192]{0:T(256)S(1)} %get-tuple-element.21, s32[192]{0:T(256)S(1)} %broadcast_subtract_fusion), kind=kLoop, calls=%fused_computation.7 | loop fusion | flops 5504448 | bytes 3149568 | tf_op jit(solution)/shard_map/reduce_sum | solution.py:36
  52.4 0.1 stack.16
  52.5 0.1 stack.17
  52.6 0.1 stack.18
  52.7 0.1 convolution_bitcast_fusion
  52.9 0.6 copy.20
  53.5 4.0 %all-to-all-start = ((f32[16,5,12]{2,1,0:T(8,128)}), f32[16,5,12]{2,1,0:T(8,128)S(1)}, u32[]{:S(2)}, u32[]{:S(2)}) async-start(f32[16,5,12]{2,1,0:T(8,128)} %copy.20), calls=%async_computation | async-start | bytes 131072 | tf_op jit(solution)/shard_map/all_to_all | solution.py:89
  57.6 0.0 copy-done.1
  57.6 1.3 %fusion.27 = s32[]{:T(128)} fusion(s32[1,8]{1,0:T(1,128)S(1)} %copy-done.1, s32[]{:T(128)} %fusion.30), kind=kLoop, calls=%fused_computation.74 | loop fusion | flops 23 | bytes 40 | tf_op jit(solution)/shard_map/reduce_sum | solution.py:100
  58.9 5.6 %all-to-all-done = f32[16,5,12]{2,1,0:T(8,128)S(1)} async-done(((f32[16,5,12]{2,1,0:T(8,128)}), f32[16,5,12]{2,1,0:T(8,128)S(1)}, u32[]{:S(2)}, u32[]{:S(2)}) %all-to-all-start) | async-done | bytes 3872 | tf_op jit(solution)/shard_map/all_to_all | solution.py:89
  64.5 0.1 fusion.32
  64.6 1.1 %fusion.28 = (f32[1,12]{1,0:T(1,128)}, f32[1,12]{1,0:T(1,128)}, f32[1,12]{1,0:T(1,128)}, f32[1,12]{1,0:T(1,128)}) fusion(f32[12]{0:T(128)S(1)} %reduce_max.21, f32[12]{0:T(128)S(1)} %get-tuple-element.9, f32[12]{0:T(128)S(1)} %get-tuple-element.10, s32[]{:T(128)} %fusion.27, f32[12]{0:T(128)S(1)} %get-tuple-element.13, f32[12]{0:T(128)S(1)} %get-tuple-element.14), kind=kLoop, calls=%fused_computation.77 | loop fusion | flops 120 | bytes 436 | tf_op jit(solution)/shard_map/mul | solution.py:104
  (16 shorter events, 0.2 us)
Async XLA Ops:
  3.5 6.6 %collective-permute-start = (bf16[12,4224]{1,0:T(8,128)(2,1)S(1)}, bf16[12,4224]{1,0:T(8,128)(2,1)S(1)}, u32[]{:S(2)}, u32[]{:S(2)}) collective-permute-start(bf16[12,4224]{1,0:T(8,128)(2,1)S(1)} %pad_maximum_fusion.1), channel_id=1, source_target_pairs={{0,4},{4,0},{1,5},{5,1},{2,6},{6,2},{3,7},{7,3},{8,12},{12,8},{9,1... | collective-permute-start | bytes 304136 | tf_op jit(solution)/shard_map/ppermute | solution.py:63
  30.6 4.4 %collective-permute-start.1 = (bf16[96,4224]{1,0:T(8,128)(2,1)S(1)}, bf16[96,4224]{1,0:T(8,128)(2,1)S(1)}, u32[]{:S(2)}, u32[]{:S(2)}) collective-permute-start(bf16[96,4224]{1,0:T(8,128)(2,1)S(1)} %all_gather.3), channel_id=1, source_target_pairs={{0,1},{1,0},{2,3},{3,2},{4,5},{5,4},{6,7},{7,6},{8,9},{9,8},{10,11... | collective-permute-start | bytes 2433032 | tf_op jit(solution)/shard_map/ppermute | solution.py:70
  35.3 1.2 %copy-start = (bf16[192,4224]{1,0:T(8,128)(2,1)}, bf16[192,4224]{1,0:T(8,128)(2,1)S(1)}, u32[]{:S(2)}) copy-start(bf16[192,4224]{1,0:T(8,128)(2,1)S(1)} %maximum_select_fusion) | copy-start | bytes 4866052
  51.2 6.4 %copy-start.1 = (s32[1,8]{1,0:T(1,128)S(1)}, s32[1,8]{1,0:T(1,128)}, u32[]{:S(2)}) copy-start(s32[1,8]{1,0:T(1,128)} %param.8) | copy-start | bytes 100
  53.5 10.9 %all-to-all-start = ((f32[16,5,12]{2,1,0:T(8,128)}), f32[16,5,12]{2,1,0:T(8,128)S(1)}, u32[]{:S(2)}, u32[]{:S(2)}) async-start(f32[16,5,12]{2,1,0:T(8,128)} %copy.20), calls=%async_computation | async-start | bytes 131072 | tf_op jit(solution)/shard_map/all_to_all | solution.py:89

commit v12 on v8

--- a/solution.py
+++ b/solution.py
@@ -81,20 +81,29 @@
     width = head.shape[1]
     features = states.shape[2]
     digits = digit_count(width * vocab_size)
-    place = RADIX ** jnp.arange(digits, dtype=jnp.int32)
     packed = pack_rows(states[0], gain, target_ids, digits)
-    packed = lax.all_gather(packed, "vocab_lo", axis=0, tiled=True)
+    low_index = lax.axis_index("vocab_lo")
+    if lax.axis_size("vocab_lo") == 2:
+        packed = jnp.concatenate([packed, lax.ppermute(packed, "vocab_lo", [(0, 1), (1, 0)])])
+        positions = jnp.arange(vocab_size, dtype=jnp.int32)
+        block_of = (positions // 2) * 2 + ((positions % 2) ^ low_index)
+    else:
+        packed = lax.all_gather(packed, "vocab_lo", axis=0, tiled=True)
+        block_of = block_ids
     packed = lax.all_gather(packed, "vocab_hi", axis=0, tiled=True)
     partner = lax.ppermute(packed, "grp_lo", [(0, 1), (1, 0)])
     pair_rows = jnp.where(core == 0, jnp.concatenate([packed, partner]), jnp.concatenate([partner, packed]))
     pair_normed = pair_rows[:, :features]
-    pair_ids = jnp.sum(pair_rows[:, features : features + digits].astype(jnp.int32) * place[None, :], axis=1)
+    pair_ids = pair_rows[:, features].astype(jnp.int32)
+    for k in range(1, digits):
+        pair_ids = pair_ids + (pair_rows[:, features + k].astype(jnp.int32) << (RADIX_BITS * k))
     span = width // 2
     columns = lax.dynamic_slice_in_dim(head, core * span, span, 1)
     offset = vocab_index * width + core * span
     local_max, sums, expected, target = partial_stats(pair_normed, columns, pair_ids, offset)
     terms = jnp.stack([local_max, sums, expected, target]).reshape(4, 2, vocab_size, count)
     pair_order = lax.dynamic_slice_in_dim(order, pair_base, 2, 0)
+    pair_order = jnp.take(pair_order, block_of, axis=1)
     route = (pair_order[:, None, :] == block_ids[None, :, None]).astype(jnp.float32)
     routed = jnp.einsum("cjs,kcsr->jckr", route, terms, precision=lax.Precision.HIGHEST)
     group_ids = jnp.arange(2, dtype=jnp.int32)

time: 67.5 us -> 66.4 us (0.984)
  blocking collectives: 27.9 us -> 20.4 us
  starting transfers between devices: 4.03 us -> 7.02 us
  waiting for transfers between devices: 5.58 us -> 8 us
  local copies, waits for them, and re-layouts: 3.26 us -> 5.12 us
  other arithmetic: 9.23 us -> 8.36 us
    all_gather x1 -> x0, blocking collectives: 7.47 us -> none  [shards(): packed = lax.all_gather(packed, 'vocab_lo', axis=0, tiled=True)]
    ppermute x0 -> x1, starting transfers between devices: none -> 2.97 us  [shards(): lax.ppermute(packed, 'vocab_lo', [(0, 1), (1, 0)])]
    ppermute x0 -> x1, waiting for transfers between devices: none -> 2.42 us  [shards(): lax.ppermute(packed, 'vocab_lo', [(0, 1), (1, 0)])]
    unnamed x3 -> x5, local copies, waits for them, and re-layouts: 0.06 us -> 1.27 us
    select_n x1, other arithmetic: 1.49 us -> 0.29 us  [shards(): jnp.where(core == 0, jnp.concatenate([packed, partner]), jnp.concatenate(...]
    concatenate x0 -> x1, other arithmetic: none -> 0.96 us  [shards(): jnp.concatenate([packed, lax.ppermute(packed, 'vocab_lo', [(0, 1), (1, 0)...]
    reduce_sum x1 -> x0, other arithmetic: 0.91 us -> none  [shards(): jnp.sum(pair_rows[:, features:features + digits].astype(jnp.int32) * plac...]
  transfers between devices with their start and end apart: 2 -> 3, of which waited for: 1 -> 2; matrix products, arithmetic and copies ran while one was open for 10% -> 11% of each run, Pallas kernels for 0% -> 0%
where the time goes in v12:
time: 66.4 us; the launch traced here: 66.1 us
  blocking collectives  20.4 us (31%)
  matrix products  14.7 us (22%)
  other arithmetic  8.36 us (13%)
  waiting for transfers between devices  8 us (12%)
  starting transfers between devices  7.02 us (11%)
  local copies, waits for them, and re-layouts  5.12 us (8%)
  Pallas kernels  1.72 us (3%)
  between operations  0.77 us (1%)
    all_gather x1, blocking collectives, shards(): packed = lax.all_gather(packed, 'vocab_hi', axis=0, tiled=True)  20.4 us
    dot_general x1, matrix products, partial_stats(): logits = jnp.dot(normed, columns, preferred_element_type=jnp.float32)  14.6 us
    all_to_all x1, waiting for transfers between devices, shards(): received = lax.all_to_all(payload, VOCAB + ('grp_lo',), 0, 0, tiled=True)  5.58 us
    all_to_all x1, starting transfers between devices, shards(): received = lax.all_to_all(payload, VOCAB + ('grp_lo',), 0, 0, tiled=True)  4.05 us
    ppermute x1, starting transfers between devices, shards(): lax.ppermute(packed, 'vocab_lo', [(0, 1), (1, 0)])  2.97 us
    ppermute x1, waiting for transfers between devices, shards(): lax.ppermute(packed, 'vocab_lo', [(0, 1), (1, 0)])  2.42 us
    pallas_call x1, Pallas kernels, pack_rows(): pl.pallas_call(partial(pack_kernel, features=features, digits=digits), ou...  1.72 us
  transfers between devices with their start and end apart: 3, of which 2 were waited for; matrix products, arithmetic and copies ran while one was open for 11% of the time, Pallas kernels for 0%

profile of v12, /device:TPU:0, one launch (start us, length us, event | category | flops | bytes accessed | tf_op | source)
XLA Modules:
  0.0 66.1 jit_solution(13724769635592749575)
XLA Ops:
  0.6 1.7 %shard_map.93 = bf16[12,4224]{1,0:T(8,128)(2,1)} custom-call(bf16[12,4096]{1,0:T(8,128)(2,1)} %bitcast.52, f32[1,4096]{1,0:T(1,128)} %bitcast.58, s32[1,12]{1,0:T(1,128)} %ids_ref.1), custom_call_target="tpu_custom_call" | custom-call | tf_op jit(solution)/shard_map/pallas_call | solution.py:64
  2.3 3.0 %collective-permute-start = (bf16[12,4224]{1,0:T(8,128)(2,1)}, bf16[12,4224]{1,0:T(8,128)(2,1)S(1)}, u32[]{:S(2)}, u32[]{:S(2)}) collective-permute-start(bf16[12,4224]{1,0:T(8,128)(2,1)} %shard_map.93), channel_id=1, source_target_pairs={{0,4},{4,0},{1,5},{5,1},{2,6},{6,2},{3,7},{7,3},{8,12},{12,8},{9,1... | collective-permute-start | bytes 304136 | tf_op jit(solution)/shard_map/ppermute | solution.py:87
  5.3 0.7 %constant_dynamic-slice_fusion = s32[2,8]{1,0:T(2,128)S(1)} fusion(s32[4,8]{1,0:T(4,128)} %param.9, s32[]{:T(128)S(6)} %select_n.122), kind=kLoop, calls=%fused_computation.48 | loop fusion | bytes 132 | tf_op jit(solution)/shard_map/dynamic_slice | solution.py:105
  6.0 0.1 copy.30
  6.1 0.6 gather_fusion
  6.7 2.4 %collective-permute-done = bf16[12,4224]{1,0:T(8,128)(2,1)S(1)} collective-permute-done((bf16[12,4224]{1,0:T(8,128)(2,1)}, bf16[12,4224]{1,0:T(8,128)(2,1)S(1)}, u32[]{:S(2)}, u32[]{:S(2)}) %collective-permute-start) | collective-permute-done | bytes 101408 | tf_op jit(solution)/shard_map/ppermute | solution.py:87
  9.1 1.0 %pad_maximum_fusion = bf16[24,4224]{1,0:T(8,128)(2,1)S(1)} fusion(bf16[12,4224]{1,0:T(8,128)(2,1)S(1)} %collective-permute-done, bf16[12,4224]{1,0:T(8,128)(2,1)} %shard_map.93), kind=kLoop, calls=%fused_computation.12 | loop fusion | flops 405504 | bytes 405504 | tf_op jit(solution)/shard_map/concatenate | solution.py:87
  10.1 20.4 %all_gather.3 = bf16[96,4224]{1,0:T(8,128)(2,1)S(1)} all-gather(bf16[24,4224]{1,0:T(8,128)(2,1)S(1)} %pad_maximum_fusion), channel_id=1, replica_groups=mesh['vocab_hi'=4,'vocab_lo'=2,'grp_hi'=2,'grp_lo'=2] {'vocab_hi'}, dimensions={0}, use_global_device_ids=true | all-gather | bytes 1013760 | tf_op jit(solution)/shard_map/all_gather | solution.py:93
  30.5 0.0 collective-permute-start.1
  30.5 0.1 select_bitcast_fusion
  30.6 0.1 copy.24
  30.7 0.1 and.90
  30.8 1.3 %dynamic_slice.16 = s32[1,1]{1,0:T(1,128)} dynamic-slice(s32[4,8]{1,0:T(4,128)} %param.9, s32[]{:T(128)S(6)} %select_n.127, s32[]{:T(128)S(6)} %select_n.129), dynamic_slice_sizes={1,1} | dynamic-slice | bytes 12 | tf_op jit(solution)/shard_map/dynamic_slice | solution.py:110
  32.0 0.6 iota_compare_fusion.3
  32.7 0.1 and.87
  32.8 0.1 and.88
  32.9 1.3 %fusion.25 = s32[]{:T(128)} fusion(s32[4,8]{1,0:T(4,128)} %param.9, s32[]{:T(128)S(6)} %select_n.111, s32[]{:T(128)S(6)} %add.100), kind=kLoop, calls=%fused_computation.71 | loop fusion | flops 23 | bytes 44 | tf_op jit(solution)/shard_map/reduce_sum | solution.py:125
  34.2 1.0 %multiply_reduce_fusion.1 = f32[12]{0:T(128)S(1)} fusion(bf16[1,12,4096]{2,1,0:T(8,128)(2,1)} %param.6), kind=kLoop, calls=%fused_computation.11 | loop fusion | flops 147444 | bytes 98352 | tf_op jit(solution)/shard_map/reduce_sum | solution.py:80
  35.2 0.1 broadcast_select_fusion
  35.3 0.0 collective-permute-done.1
  35.3 0.3 maximum_select_fusion
  35.6 0.0 copy-start
  35.6 1.2 %copy-done = bf16[192,4224]{1,0:T(8,128)(2,1)} copy-done((bf16[192,4224]{1,0:T(8,128)(2,1)}, bf16[192,4224]{1,0:T(8,128)(2,1)S(1)}, u32[]{:S(2)}) %copy-start) | copy-done | bytes 1622040
  36.8 0.2 subtract_reduce_fusion
  37.0 14.6 %fusion.28 = (f32[192]{0:T(256)S(1)}, f32[192,4096]{1,0:T(8,128)S(1)}) fusion(bf16[4096,8192]{1,0:T(8,128)(2,1)} %param.11, s32[]{:T(128)S(6)} %select_n.117, bf16[192,4224]{1,0:T(8,128)(2,1)} %copy-done), kind=kOutput, calls=%fused_computation.74 | convolution fusion | flops 6443237376 | bytes 38273796 | tf_op jit(solution)/shard_map/dot_general | solution.py:32
  51.6 0.0 copy-start.1
  51.6 0.1 stack.15
  51.7 1.1 %fusion.2 = (f32[192]{0:T(256)S(1)}, f32[192]{0:T(256)S(1)}, f32[192]{0:T(256)S(1)}) fusion(f32[192,4096]{1,0:T(8,128)S(1)} %get-tuple-element.20, f32[192]{0:T(256)S(1)} %get-tuple-element.19, s32[192]{0:T(256)S(1)} %subtract_reduce_fusion), kind=kLoop, calls=%fused_computation.7 | loop fusion | flops 5504448 | bytes 3149568 | tf_op jit(solution)/shard_map/reduce_sum | solution.py:39
  52.8 0.1 stack.16
  52.9 0.1 stack.17
  53.0 0.1 stack.18
  53.1 0.1 convolution_bitcast_fusion
  53.3 0.6 copy.26
  53.9 4.0 %all-to-all-start = ((f32[16,5,12]{2,1,0:T(8,128)}), f32[16,5,12]{2,1,0:T(8,128)S(1)}, u32[]{:S(2)}, u32[]{:S(2)}) async-start(f32[16,5,12]{2,1,0:T(8,128)} %copy.26), calls=%async_computation | async-start | bytes 131072 | tf_op jit(solution)/shard_map/all_to_all | solution.py:115
  58.0 0.0 copy-done.1
  58.0 1.3 %fusion.22 = s32[]{:T(128)} fusion(s32[1,8]{1,0:T(1,128)S(1)} %copy-done.1, s32[]{:T(128)} %fusion.25), kind=kLoop, calls=%fused_computation.58 | loop fusion | flops 23 | bytes 40 | tf_op jit(solution)/shard_map/reduce_sum | solution.py:126
  59.3 5.6 %all-to-all-done = f32[16,5,12]{2,1,0:T(8,128)S(1)} async-done(((f32[16,5,12]{2,1,0:T(8,128)}), f32[16,5,12]{2,1,0:T(8,128)S(1)}, u32[]{:S(2)}, u32[]{:S(2)}) %all-to-all-start) | async-done | bytes 3872 | tf_op jit(solution)/shard_map/all_to_all | solution.py:115
  64.9 0.1 fusion.27
  65.0 1.1 %fusion.23 = (f32[1,12]{1,0:T(1,128)}, f32[1,12]{1,0:T(1,128)}, f32[1,12]{1,0:T(1,128)}, f32[1,12]{1,0:T(1,128)}) fusion(f32[12]{0:T(128)S(1)} %reduce_max.21, f32[12]{0:T(128)S(1)} %get-tuple-element.9, f32[12]{0:T(128)S(1)} %get-tuple-element.10, s32[]{:T(128)} %fusion.22, f32[12]{0:T(128)S(1)} %get-tuple-element.13, f32[12]{0:T(128)S(1)} %get-tuple-element.14), kind=kLoop, calls=%fused_computation.61 | loop fusion | flops 120 | bytes 436 | tf_op jit(solution)/shard_map/mul | solution.py:130
  (11 shorter events, 0.2 us)
Async XLA Ops:
  2.3 6.8 %collective-permute-start = (bf16[12,4224]{1,0:T(8,128)(2,1)}, bf16[12,4224]{1,0:T(8,128)(2,1)S(1)}, u32[]{:S(2)}, u32[]{:S(2)}) collective-permute-start(bf16[12,4224]{1,0:T(8,128)(2,1)} %shard_map.93), channel_id=1, source_target_pairs={{0,4},{4,0},{1,5},{5,1},{2,6},{6,2},{3,7},{7,3},{8,12},{12,8},{9,1... | collective-permute-start | bytes 304136 | tf_op jit(solution)/shard_map/ppermute | solution.py:87
  30.5 4.8 %collective-permute-start.1 = (bf16[96,4224]{1,0:T(8,128)(2,1)S(1)}, bf16[96,4224]{1,0:T(8,128)(2,1)S(1)}, u32[]{:S(2)}, u32[]{:S(2)}) collective-permute-start(bf16[96,4224]{1,0:T(8,128)(2,1)S(1)} %all_gather.3), channel_id=1, source_target_pairs={{0,1},{1,0},{2,3},{3,2},{4,5},{5,4},{6,7},{7,6},{8,9},{9,8},{10,11... | collective-permute-start | bytes 2433032 | tf_op jit(solution)/shard_map/ppermute | solution.py:94
  35.6 1.2 %copy-start = (bf16[192,4224]{1,0:T(8,128)(2,1)}, bf16[192,4224]{1,0:T(8,128)(2,1)S(1)}, u32[]{:S(2)}) copy-start(bf16[192,4224]{1,0:T(8,128)(2,1)S(1)} %maximum_select_fusion) | copy-start | bytes 4866052
  51.6 6.4 %copy-start.1 = (s32[1,8]{1,0:T(1,128)S(1)}, s32[1,8]{1,0:T(1,128)}, u32[]{:S(2)}) copy-start(s32[1,8]{1,0:T(1,128)} %param.8) | copy-start | bytes 100
  53.9 11.0 %all-to-all-start = ((f32[16,5,12]{2,1,0:T(8,128)}), f32[16,5,12]{2,1,0:T(8,128)S(1)}, u32[]{:S(2)}, u32[]{:S(2)}) async-start(f32[16,5,12]{2,1,0:T(8,128)} %copy.26), calls=%async_computation | async-start | bytes 131072 | tf_op jit(solution)/shard_map/all_to_all | solution.py:115

commit v13 on v11

--- a/solution.py
+++ b/solution.py
@@ -75,18 +75,18 @@
     columns = lax.dynamic_slice_in_dim(head, core * span, span, 1)
     offset = vocab_index * width + core * span
     local_max, sums, expected, target = partial_stats(pair_normed, columns, pair_ids, offset)
-    terms = jnp.stack([local_max, sums, expected, target]).reshape(4, 2, vocab_size, count)
+    own_block = (block_of[:, None] == vocab_index).astype(jnp.float32) * root_mean[None, :]
+    blank = jnp.zeros_like(own_block)
+    root_terms = jnp.where(
+        core == 0, jnp.concatenate([own_block, blank]), jnp.concatenate([blank, own_block])
+    ).reshape(-1)
+    terms = jnp.stack([local_max, sums, expected, target, root_terms]).reshape(5, 2, vocab_size, count)
     pair_order = lax.dynamic_slice_in_dim(order, pair_base, 2, 0)
     pair_order = jnp.take(pair_order, block_of, axis=1)
     route = (pair_order[:, None, :] == block_ids[None, :, None]).astype(jnp.float32)
-    routed = jnp.einsum("cjs,kcsr->jckr", route, terms, precision=lax.Precision.HIGHEST)
-    group_ids = jnp.arange(2, dtype=jnp.int32)
-    home = own_order[vocab_index]
-    root_slot = (block_ids[:, None] == home) & (group_ids[None, :] == core)
-    root_rows = jnp.where(root_slot[:, :, None], root_mean[None, None, :], 0.0)
-    payload = jnp.concatenate([routed, root_rows[:, :, None, :]], axis=2)
-    payload = payload.reshape(vocab_size * 2, 5, count)
-    received = lax.all_to_all(payload, VOCAB + ("grp_lo",), 0, 0, tiled=True)
+    routed = jnp.einsum("cjs,kcsr->cjkr", route, terms, precision=lax.Precision.HIGHEST)
+    payload = routed.reshape(2 * vocab_size, 5, count)
+    received = lax.all_to_all(payload, ("grp_lo",) + VOCAB, 0, 0, tiled=True)
     shard_max, shard_sums, shard_expected, shard_target, shard_root = (
         received[:, 0], received[:, 1], received[:, 2], received[:, 3], received[:, 4]
     )

time: 66 us -> 64.8 us (0.982)
  local copies, waits for them, and re-layouts: 5.13 us -> 3.58 us
    dynamic_slice x1 -> x0, local copies, waits for them, and re-layouts: 1.27 us -> none  [shards(): home = own_order[vocab_index]]
    mul x0 -> x2, other arithmetic: none -> 1.19 us  [the longest x1 1.12 us: shards(): own_root * keep]
  transfers between devices with their start and end apart: 3 -> 3, of which waited for: 2 -> 3; matrix products, arithmetic and copies ran while one was open for 10% -> 7% of each run, Pallas kernels for 0% -> 0%
where the time goes in v13:
time: 64.8 us; the launch traced here: 64.5 us
  blocking collectives  20.4 us (31%)
  matrix products  14.7 us (23%)
  other arithmetic  9.59 us (15%)
  waiting for transfers between devices  8.4 us (13%)
  starting transfers between devices  7.02 us (11%)
  local copies, waits for them, and re-layouts  3.58 us (6%)
  between operations  0.81 us (1%)
    all_gather x1, blocking collectives, shards(): packed = lax.all_gather(packed, 'vocab_hi', axis=0, tiled=True)  20.4 us
    dot_general x1, matrix products, partial_stats(): logits = jnp.dot(normed, columns, preferred_element_type=jnp.float32)  14.6 us
    all_to_all x1, waiting for transfers between devices, shards(): received = lax.all_to_all(payload, ('grp_lo',) + VOCAB, 0, 0, tiled=True)  5.44 us
    all_to_all x1, starting transfers between devices, shards(): received = lax.all_to_all(payload, ('grp_lo',) + VOCAB, 0, 0, tiled=True)  3.99 us
    ppermute x1, starting transfers between devices, shards(): lax.ppermute(packed, 'vocab_lo', [(0, 1), (1, 0)])  3.03 us
    ppermute x1, waiting for transfers between devices, shards(): lax.ppermute(packed, 'vocab_lo', [(0, 1), (1, 0)])  2.9 us
    reduce_sum x1, other arithmetic, shards(): source_block = jnp.sum(jnp.where(own_order == vocab_index, block_ids, 0))  1.32 us
    reduce_sum x1, other arithmetic, shards(): length_own = jnp.sum(jnp.where(block_ids == source_block, lengths[0], 0))  1.31 us
  transfers between devices with their start and end apart: 3, of which 3 were waited for; matrix products, arithmetic and copies ran while one was open for 7% of the time, Pallas kernels for 0%

profile of v13, /device:TPU:0, one launch (start us, length us, event | category | flops | bytes accessed | tf_op | source)
XLA Modules:
  0.0 64.5 jit_solution(4614750182680021576)
XLA Ops:
  0.6 1.1 %fusion.4 = f32[12]{0:T(128)S(1)} fusion(bf16[1,12,4096]{2,1,0:T(8,128)(2,1)} %param.6), kind=kLoop, calls=%fused_computation.13 | loop fusion | flops 147444 | bytes 98352 | tf_op jit(solution)/shard_map/reduce_sum | solution.py:23
  1.7 1.0 %fusion.6 = bf16[12,4096]{1,0:T(8,128)(2,1)S(1)} fusion(bf16[1,12,4096]{2,1,0:T(8,128)(2,1)} %param.6, f32[4096]{0:T(1024)} %param.10, f32[12]{0:T(128)S(1)} %get-tuple-element.20), kind=kLoop, calls=%fused_computation.15 | loop fusion | flops 196608 | bytes 213040 | tf_op jit(solution)/shard_map/convert_element_type | solution.py:24
  2.7 0.7 %and_convert_fusion = bf16[12,2]{1,0:T(8,128)(2,1)S(1)} fusion(s32[2]{0:T(128)S(1)} %iota_multiply_fusion, s32[12]{0:T(128)} %bitcast.54), kind=kLoop, calls=%fused_computation.30 | loop fusion | flops 72 | bytes 104 | tf_op jit(solution)/shard_map/convert_element_type | solution.py:58
  3.5 3.0 %collective-permute-start = (bf16[12,4224]{1,0:T(8,128)(2,1)S(1)}, bf16[12,4224]{1,0:T(8,128)(2,1)S(1)}, u32[]{:S(2)}, u32[]{:S(2)}) collective-permute-start(bf16[12,4224]{1,0:T(8,128)(2,1)S(1)} %pad_maximum_fusion.1), channel_id=1, source_target_pairs={{0,4},{4,0},{1,5},{5,1},{2,6},{6,2},{3,7},{7,3},{8,12},{12,8},{9,1... | collective-permute-start | bytes 304136 | tf_op jit(solution)/shard_map/ppermute | solution.py:63
  6.5 0.7 %constant_dynamic-slice_fusion = s32[2,8]{1,0:T(2,128)S(1)} fusion(s32[4,8]{1,0:T(4,128)} %param.9, s32[]{:T(128)S(6)} %select_n.159), kind=kLoop, calls=%fused_computation.62 | loop fusion | bytes 132 | tf_op jit(solution)/shard_map/dynamic_slice | solution.py:84
  7.2 2.9 %collective-permute-done = bf16[12,4224]{1,0:T(8,128)(2,1)S(1)} collective-permute-done((bf16[12,4224]{1,0:T(8,128)(2,1)S(1)}, bf16[12,4224]{1,0:T(8,128)(2,1)S(1)}, u32[]{:S(2)}, u32[]{:S(2)}) %collective-permute-start) | collective-permute-done | bytes 101408 | tf_op jit(solution)/shard_map/ppermute | solution.py:63
  10.1 0.1 pad_maximum_fusion
  10.2 20.4 %all_gather.3 = bf16[96,4224]{1,0:T(8,128)(2,1)S(1)} all-gather(bf16[24,4224]{1,0:T(8,128)(2,1)S(1)} %pad_maximum_fusion), channel_id=1, replica_groups=mesh['vocab_hi'=4,'vocab_lo'=2,'grp_hi'=2,'grp_lo'=2] {'vocab_hi'}, dimensions={0}, use_global_device_ids=true | all-gather | bytes 1013760 | tf_op jit(solution)/shard_map/all_gather | solution.py:69
  30.6 0.0 collective-permute-start.1
  30.6 0.1 copy.25
  30.7 0.6 gather_fusion
  31.3 0.1 select_bitcast_fusion
  31.4 0.1 copy.18
  31.4 1.3 %fusion.24 = s32[]{:T(128)} fusion(s32[4,8]{1,0:T(4,128)} %param.9, s32[]{:T(128)S(6)} %select_n.152, s32[]{:T(128)S(6)} %add.113), kind=kLoop, calls=%fused_computation.86 | loop fusion | flops 23 | bytes 44 | tf_op jit(solution)/shard_map/reduce_sum | solution.py:99
  32.8 0.1 broadcast_multiply_fusion
  32.8 0.1 collective-permute-done.1
  32.9 0.3 maximum_select_fusion
  33.2 0.0 copy-start
  33.2 1.2 %copy-done = bf16[192,4224]{1,0:T(8,128)(2,1)} copy-done((bf16[192,4224]{1,0:T(8,128)(2,1)}, bf16[192,4224]{1,0:T(8,128)(2,1)S(1)}, u32[]{:S(2)}) %copy-start) | copy-done | bytes 1622040
  34.4 0.1 multiply_reduce_fusion.1
  34.5 14.6 %fusion.26 = (f32[192]{0:T(256)S(1)}, f32[192,4096]{1,0:T(8,128)S(1)}) fusion(bf16[4096,8192]{1,0:T(8,128)(2,1)} %param.11, s32[]{:T(128)S(6)} %select_n.166, bf16[192,4224]{1,0:T(8,128)(2,1)} %copy-done), kind=kOutput, calls=%fused_computation.89 | convolution fusion | flops 6443237376 | bytes 38273796 | tf_op jit(solution)/shard_map/dot_general | solution.py:29
  49.1 0.0 copy-start.1
  49.1 0.1 stack.17
  49.2 1.1 %multiply_reduce_fusion = (f32[192]{0:T(256)S(1)}, f32[192]{0:T(256)S(1)}, f32[192]{0:T(256)S(1)}) fusion(f32[192,4096]{1,0:T(8,128)S(1)} %get-tuple-element.22, f32[192]{0:T(256)S(1)} %get-tuple-element.21, s32[192]{0:T(256)S(1)} %broadcast_subtract_fusion), kind=kLoop, calls=%fused_computation.5 | loop fusion | flops 5504448 | bytes 3149568 | tf_op jit(solution)/shard_map/reduce_sum | solution.py:37
  50.3 0.1 stack.18
  50.4 0.1 stack.19
  50.5 0.1 stack.20
  50.6 0.1 convolution_bitcast_fusion
  50.8 0.6 copy.20
  51.4 4.0 %all-to-all-start = ((f32[16,5,12]{2,1,0:T(8,128)}), f32[16,5,12]{2,1,0:T(8,128)S(1)}, u32[]{:S(2)}, u32[]{:S(2)}) async-start(f32[16,5,12]{2,1,0:T(8,128)} %copy.20), calls=%async_computation | async-start | bytes 131072 | tf_op jit(solution)/shard_map/all_to_all | solution.py:89
  55.4 0.0 copy-done.1
  55.4 1.3 %fusion.21 = s32[]{:T(128)} fusion(s32[1,8]{1,0:T(1,128)S(1)} %copy-done.1, s32[]{:T(128)} %fusion.24), kind=kLoop, calls=%fused_computation.73 | loop fusion | flops 23 | bytes 40 | tf_op jit(solution)/shard_map/reduce_sum | solution.py:100
  56.7 5.4 %all-to-all-done = f32[16,5,12]{2,1,0:T(8,128)S(1)} async-done(((f32[16,5,12]{2,1,0:T(8,128)}), f32[16,5,12]{2,1,0:T(8,128)S(1)}, u32[]{:S(2)}, u32[]{:S(2)}) %all-to-all-start) | async-done | bytes 3872 | tf_op jit(solution)/shard_map/all_to_all | solution.py:89
  62.2 0.1 fusion.25
  62.2 1.1 %bitcast_select_fusion.1 = f32[1,12]{1,0:T(1,128)} fusion(f32[12]{0:T(128)S(1)} %get-tuple-element.14, s32[]{:T(128)} %fusion.21), kind=kLoop, calls=%fused_computation.74 | loop fusion | flops 24 | bytes 100 | tf_op jit(solution)/shard_map/mul | solution.py:105
  63.4 1.1 %fusion.22 = (f32[1,12]{1,0:T(1,128)}, f32[1,12]{1,0:T(1,128)}, f32[1,12]{1,0:T(1,128)}) fusion(f32[12]{0:T(128)S(1)} %reduce_max.21, f32[12]{0:T(128)S(1)} %get-tuple-element.9, f32[12]{0:T(128)S(1)} %get-tuple-element.10, s32[]{:T(128)} %fusion.21, f32[12]{0:T(128)S(1)} %get-tuple-element.13), kind=kLoop, calls=%fused_computation.76 | loop fusion | flops 108 | bytes 340 | tf_op jit(solution)/shard_map/mul | solution.py:104
  (16 shorter events, 0.2 us)
Async XLA Ops:
  3.5 6.6 %collective-permute-start = (bf16[12,4224]{1,0:T(8,128)(2,1)S(1)}, bf16[12,4224]{1,0:T(8,128)(2,1)S(1)}, u32[]{:S(2)}, u32[]{:S(2)}) collective-permute-start(bf16[12,4224]{1,0:T(8,128)(2,1)S(1)} %pad_maximum_fusion.1), channel_id=1, source_target_pairs={{0,4},{4,0},{1,5},{5,1},{2,6},{6,2},{3,7},{7,3},{8,12},{12,8},{9,1... | collective-permute-start | bytes 304136 | tf_op jit(solution)/shard_map/ppermute | solution.py:63
  30.6 2.3 %collective-permute-start.1 = (bf16[96,4224]{1,0:T(8,128)(2,1)S(1)}, bf16[96,4224]{1,0:T(8,128)(2,1)S(1)}, u32[]{:S(2)}, u32[]{:S(2)}) collective-permute-start(bf16[96,4224]{1,0:T(8,128)(2,1)S(1)} %all_gather.3), channel_id=1, source_target_pairs={{0,1},{1,0},{2,3},{3,2},{4,5},{5,4},{6,7},{7,6},{8,9},{9,8},{10,11... | collective-permute-start | bytes 2433032 | tf_op jit(solution)/shard_map/ppermute | solution.py:70
  33.2 1.2 %copy-start = (bf16[192,4224]{1,0:T(8,128)(2,1)}, bf16[192,4224]{1,0:T(8,128)(2,1)S(1)}, u32[]{:S(2)}) copy-start(bf16[192,4224]{1,0:T(8,128)(2,1)S(1)} %maximum_select_fusion) | copy-start | bytes 4866052
  49.1 6.3 %copy-start.1 = (s32[1,8]{1,0:T(1,128)S(1)}, s32[1,8]{1,0:T(1,128)}, u32[]{:S(2)}) copy-start(s32[1,8]{1,0:T(1,128)} %param.8) | copy-start | bytes 100
  51.4 10.8 %all-to-all-start = ((f32[16,5,12]{2,1,0:T(8,128)}), f32[16,5,12]{2,1,0:T(8,128)S(1)}, u32[]{:S(2)}, u32[]{:S(2)}) async-start(f32[16,5,12]{2,1,0:T(8,128)} %copy.20), calls=%async_computation | async-start | bytes 131072 | tf_op jit(solution)/shard_map/all_to_all | solution.py:89

commit v14 on v13

--- a/solution.py
+++ b/solution.py
@@ -75,20 +75,27 @@
     columns = lax.dynamic_slice_in_dim(head, core * span, span, 1)
     offset = vocab_index * width + core * span
     local_max, sums, expected, target = partial_stats(pair_normed, columns, pair_ids, offset)
-    own_block = (block_of[:, None] == vocab_index).astype(jnp.float32) * root_mean[None, :]
-    blank = jnp.zeros_like(own_block)
-    root_terms = jnp.where(
-        core == 0, jnp.concatenate([own_block, blank]), jnp.concatenate([blank, own_block])
-    ).reshape(-1)
-    terms = jnp.stack([local_max, sums, expected, target, root_terms]).reshape(5, 2, vocab_size, count)
+    own_length = lax.dynamic_index_in_dim(lengths[0], vocab_index, 0, keepdims=False)
+    own_keep = (jnp.arange(count, dtype=jnp.int32) < own_length).astype(jnp.float32)
+    at_home = (block_of[:, None] == vocab_index).astype(jnp.float32)
+    blank = jnp.zeros((vocab_size, count), jnp.float32)
+
+    def home_term(values):
+        own_block = at_home * values[None, :]
+        return jnp.where(
+            core == 0, jnp.concatenate([own_block, blank]), jnp.concatenate([blank, own_block])
+        ).reshape(-1)
+
+    terms = jnp.stack([local_max, sums, expected, target, home_term(root_mean), home_term(own_keep)])
+    terms = terms.reshape(6, 2, vocab_size, count)
     pair_order = lax.dynamic_slice_in_dim(order, pair_base, 2, 0)
     pair_order = jnp.take(pair_order, block_of, axis=1)
     route = (pair_order[:, None, :] == block_ids[None, :, None]).astype(jnp.float32)
     routed = jnp.einsum("cjs,kcsr->cjkr", route, terms, precision=lax.Precision.HIGHEST)
-    payload = routed.reshape(2 * vocab_size, 5, count)
+    payload = routed.reshape(2 * vocab_size, 6, count)
     received = lax.all_to_all(payload, ("grp_lo",) + VOCAB, 0, 0, tiled=True)
-    shard_max, shard_sums, shard_expected, shard_target, shard_root = (
-        received[:, 0], received[:, 1], received[:, 2], received[:, 3], received[:, 4]
+    shard_max, shard_sums, shard_expected, shard_target, shard_root, shard_keep = (
+        received[:, k] for k in range(6)
     )
     peak = jnp.max(shard_max, axis=0)
     scale = jnp.exp(shard_max - peak[None, :])
@@ -96,9 +103,7 @@
     own_expected = jnp.sum(shard_expected * scale, axis=0)
     own_target = jnp.sum(shard_target, axis=0)
     own_root = jnp.sum(shard_root, axis=0)
-    source_block = jnp.sum(jnp.where(own_order == vocab_index, block_ids, 0))
-    length_own = jnp.sum(jnp.where(block_ids == source_block, lengths[0], 0))
-    keep = (jnp.arange(count, dtype=jnp.int32) < length_own).astype(jnp.float32)
+    keep = jnp.sum(shard_keep, axis=0)
     log_total = jnp.log(totals)
     log_prob = (own_target - peak - log_total) * keep
     entropy = (peak + log_total - own_expected / totals) * keep

time: 64.8 us -> 62.8 us (0.969)
  blocking collectives: 20.4 us -> 31 us
  waiting for transfers between devices: 8.4 us -> 3.56 us
  starting transfers between devices: 7.02 us -> 3.03 us
  other arithmetic: 9.59 us -> 5.91 us
    all_to_all x0 -> x1, blocking collectives: none -> 10.6 us  [shards(): received = lax.all_to_all(payload, ('grp_lo',) + VOCAB, 0, 0, tiled=True)]
    all_to_all x1 -> x0, waiting for transfers between devices: 5.44 us -> none  [shards(): received = lax.all_to_all(payload, ('grp_lo',) + VOCAB, 0, 0, tiled=True)]
    all_to_all x1 -> x0, starting transfers between devices: 3.99 us -> none  [shards(): received = lax.all_to_all(payload, ('grp_lo',) + VOCAB, 0, 0, tiled=True)]
    reduce_sum x2 -> x0, other arithmetic: 2.63 us -> none  [the longest x1 1.32 us: shards(): source_block = jnp.sum(jnp.where(own_order == vocab_index, block_ids, 0))]
    dynamic_slice x0 -> x1, local copies, waits for them, and re-layouts: none -> 1.24 us  [shards(): lax.dynamic_index_in_dim(lengths[0], vocab_index, 0, keepdims=False)]
    mul x2 -> x1, other arithmetic: 1.19 us -> 0.07 us  [home_term(): own_block = at_home * values[None, :]]
    dynamic_slice x1, local copies, waits for them, and re-layouts: 0.69 us -> 0.01 us  [shards(): pair_order = lax.dynamic_slice_in_dim(order, pair_base, 2, 0)]
    ppermute x1, waiting for transfers between devices: 2.9 us -> 3.55 us  [shards(): lax.ppermute(packed, 'vocab_lo', [(0, 1), (1, 0)])]
  transfers between devices with their start and end apart: 3 -> 2, of which waited for: 3 -> 1; matrix products, arithmetic and copies ran while one was open for 7% -> 4% of each run, Pallas kernels for 0% -> 0%
where the time goes in v14:
time: 62.8 us; the launch traced here: 62.6 us
  blocking collectives  31 us (49%)
  matrix products  14.7 us (23%)
  other arithmetic  5.91 us (9%)
  waiting for transfers between devices  3.56 us (6%)
  local copies, waits for them, and re-layouts  3.52 us (6%)
  starting transfers between devices  3.03 us (5%)
  between operations  0.83 us (1%)
    all_gather x1, blocking collectives, shards(): packed = lax.all_gather(packed, 'vocab_hi', axis=0, tiled=True)  20.4 us
    dot_general x1, matrix products, partial_stats(): logits = jnp.dot(normed, columns, preferred_element_type=jnp.float32)  14.6 us
    all_to_all x1, blocking collectives, shards(): received = lax.all_to_all(payload, ('grp_lo',) + VOCAB, 0, 0, tiled=True)  10.6 us
    ppermute x1, waiting for transfers between devices, shards(): lax.ppermute(packed, 'vocab_lo', [(0, 1), (1, 0)])  3.55 us
    ppermute x1, starting transfers between devices, shards(): lax.ppermute(packed, 'vocab_lo', [(0, 1), (1, 0)])  3.03 us
    unnamed x9, local copies, waits for them, and re-layouts  1.29 us
  transfers between devices with their start and end apart: 2, of which 1 were waited for; matrix products, arithmetic and copies ran while one was open for 4% of the time, Pallas kernels for 0%

profile of v14, /device:TPU:0, one launch (start us, length us, event | category | flops | bytes accessed | tf_op | source)
XLA Modules:
  0.0 62.6 jit_solution(16004576859688339365)
XLA Ops:
  0.6 0.0 copy-start
  0.7 1.1 %fusion.4 = f32[12]{0:T(128)S(1)} fusion(bf16[1,12,4096]{2,1,0:T(8,128)(2,1)} %param.6), kind=kLoop, calls=%fused_computation.13 | loop fusion | flops 147444 | bytes 98352 | tf_op jit(solution)/shard_map/reduce_sum | solution.py:23
  1.7 1.0 %fusion.6 = bf16[12,4096]{1,0:T(8,128)(2,1)S(1)} fusion(bf16[1,12,4096]{2,1,0:T(8,128)(2,1)} %param.6, f32[4096]{0:T(1024)} %param.10, f32[12]{0:T(128)S(1)} %get-tuple-element.25), kind=kLoop, calls=%fused_computation.15 | loop fusion | flops 196608 | bytes 213040 | tf_op jit(solution)/shard_map/convert_element_type | solution.py:24
  2.7 0.7 %and_convert_fusion = bf16[12,2]{1,0:T(8,128)(2,1)S(1)} fusion(s32[2]{0:T(128)S(1)} %iota_multiply_fusion, s32[12]{0:T(128)} %bitcast.56), kind=kLoop, calls=%fused_computation.32 | loop fusion | flops 72 | bytes 104 | tf_op jit(solution)/shard_map/convert_element_type | solution.py:58
  3.5 3.0 %collective-permute-start = (bf16[12,4224]{1,0:T(8,128)(2,1)S(1)}, bf16[12,4224]{1,0:T(8,128)(2,1)S(1)}, u32[]{:S(2)}, u32[]{:S(2)}) collective-permute-start(bf16[12,4224]{1,0:T(8,128)(2,1)S(1)} %pad_maximum_fusion.1), channel_id=1, source_target_pairs={{0,4},{4,0},{1,5},{5,1},{2,6},{6,2},{3,7},{7,3},{8,12},{12,8},{9,1... | collective-permute-start | bytes 304136 | tf_op jit(solution)/shard_map/ppermute | solution.py:63
  6.6 3.6 %collective-permute-done = bf16[12,4224]{1,0:T(8,128)(2,1)S(1)} collective-permute-done((bf16[12,4224]{1,0:T(8,128)(2,1)S(1)}, bf16[12,4224]{1,0:T(8,128)(2,1)S(1)}, u32[]{:S(2)}, u32[]{:S(2)}) %collective-permute-start) | collective-permute-done | bytes 101408 | tf_op jit(solution)/shard_map/ppermute | solution.py:63
  10.1 0.1 pad_maximum_fusion
  10.2 20.4 %all_gather.3 = bf16[96,4224]{1,0:T(8,128)(2,1)S(1)} all-gather(bf16[24,4224]{1,0:T(8,128)(2,1)S(1)} %pad_maximum_fusion), channel_id=1, replica_groups=mesh['vocab_hi'=4,'vocab_lo'=2,'grp_hi'=2,'grp_lo'=2] {'vocab_hi'}, dimensions={0}, use_global_device_ids=true | all-gather | bytes 1013760 | tf_op jit(solution)/shard_map/all_gather | solution.py:69
  30.6 0.0 collective-permute-start.1
  30.6 0.0 copy-done
  30.6 0.1 copy.25
  30.7 0.6 gather_fusion
  31.3 0.1 select_bitcast_fusion
  31.4 0.1 copy.18
  31.4 1.2 %constant_dynamic-slice_fusion = s32[1,1]{1,0:T(1,128)} fusion(s32[1,8]{1,0:T(1,128)} %param.8, s32[]{:T(128)S(6)} %select_n.170), kind=kLoop, calls=%fused_computation.63 | loop fusion | bytes 12 | tf_op jit(solution)/shard_map/jit(dynamic_index_in_dim)/dynamic_slice | solution.py:78
  32.7 0.7 %compare_convert_fusion = f32[12]{0:T(128)S(1)} fusion(s32[]{:T(128)} %bitcast.7), kind=kLoop, calls=%fused_computation.42 | loop fusion | flops 24 | bytes 52 | tf_op jit(solution)/shard_map/convert_element_type | solution.py:79
  33.4 0.1 broadcast_multiply_fusion
  33.4 0.0 collective-permute-done.1
  33.4 0.3 maximum_select_fusion
  33.7 0.0 copy-start.1
  33.7 1.2 %copy-done.1 = bf16[192,4224]{1,0:T(8,128)(2,1)} copy-done((bf16[192,4224]{1,0:T(8,128)(2,1)}, bf16[192,4224]{1,0:T(8,128)(2,1)S(1)}, u32[]{:S(2)}) %copy-start.1) | copy-done | bytes 1622040
  34.9 0.1 multiply_reduce_fusion.1
  35.0 14.6 %fusion.23 = (f32[192]{0:T(256)S(1)}, f32[192,4096]{1,0:T(8,128)S(1)}) fusion(bf16[4096,8192]{1,0:T(8,128)(2,1)} %param.11, s32[]{:T(128)S(6)} %select_n.160, bf16[192,4224]{1,0:T(8,128)(2,1)} %copy-done.1), kind=kOutput, calls=%fused_computation.88 | convolution fusion | flops 6443237376 | bytes 38273796 | tf_op jit(solution)/shard_map/dot_general | solution.py:29
  49.6 0.1 stack.19
  49.7 1.1 %multiply_reduce_fusion = (f32[192]{0:T(256)S(1)}, f32[192]{0:T(256)S(1)}, f32[192]{0:T(256)S(1)}) fusion(f32[192,4096]{1,0:T(8,128)S(1)} %get-tuple-element.27, f32[192]{0:T(256)S(1)} %get-tuple-element.26, s32[192]{0:T(256)S(1)} %broadcast_subtract_fusion), kind=kLoop, calls=%fused_computation.5 | loop fusion | flops 5504448 | bytes 3149568 | tf_op jit(solution)/shard_map/reduce_sum | solution.py:37
  50.8 0.1 stack.20
  50.9 0.1 stack.21
  51.0 0.1 stack.22
  51.1 0.1 convolution_bitcast_fusion
  51.3 10.6 %all_to_all.5 = f32[16,6,12]{2,1,0:T(8,128)S(1)} all-to-all(f32[16,6,12]{2,1,0:T(8,128)S(1)} %copy.20), channel_id=1, replica_groups=mesh['vocab_hi'=4,'vocab_lo'=2,'grp_hi'=2,'grp_lo'=2] {'grp_lo','vocab_h..., dimensions={0} | all-to-all | bytes 9216 | tf_op jit(solution)/shard_map/all_to_all | solution.py:96
  61.9 0.1 fusion.22
  62.0 0.5 fusion.21
  (19 shorter events, 0.2 us)
Async XLA Ops:
  0.6 30.0 %copy-start = (s32[4,8]{1,0:T(4,128)S(1)}, s32[4,8]{1,0:T(4,128)}, u32[]{:S(2)}) copy-start(s32[4,8]{1,0:T(4,128)} %param.9) | copy-start | bytes 388
  3.5 6.6 %collective-permute-start = (bf16[12,4224]{1,0:T(8,128)(2,1)S(1)}, bf16[12,4224]{1,0:T(8,128)(2,1)S(1)}, u32[]{:S(2)}, u32[]{:S(2)}) collective-permute-start(bf16[12,4224]{1,0:T(8,128)(2,1)S(1)} %pad_maximum_fusion.1), channel_id=1, source_target_pairs={{0,4},{4,0},{1,5},{5,1},{2,6},{6,2},{3,7},{7,3},{8,12},{12,8},{9,1... | collective-permute-start | bytes 304136 | tf_op jit(solution)/shard_map/ppermute | solution.py:63
  30.6 2.8 %collective-permute-start.1 = (bf16[96,4224]{1,0:T(8,128)(2,1)S(1)}, bf16[96,4224]{1,0:T(8,128)(2,1)S(1)}, u32[]{:S(2)}, u32[]{:S(2)}) collective-permute-start(bf16[96,4224]{1,0:T(8,128)(2,1)S(1)} %all_gather.3), channel_id=1, source_target_pairs={{0,1},{1,0},{2,3},{3,2},{4,5},{5,4},{6,7},{7,6},{8,9},{9,8},{10,11... | collective-permute-start | bytes 2433032 | tf_op jit(solution)/shard_map/ppermute | solution.py:70
  33.7 1.2 %copy-start.1 = (bf16[192,4224]{1,0:T(8,128)(2,1)}, bf16[192,4224]{1,0:T(8,128)(2,1)S(1)}, u32[]{:S(2)}) copy-start(bf16[192,4224]{1,0:T(8,128)(2,1)S(1)} %maximum_select_fusion) | copy-start | bytes 4866052

commit v15 on v14

--- a/solution.py
+++ b/solution.py
@@ -60,12 +60,22 @@
     packed = jnp.concatenate([normed, coded], axis=1)
     low_index = lax.axis_index("vocab_lo")
     if lax.axis_size("vocab_lo") == 2:
-        packed = jnp.concatenate([packed, lax.ppermute(packed, "vocab_lo", [(0, 1), (1, 0)])])
         positions = jnp.arange(vocab_size, dtype=jnp.int32)
         block_of = (positions // 2) * 2 + ((positions % 2) ^ low_index)
+        received_low = lax.ppermute(packed, "vocab_lo", [(0, 1), (1, 0)])
+    else:
+        block_of = block_ids
+        received_low = packed
+    pair_order = lax.dynamic_slice_in_dim(order, pair_base, 2, 0)
+    pair_order = jnp.take(pair_order, block_of, axis=1)
+    route = (pair_order[:, None, :] == block_ids[None, :, None]).astype(jnp.float32)
+    own_length = lax.dynamic_index_in_dim(lengths[0], vocab_index, 0, keepdims=False)
+    own_keep = (jnp.arange(count, dtype=jnp.int32) < own_length).astype(jnp.float32)
+    route, own_keep, received_low = lax.optimization_barrier((route, own_keep, received_low))
+    if lax.axis_size("vocab_lo") == 2:
+        packed = jnp.concatenate([packed, received_low])
     else:
         packed = lax.all_gather(packed, "vocab_lo", axis=0, tiled=True)
-        block_of = block_ids
     packed = lax.all_gather(packed, "vocab_hi", axis=0, tiled=True)
     partner = lax.ppermute(packed, "grp_lo", [(0, 1), (1, 0)])
     pair_rows = jnp.where(core == 0, jnp.concatenate([packed, partner]), jnp.concatenate([partner, packed]))
@@ -75,8 +85,6 @@
     columns = lax.dynamic_slice_in_dim(head, core * span, span, 1)
     offset = vocab_index * width + core * span
     local_max, sums, expected, target = partial_stats(pair_normed, columns, pair_ids, offset)
-    own_length = lax.dynamic_index_in_dim(lengths[0], vocab_index, 0, keepdims=False)
-    own_keep = (jnp.arange(count, dtype=jnp.int32) < own_length).astype(jnp.float32)
     at_home = (block_of[:, None] == vocab_index).astype(jnp.float32)
     blank = jnp.zeros((vocab_size, count), jnp.float32)
 
@@ -88,9 +96,6 @@
 
     terms = jnp.stack([local_max, sums, expected, target, home_term(root_mean), home_term(own_keep)])
     terms = terms.reshape(6, 2, vocab_size, count)
-    pair_order = lax.dynamic_slice_in_dim(order, pair_base, 2, 0)
-    pair_order = jnp.take(pair_order, block_of, axis=1)
-    route = (pair_order[:, None, :] == block_ids[None, :, None]).astype(jnp.float32)
     routed = jnp.einsum("cjs,kcsr->cjkr", route, terms, precision=lax.Precision.HIGHEST)
     payload = routed.reshape(2 * vocab_size, 6, count)
     received = lax.all_to_all(payload, ("grp_lo",) + VOCAB, 0, 0, tiled=True)

time: 62.8 us -> 62.2 us (level)
    ppermute x1, waiting for transfers between devices: 3.55 us -> 0.8 us  [shards(): received_low = lax.ppermute(packed, 'vocab_lo', [(0, 1), (1, 0)])]
    ppermute x1, waiting for transfers between devices: 0.01 us -> 2.23 us  [shards(): partner = lax.ppermute(packed, 'grp_lo', [(0, 1), (1, 0)])]
  transfers between devices with their start and end apart: 2 -> 2, of which waited for: 1 -> 2; matrix products, arithmetic and copies ran while one was open for 4% -> 5% of each run, Pallas kernels for 0% -> 0%
where the time goes in v15:
time: 62.2 us; the launch traced here: 62 us
  blocking collectives  30.9 us (50%)
  matrix products  14.7 us (24%)
  other arithmetic  5.91 us (10%)
  local copies, waits for them, and re-layouts  3.52 us (6%)
  waiting for transfers between devices  3.04 us (5%)
  starting transfers between devices  3.03 us (5%)
  between operations  0.84 us (1%)
    all_gather x1, blocking collectives, shards(): packed = lax.all_gather(packed, 'vocab_hi', axis=0, tiled=True)  20.4 us
    dot_general x1, matrix products, partial_stats(): logits = jnp.dot(normed, columns, preferred_element_type=jnp.float32)  14.6 us
    all_to_all x1, blocking collectives, shards(): received = lax.all_to_all(payload, ('grp_lo',) + VOCAB, 0, 0, tiled=True)  10.5 us
    ppermute x1, starting transfers between devices, shards(): received_low = lax.ppermute(packed, 'vocab_lo', [(0, 1), (1, 0)])  3.03 us
    ppermute x1, waiting for transfers between devices, shards(): partner = lax.ppermute(packed, 'grp_lo', [(0, 1), (1, 0)])  2.23 us
    unnamed x9, local copies, waits for them, and re-layouts  1.29 us
  transfers between devices with their start and end apart: 2, of which 2 were waited for; matrix products, arithmetic and copies ran while one was open for 5% of the time, Pallas kernels for 0%

profile of v15, /device:TPU:0, one launch (start us, length us, event | category | flops | bytes accessed | tf_op | source)
XLA Modules:
  0.0 62.0 jit_solution(1884767683961350856)
XLA Ops:
  0.6 0.0 copy-start
  0.7 1.1 %fusion.4 = f32[12]{0:T(128)S(1)} fusion(bf16[1,12,4096]{2,1,0:T(8,128)(2,1)} %param.6), kind=kLoop, calls=%fused_computation.13 | loop fusion | flops 147444 | bytes 98352 | tf_op jit(solution)/shard_map/reduce_sum | solution.py:23
  1.7 1.0 %fusion.6 = bf16[12,4096]{1,0:T(8,128)(2,1)S(1)} fusion(bf16[1,12,4096]{2,1,0:T(8,128)(2,1)} %param.6, f32[4096]{0:T(1024)} %param.10, f32[12]{0:T(128)S(1)} %get-tuple-element.31), kind=kLoop, calls=%fused_computation.15 | loop fusion | flops 196608 | bytes 213040 | tf_op jit(solution)/shard_map/convert_element_type | solution.py:24
  2.7 0.7 %and_convert_fusion = bf16[12,2]{1,0:T(8,128)(2,1)S(1)} fusion(s32[2]{0:T(128)S(1)} %iota_multiply_fusion, s32[12]{0:T(128)} %bitcast.56), kind=kLoop, calls=%fused_computation.33 | loop fusion | flops 72 | bytes 104 | tf_op jit(solution)/shard_map/convert_element_type | solution.py:58
  3.5 3.0 %collective-permute-start = (bf16[12,4224]{1,0:T(8,128)(2,1)S(1)}, bf16[12,4224]{1,0:T(8,128)(2,1)S(1)}, u32[]{:S(2)}, u32[]{:S(2)}) collective-permute-start(bf16[12,4224]{1,0:T(8,128)(2,1)S(1)} %pad_maximum_fusion.1), channel_id=1, source_target_pairs={{0,4},{4,0},{1,5},{5,1},{2,6},{6,2},{3,7},{7,3},{8,12},{12,8},{9,1... | collective-permute-start | bytes 304136 | tf_op jit(solution)/shard_map/ppermute | solution.py:65
  6.6 0.0 copy-done
  6.6 0.1 copy.25
  6.7 0.6 gather_fusion
  7.3 0.1 select_bitcast_fusion
  7.3 0.1 copy.18
  7.4 1.2 %constant_dynamic-slice_fusion = s32[1,1]{1,0:T(1,128)} fusion(s32[1,8]{1,0:T(1,128)} %param.8, s32[]{:T(128)S(6)} %select_n.158), kind=kLoop, calls=%fused_computation.64 | loop fusion | bytes 12 | tf_op jit(solution)/shard_map/jit(dynamic_index_in_dim)/dynamic_slice | solution.py:72
  8.7 0.6 %compare_convert_fusion.1 = f32[12]{0:T(128)S(1)} fusion(s32[]{:T(128)} %bitcast.2), kind=kLoop, calls=%fused_computation.49 | loop fusion | flops 24 | bytes 52 | tf_op jit(solution)/shard_map/convert_element_type | solution.py:73
  9.3 0.8 %collective-permute-done = bf16[12,4224]{1,0:T(8,128)(2,1)S(1)} collective-permute-done((bf16[12,4224]{1,0:T(8,128)(2,1)S(1)}, bf16[12,4224]{1,0:T(8,128)(2,1)S(1)}, u32[]{:S(2)}, u32[]{:S(2)}) %collective-permute-start) | collective-permute-done | bytes 101408 | tf_op jit(solution)/shard_map/ppermute | solution.py:65
  10.1 0.1 pad_maximum_fusion
  10.2 20.4 %all_gather.3 = bf16[96,4224]{1,0:T(8,128)(2,1)S(1)} all-gather(bf16[24,4224]{1,0:T(8,128)(2,1)S(1)} %pad_maximum_fusion), channel_id=1, replica_groups=mesh['vocab_hi'=4,'vocab_lo'=2,'grp_hi'=2,'grp_lo'=2] {'vocab_hi'}, dimensions={0}, use_global_device_ids=true | all-gather | bytes 1013760 | tf_op jit(solution)/shard_map/all_gather | solution.py:79
  30.6 0.0 collective-permute-start.1
  30.6 0.1 broadcast_multiply_fusion
  30.7 2.2 %collective-permute-done.1 = bf16[96,4224]{1,0:T(8,128)(2,1)S(1)} collective-permute-done((bf16[96,4224]{1,0:T(8,128)(2,1)S(1)}, bf16[96,4224]{1,0:T(8,128)(2,1)S(1)}, u32[]{:S(2)}, u32[]{:S(2)}) %collective-permute-start.1) | collective-permute-done | bytes 811040 | tf_op jit(solution)/shard_map/ppermute | solution.py:80
  32.9 0.3 maximum_select_fusion
  33.2 0.0 copy-start.1
  33.2 1.2 %copy-done.1 = bf16[192,4224]{1,0:T(8,128)(2,1)} copy-done((bf16[192,4224]{1,0:T(8,128)(2,1)}, bf16[192,4224]{1,0:T(8,128)(2,1)S(1)}, u32[]{:S(2)}) %copy-start.1) | copy-done | bytes 1622040
  34.4 0.1 multiply_reduce_fusion.1
  34.5 14.6 %fusion.22 = (f32[192]{0:T(256)S(1)}, f32[192,4096]{1,0:T(8,128)S(1)}) fusion(bf16[4096,8192]{1,0:T(8,128)(2,1)} %param.11, s32[]{:T(128)S(6)} %select_n.161, bf16[192,4224]{1,0:T(8,128)(2,1)} %copy-done.1), kind=kOutput, calls=%fused_computation.88 | convolution fusion | flops 6443237376 | bytes 38273796 | tf_op jit(solution)/shard_map/dot_general | solution.py:29
  49.1 0.1 stack.19
  49.2 1.1 %multiply_reduce_fusion = (f32[192]{0:T(256)S(1)}, f32[192]{0:T(256)S(1)}, f32[192]{0:T(256)S(1)}) fusion(f32[192,4096]{1,0:T(8,128)S(1)} %get-tuple-element.33, f32[192]{0:T(256)S(1)} %get-tuple-element.32, s32[192]{0:T(256)S(1)} %broadcast_subtract_fusion), kind=kLoop, calls=%fused_computation.5 | loop fusion | flops 5504448 | bytes 3149568 | tf_op jit(solution)/shard_map/reduce_sum | solution.py:37
  50.3 0.1 stack.20
  50.4 0.1 stack.21
  50.5 0.1 stack.22
  50.6 0.2 convolution_bitcast_fusion
  50.8 10.5 %all_to_all.5 = f32[16,6,12]{2,1,0:T(8,128)S(1)} all-to-all(f32[16,6,12]{2,1,0:T(8,128)S(1)} %copy.20), channel_id=1, replica_groups=mesh['vocab_hi'=4,'vocab_lo'=2,'grp_hi'=2,'grp_lo'=2] {'grp_lo','vocab_h..., dimensions={0} | all-to-all | bytes 9216 | tf_op jit(solution)/shard_map/all_to_all | solution.py:101
  61.3 0.1 fusion.21
  61.5 0.5 fusion.20
  (20 shorter events, 0.2 us)
Async XLA Ops:
  0.6 6.0 %copy-start = (s32[4,8]{1,0:T(4,128)S(1)}, s32[4,8]{1,0:T(4,128)}, u32[]{:S(2)}) copy-start(s32[4,8]{1,0:T(4,128)} %param.9) | copy-start | bytes 388
  3.5 6.6 %collective-permute-start = (bf16[12,4224]{1,0:T(8,128)(2,1)S(1)}, bf16[12,4224]{1,0:T(8,128)(2,1)S(1)}, u32[]{:S(2)}, u32[]{:S(2)}) collective-permute-start(bf16[12,4224]{1,0:T(8,128)(2,1)S(1)} %pad_maximum_fusion.1), channel_id=1, source_target_pairs={{0,4},{4,0},{1,5},{5,1},{2,6},{6,2},{3,7},{7,3},{8,12},{12,8},{9,1... | collective-permute-start | bytes 304136 | tf_op jit(solution)/shard_map/ppermute | solution.py:65
  30.6 2.3 %collective-permute-start.1 = (bf16[96,4224]{1,0:T(8,128)(2,1)S(1)}, bf16[96,4224]{1,0:T(8,128)(2,1)S(1)}, u32[]{:S(2)}, u32[]{:S(2)}) collective-permute-start(bf16[96,4224]{1,0:T(8,128)(2,1)S(1)} %all_gather.3), channel_id=1, source_target_pairs={{0,1},{1,0},{2,3},{3,2},{4,5},{5,4},{6,7},{7,6},{8,9},{9,8},{10,11... | collective-permute-start | bytes 2433032 | tf_op jit(solution)/shard_map/ppermute | solution.py:80
  33.2 1.2 %copy-start.1 = (bf16[192,4224]{1,0:T(8,128)(2,1)}, bf16[192,4224]{1,0:T(8,128)(2,1)S(1)}, u32[]{:S(2)}) copy-start(bf16[192,4224]{1,0:T(8,128)(2,1)S(1)} %maximum_select_fusion) | copy-start | bytes 4866052

commit v16 on v15

--- a/solution.py
+++ b/solution.py
@@ -79,7 +79,11 @@
     packed = lax.all_gather(packed, "vocab_hi", axis=0, tiled=True)
     partner = lax.ppermute(packed, "grp_lo", [(0, 1), (1, 0)])
     pair_rows = jnp.where(core == 0, jnp.concatenate([packed, partner]), jnp.concatenate([partner, packed]))
-    pair_normed = pair_rows[:, :features]
+    pair_normed = jnp.where(
+        core == 0,
+        jnp.concatenate([packed[:, :features], partner[:, :features]]),
+        jnp.concatenate([partner[:, :features], packed[:, :features]]),
+    )
     pair_ids = jnp.sum(pair_rows[:, features : features + digits].astype(jnp.int32) * place[None, :], axis=1)
     span = width // 2
     columns = lax.dynamic_slice_in_dim(head, core * span, span, 1)

time: 62.2 us -> 64 us (1.029)
  other arithmetic: 5.91 us -> 7.52 us
  matrix products: 14.7 us -> 16 us
  local copies, waits for them, and re-layouts: 3.52 us -> 2.46 us
    reduce_sum x1, other arithmetic: 1.14 us -> 3.02 us  [partial_stats(): jnp.sum(weights * logits, axis=1)]
    dot_general x1, matrix products: 14.6 us -> 15.8 us  [partial_stats(): logits = jnp.dot(normed, columns, preferred_element_type=jnp.float32)]
    unnamed x9 -> x7, local copies, waits for them, and re-layouts: 1.29 us -> 0.1 us
  transfers between devices with their start and end apart: 2 -> 2, of which waited for: 2 -> 2; matrix products, arithmetic and copies ran while one was open for 5% -> 4% of each run, Pallas kernels for 0% -> 0%
where the time goes in v16:
time: 64 us; the launch traced here: 63.7 us
  blocking collectives  30.9 us (48%)
  matrix products  16 us (25%)
  other arithmetic  7.52 us (12%)
  starting transfers between devices  3.03 us (5%)
  waiting for transfers between devices  2.97 us (5%)
  local copies, waits for them, and re-layouts  2.46 us (4%)
  between operations  0.84 us (1%)
    all_gather x1, blocking collectives, shards(): packed = lax.all_gather(packed, 'vocab_hi', axis=0, tiled=True)  20.4 us
    dot_general x1, matrix products, partial_stats(): logits = jnp.dot(normed, columns, preferred_element_type=jnp.float32)  15.8 us
    all_to_all x1, blocking collectives, shards(): received = lax.all_to_all(payload, ('grp_lo',) + VOCAB, 0, 0, tiled=True)  10.5 us
    ppermute x1, starting transfers between devices, shards(): received_low = lax.ppermute(packed, 'vocab_lo', [(0, 1), (1, 0)])  3.03 us
    reduce_sum x1, other arithmetic, partial_stats(): jnp.sum(weights * logits, axis=1)  3.02 us
    ppermute x1, waiting for transfers between devices, shards(): partner = lax.ppermute(packed, 'grp_lo', [(0, 1), (1, 0)])  2.16 us
  transfers between devices with their start and end apart: 2, of which 2 were waited for; matrix products, arithmetic and copies ran while one was open for 4% of the time, Pallas kernels for 0%

profile of v16, /device:TPU:0, one launch (start us, length us, event | category | flops | bytes accessed | tf_op | source)
XLA Modules:
  0.0 63.7 jit_solution(5591829830939727929)
XLA Ops:
  0.6 0.0 copy-start
  0.7 1.1 %fusion.9 = f32[12]{0:T(128)S(1)} fusion(bf16[1,12,4096]{2,1,0:T(8,128)(2,1)} %param.6), kind=kLoop, calls=%fused_computation.18 | loop fusion | flops 147444 | bytes 98352 | tf_op jit(solution)/shard_map/reduce_sum | solution.py:23
  1.7 0.7 %and_convert_fusion = bf16[12,2]{1,0:T(8,128)(2,1)S(1)} fusion(s32[2]{0:T(128)S(1)} %iota_multiply_fusion, s32[12]{0:T(128)} %bitcast.56), kind=kLoop, calls=%fused_computation.41 | loop fusion | flops 72 | bytes 104 | tf_op jit(solution)/shard_map/convert_element_type | solution.py:58
  2.5 1.0 %fusion.11 = bf16[12,4096]{1,0:T(8,128)(2,1)S(1)} fusion(bf16[1,12,4096]{2,1,0:T(8,128)(2,1)} %param.6, f32[4096]{0:T(1024)} %param.10, f32[12]{0:T(128)S(1)} %get-tuple-element.31), kind=kLoop, calls=%fused_computation.20 | loop fusion | flops 196608 | bytes 213040 | tf_op jit(solution)/shard_map/convert_element_type | solution.py:24
  3.5 3.0 %collective-permute-start = (bf16[12,4224]{1,0:T(8,128)(2,1)S(1)}, bf16[12,4224]{1,0:T(8,128)(2,1)S(1)}, u32[]{:S(2)}, u32[]{:S(2)}) collective-permute-start(bf16[12,4224]{1,0:T(8,128)(2,1)S(1)} %pad_maximum_fusion.1), channel_id=1, source_target_pairs={{0,4},{4,0},{1,5},{5,1},{2,6},{6,2},{3,7},{7,3},{8,12},{12,8},{9,1... | collective-permute-start | bytes 304136 | tf_op jit(solution)/shard_map/ppermute | solution.py:65
  6.6 0.0 copy-done
  6.6 0.1 copy.25
  6.7 0.6 gather_fusion
  7.2 0.1 select_bitcast_fusion
  7.3 0.1 copy.18
  7.4 1.2 %constant_dynamic-slice_fusion = s32[1,1]{1,0:T(1,128)} fusion(s32[1,8]{1,0:T(1,128)} %param.8, s32[]{:T(128)S(6)} %select_n.166), kind=kLoop, calls=%fused_computation.72 | loop fusion | bytes 12 | tf_op jit(solution)/shard_map/jit(dynamic_index_in_dim)/dynamic_slice | solution.py:72
  8.7 0.6 %compare_convert_fusion.1 = f32[12]{0:T(128)S(1)} fusion(s32[]{:T(128)} %bitcast.2), kind=kLoop, calls=%fused_computation.57 | loop fusion | flops 24 | bytes 52 | tf_op jit(solution)/shard_map/convert_element_type | solution.py:73
  9.3 0.8 %collective-permute-done = bf16[12,4224]{1,0:T(8,128)(2,1)S(1)} collective-permute-done((bf16[12,4224]{1,0:T(8,128)(2,1)S(1)}, bf16[12,4224]{1,0:T(8,128)(2,1)S(1)}, u32[]{:S(2)}, u32[]{:S(2)}) %collective-permute-start) | collective-permute-done | bytes 101408 | tf_op jit(solution)/shard_map/ppermute | solution.py:65
  10.1 0.1 pad_maximum_fusion
  10.2 20.4 %all_gather.3 = bf16[96,4224]{1,0:T(8,128)(2,1)S(1)} all-gather(bf16[24,4224]{1,0:T(8,128)(2,1)S(1)} %pad_maximum_fusion), channel_id=1, replica_groups=mesh['vocab_hi'=4,'vocab_lo'=2,'grp_hi'=2,'grp_lo'=2] {'vocab_hi'}, dimensions={0}, use_global_device_ids=true | all-gather | bytes 1013760 | tf_op jit(solution)/shard_map/all_gather | solution.py:79
  30.6 0.0 collective-permute-start.1
  30.6 0.1 slice.40
  30.7 0.1 broadcast_multiply_fusion
  30.8 2.2 %collective-permute-done.1 = bf16[96,4224]{1,0:T(8,128)(2,1)S(1)} collective-permute-done((bf16[96,4224]{1,0:T(8,128)(2,1)S(1)}, bf16[96,4224]{1,0:T(8,128)(2,1)S(1)}, u32[]{:S(2)}, u32[]{:S(2)}) %collective-permute-start.1) | collective-permute-done | bytes 811040 | tf_op jit(solution)/shard_map/ppermute | solution.py:80
  32.9 0.1 slice.41
  33.0 15.8 %fusion.29 = (f32[192]{0:T(256)S(1)}, f32[192,4096]{1,0:T(8,128)}) fusion(bf16[4096,8192]{1,0:T(8,128)(2,1)} %param.11, s32[]{:T(128)S(6)} %select_n.169, bf16[96,4096]{1,0:T(8,128)(2,1)S(1)} %slice.41, bf16[96,4096]{1,0:T(8,128)(2,1)S(1)} %slice.40, pred[]{:T(512)S(6)} %eq.45), kind=kOutput, calls=%fused_computation.97 | convolution fusion | flops 6450315264 | bytes 38273796 | tf_op jit(solution)/shard_map/dot_general | solution.py:29
  48.8 0.1 stack.19
  48.9 0.1 multiply_reduce_fusion.1
  49.0 3.0 %multiply_reduce_fusion = (f32[192]{0:T(256)S(1)}, f32[192]{0:T(256)S(1)}, f32[192]{0:T(256)S(1)}) fusion(f32[192,4096]{1,0:T(8,128)} %get-tuple-element.33, f32[192]{0:T(256)S(1)} %get-tuple-element.32, s32[192]{0:T(256)S(1)} %broadcast_subtract_fusion), kind=kLoop, calls=%fused_computation.5 | loop fusion | flops 5504448 | bytes 3149568 | tf_op jit(solution)/shard_map/reduce_sum | solution.py:37
  52.0 0.1 stack.21
  52.1 0.1 stack.20
  52.2 0.1 stack.22
  52.4 0.2 convolution_bitcast_fusion
  52.6 10.5 %all_to_all.5 = f32[16,6,12]{2,1,0:T(8,128)S(1)} all-to-all(f32[16,6,12]{2,1,0:T(8,128)S(1)} %copy.20), channel_id=1, replica_groups=mesh['vocab_hi'=4,'vocab_lo'=2,'grp_hi'=2,'grp_lo'=2] {'grp_lo','vocab_h..., dimensions={0} | all-to-all | bytes 9216 | tf_op jit(solution)/shard_map/all_to_all | solution.py:105
  63.1 0.1 fusion.28
  63.2 0.5 fusion.26
  (20 shorter events, 0.2 us)
Async XLA Ops:
  0.6 6.0 %copy-start = (s32[4,8]{1,0:T(4,128)S(1)}, s32[4,8]{1,0:T(4,128)}, u32[]{:S(2)}) copy-start(s32[4,8]{1,0:T(4,128)} %param.9) | copy-start | bytes 388
  3.5 6.6 %collective-permute-start = (bf16[12,4224]{1,0:T(8,128)(2,1)S(1)}, bf16[12,4224]{1,0:T(8,128)(2,1)S(1)}, u32[]{:S(2)}, u32[]{:S(2)}) collective-permute-start(bf16[12,4224]{1,0:T(8,128)(2,1)S(1)} %pad_maximum_fusion.1), channel_id=1, source_target_pairs={{0,4},{4,0},{1,5},{5,1},{2,6},{6,2},{3,7},{7,3},{8,12},{12,8},{9,1... | collective-permute-start | bytes 304136 | tf_op jit(solution)/shard_map/ppermute | solution.py:65
  30.6 2.3 %collective-permute-start.1 = (bf16[96,4224]{1,0:T(8,128)(2,1)S(1)}, bf16[96,4224]{1,0:T(8,128)(2,1)S(1)}, u32[]{:S(2)}, u32[]{:S(2)}) collective-permute-start(bf16[96,4224]{1,0:T(8,128)(2,1)S(1)} %all_gather.3), channel_id=1, source_target_pairs={{0,1},{1,0},{2,3},{3,2},{4,5},{5,4},{6,7},{7,6},{8,9},{9,8},{10,11... | collective-permute-start | bytes 2433032 | tf_op jit(solution)/shard_map/ppermute | solution.py:80

commit v17 on v15

--- a/solution.py
+++ b/solution.py
@@ -1,6 +1,9 @@
+from functools import partial
+
 import jax
 import jax.numpy as jnp
 from jax import lax
+from jax.experimental import pallas as pl
 from jax.sharding import Mesh, PartitionSpec as P
 
 EPSILON = 1e-05
@@ -39,6 +42,31 @@
     )
 
 
+def pack_kernel(states_ref, gain_ref, ids_ref, out_ref, *, features, digits):
+    values = states_ref[...].astype(jnp.float32)
+    mean_square = jnp.mean(values * values, axis=1, keepdims=True)
+    normed = (values * lax.rsqrt(mean_square + EPSILON) * gain_ref[...]).astype(jnp.bfloat16)
+    out_ref[:, :features] = normed
+    ids = ids_ref[...]
+    count = ids.shape[1]
+    row = lax.broadcasted_iota(jnp.int32, (count, count), 0)
+    col = lax.broadcasted_iota(jnp.int32, (count, count), 1)
+    token = jnp.sum(jnp.where(row == col, jnp.broadcast_to(ids, (count, count)), 0), axis=1, keepdims=True)
+    lane = lax.broadcasted_iota(jnp.int32, (count, LANES), 1)
+    code = jnp.zeros((count, LANES), jnp.int32)
+    for k in range(digits):
+        code = jnp.where(lane == k, (token >> (RADIX_BITS * k)) & (RADIX - 1), code)
+    out_ref[:, features:] = code.astype(jnp.float32).astype(jnp.bfloat16)
+
+
+def pack_rows(block_states, gain, token_ids, digits):
+    count, features = block_states.shape
+    return pl.pallas_call(
+        partial(pack_kernel, features=features, digits=digits),
+        out_shape=jax.ShapeDtypeStruct((count, features + LANES), jnp.bfloat16),
+    )(block_states, gain.reshape(1, features), token_ids)
+
+
 def shards(states, target_ids, lengths, order, gain, head):
     count = states.shape[1]
     vocab_size = lax.axis_size(VOCAB)
@@ -49,15 +77,12 @@
     pair_base = group_index - core
     own_order = lax.dynamic_index_in_dim(order, group_index, 0, keepdims=False)
     block_ids = jnp.arange(vocab_size, dtype=jnp.int32)
-    normed, root_mean = normalize(states[0], gain)
+    root_mean = jnp.sqrt(jnp.mean(jnp.square(states[0].astype(jnp.float32)), axis=-1))
     width = head.shape[1]
-    features = normed.shape[1]
+    features = states.shape[2]
     digits = digit_count(width * vocab_size)
     place = RADIX ** jnp.arange(digits, dtype=jnp.int32)
-    shifts = RADIX_BITS * jnp.arange(digits, dtype=jnp.int32)
-    coded = ((target_ids[0][:, None] >> shifts[None, :]) & (RADIX - 1)).astype(jnp.bfloat16)
-    coded = jnp.pad(coded, ((0, 0), (0, LANES - digits)))
-    packed = jnp.concatenate([normed, coded], axis=1)
+    packed = pack_rows(states[0], gain, target_ids, digits)
     low_index = lax.axis_index("vocab_lo")
     if lax.axis_size("vocab_lo") == 2:
         positions = jnp.arange(vocab_size, dtype=jnp.int32)

time: 62.2 us -> 62.1 us (level)
  Pallas kernels: 0 us -> 1.72 us
  other arithmetic: 5.91 us -> 5.05 us
  waiting for transfers between devices: 3.04 us -> 2.18 us
    convert_element_type x2 -> x0, other arithmetic: 1.74 us -> none  [the longest x1 1.01 us: normalize(): (values * lax.rsqrt(mean_square + EPSILON)[:, None] * gain).astype(jnp.bf...]
    pallas_call x0 -> x1, Pallas kernels: none -> 1.72 us  [pack_rows(): pl.pallas_call(partial(pack_kernel, features=features, digits=digits), ou...]
    ppermute x1, waiting for transfers between devices: 2.23 us -> 1.17 us  [shards(): partner = lax.ppermute(packed, 'grp_lo', [(0, 1), (1, 0)])]
    concatenate x1, other arithmetic: 0.06 us -> 0.96 us  [shards(): packed = jnp.concatenate([packed, received_low])]
  transfers between devices with their start and end apart: 2 -> 2, of which waited for: 2 -> 2; matrix products, arithmetic and copies ran while one was open for 5% -> 6% of each run, Pallas kernels for 0% -> 0%
where the time goes in v17:
time: 62.1 us; the launch traced here: 61.9 us
  blocking collectives  30.9 us (50%)
  matrix products  14.7 us (24%)
  other arithmetic  5.05 us (8%)
  local copies, waits for them, and re-layouts  3.51 us (6%)
  starting transfers between devices  2.97 us (5%)
  waiting for transfers between devices  2.18 us (4%)
  Pallas kernels  1.72 us (3%)
  between operations  0.83 us (1%)
    all_gather x1, blocking collectives, shards(): packed = lax.all_gather(packed, 'vocab_hi', axis=0, tiled=True)  20.4 us
    dot_general x1, matrix products, partial_stats(): logits = jnp.dot(normed, columns, preferred_element_type=jnp.float32)  14.6 us
    all_to_all x1, blocking collectives, shards(): received = lax.all_to_all(payload, ('grp_lo',) + VOCAB, 0, 0, tiled=True)  10.5 us
    ppermute x1, starting transfers between devices, shards(): received_low = lax.ppermute(packed, 'vocab_lo', [(0, 1), (1, 0)])  2.97 us
    pallas_call x1, Pallas kernels, pack_rows(): pl.pallas_call(partial(pack_kernel, features=features, digits=digits), ou...  1.72 us
    unnamed x9, local copies, waits for them, and re-layouts  1.29 us
  transfers between devices with their start and end apart: 2, of which 2 were waited for; matrix products, arithmetic and copies ran while one was open for 6% of the time, Pallas kernels for 0%

profile of v17, /device:TPU:0, one launch (start us, length us, event | category | flops | bytes accessed | tf_op | source)
XLA Modules:
  0.0 61.9 jit_solution(8768653365930208026)
XLA Ops:
  0.6 0.0 copy-start
  0.6 1.7 %shard_map.93 = bf16[12,4224]{1,0:T(8,128)(2,1)} custom-call(bf16[12,4096]{1,0:T(8,128)(2,1)} %bitcast.50, f32[1,4096]{1,0:T(1,128)} %bitcast.55, s32[1,12]{1,0:T(1,128)} %ids_ref.1), custom_call_target="tpu_custom_call" | custom-call | tf_op jit(solution)/shard_map/pallas_call | solution.py:64
  2.4 3.0 %collective-permute-start = (bf16[12,4224]{1,0:T(8,128)(2,1)}, bf16[12,4224]{1,0:T(8,128)(2,1)S(1)}, u32[]{:S(2)}, u32[]{:S(2)}) collective-permute-start(bf16[12,4224]{1,0:T(8,128)(2,1)} %shard_map.93), channel_id=1, source_target_pairs={{0,4},{4,0},{1,5},{5,1},{2,6},{6,2},{3,7},{7,3},{8,12},{12,8},{9,1... | collective-permute-start | bytes 304136 | tf_op jit(solution)/shard_map/ppermute | solution.py:90
  5.4 0.0 copy-done
  5.4 0.1 copy.25
  5.5 0.6 gather_fusion
  6.1 0.1 select_bitcast_fusion
  6.1 0.1 copy.18
  6.2 1.2 %constant_dynamic-slice_fusion = s32[1,1]{1,0:T(1,128)} fusion(s32[1,8]{1,0:T(1,128)} %param.8, s32[]{:T(128)S(6)} %select_n.158), kind=kLoop, calls=%fused_computation.58 | loop fusion | bytes 12 | tf_op jit(solution)/shard_map/jit(dynamic_index_in_dim)/dynamic_slice | solution.py:97
  7.5 0.6 %compare_convert_fusion.1 = f32[12]{0:T(128)S(1)} fusion(s32[]{:T(128)} %bitcast.2), kind=kLoop, calls=%fused_computation.43 | loop fusion | flops 24 | bytes 52 | tf_op jit(solution)/shard_map/convert_element_type | solution.py:98
  8.1 1.0 %collective-permute-done = bf16[12,4224]{1,0:T(8,128)(2,1)S(1)} collective-permute-done((bf16[12,4224]{1,0:T(8,128)(2,1)}, bf16[12,4224]{1,0:T(8,128)(2,1)S(1)}, u32[]{:S(2)}, u32[]{:S(2)}) %collective-permute-start) | collective-permute-done | bytes 101408 | tf_op jit(solution)/shard_map/ppermute | solution.py:90
  9.1 1.0 %pad_maximum_fusion = bf16[24,4224]{1,0:T(8,128)(2,1)S(1)} fusion(bf16[12,4224]{1,0:T(8,128)(2,1)S(1)} %collective-permute-done, bf16[12,4224]{1,0:T(8,128)(2,1)} %shard_map.93), kind=kLoop, calls=%fused_computation.12 | loop fusion | flops 405504 | bytes 405504 | tf_op jit(solution)/shard_map/concatenate | solution.py:101
  10.1 20.4 %all_gather.3 = bf16[96,4224]{1,0:T(8,128)(2,1)S(1)} all-gather(bf16[24,4224]{1,0:T(8,128)(2,1)S(1)} %pad_maximum_fusion), channel_id=1, replica_groups=mesh['vocab_hi'=4,'vocab_lo'=2,'grp_hi'=2,'grp_lo'=2] {'vocab_hi'}, dimensions={0}, use_global_device_ids=true | all-gather | bytes 1013760 | tf_op jit(solution)/shard_map/all_gather | solution.py:104
  30.5 0.0 collective-permute-start.1
  30.5 1.1 %multiply_reduce_fusion.1 = f32[12]{0:T(128)S(1)} fusion(bf16[1,12,4096]{2,1,0:T(8,128)(2,1)} %param.6), kind=kLoop, calls=%fused_computation.11 | loop fusion | flops 147444 | bytes 98352 | tf_op jit(solution)/shard_map/reduce_sum | solution.py:80
  31.6 0.1 broadcast_multiply_fusion
  31.7 1.2 %collective-permute-done.1 = bf16[96,4224]{1,0:T(8,128)(2,1)S(1)} collective-permute-done((bf16[96,4224]{1,0:T(8,128)(2,1)S(1)}, bf16[96,4224]{1,0:T(8,128)(2,1)S(1)}, u32[]{:S(2)}, u32[]{:S(2)}) %collective-permute-start.1) | collective-permute-done | bytes 811040 | tf_op jit(solution)/shard_map/ppermute | solution.py:105
  32.8 0.3 maximum_select_fusion
  33.1 0.0 copy-start.1
  33.1 1.2 %copy-done.1 = bf16[192,4224]{1,0:T(8,128)(2,1)} copy-done((bf16[192,4224]{1,0:T(8,128)(2,1)}, bf16[192,4224]{1,0:T(8,128)(2,1)S(1)}, u32[]{:S(2)}) %copy-start.1) | copy-done | bytes 1622040
  34.3 0.1 multiply_reduce_fusion.2
  34.4 14.6 %fusion.19 = (f32[192]{0:T(256)S(1)}, f32[192,4096]{1,0:T(8,128)S(1)}) fusion(bf16[4096,8192]{1,0:T(8,128)(2,1)} %param.11, s32[]{:T(128)S(6)} %select_n.161, bf16[192,4224]{1,0:T(8,128)(2,1)} %copy-done.1), kind=kOutput, calls=%fused_computation.80 | convolution fusion | flops 6443237376 | bytes 38273796 | tf_op jit(solution)/shard_map/dot_general | solution.py:32
  49.0 0.1 stack.19
  49.1 1.1 %multiply_reduce_fusion = (f32[192]{0:T(256)S(1)}, f32[192]{0:T(256)S(1)}, f32[192]{0:T(256)S(1)}) fusion(f32[192,4096]{1,0:T(8,128)S(1)} %get-tuple-element.31, f32[192]{0:T(256)S(1)} %get-tuple-element.30, s32[192]{0:T(256)S(1)} %broadcast_subtract_fusion), kind=kLoop, calls=%fused_computation.5 | loop fusion | flops 5504448 | bytes 3149568 | tf_op jit(solution)/shard_map/reduce_sum | solution.py:40
  50.2 0.1 stack.20
  50.3 0.1 stack.21
  50.4 0.1 stack.22
  50.6 0.2 convolution_bitcast_fusion
  50.8 10.5 %all_to_all.5 = f32[16,6,12]{2,1,0:T(8,128)S(1)} all-to-all(f32[16,6,12]{2,1,0:T(8,128)S(1)} %copy.20), channel_id=1, replica_groups=mesh['vocab_hi'=4,'vocab_lo'=2,'grp_hi'=2,'grp_lo'=2] {'grp_lo','vocab_h..., dimensions={0} | all-to-all | bytes 9216 | tf_op jit(solution)/shard_map/all_to_all | solution.py:126
  61.3 0.1 fusion.18
  61.4 0.5 fusion.17
  (17 shorter events, 0.2 us)
Async XLA Ops:
  0.6 4.8 %copy-start = (s32[4,8]{1,0:T(4,128)S(1)}, s32[4,8]{1,0:T(4,128)}, u32[]{:S(2)}) copy-start(s32[4,8]{1,0:T(4,128)} %param.9) | copy-start | bytes 388
  2.4 6.8 %collective-permute-start = (bf16[12,4224]{1,0:T(8,128)(2,1)}, bf16[12,4224]{1,0:T(8,128)(2,1)S(1)}, u32[]{:S(2)}, u32[]{:S(2)}) collective-permute-start(bf16[12,4224]{1,0:T(8,128)(2,1)} %shard_map.93), channel_id=1, source_target_pairs={{0,4},{4,0},{1,5},{5,1},{2,6},{6,2},{3,7},{7,3},{8,12},{12,8},{9,1... | collective-permute-start | bytes 304136 | tf_op jit(solution)/shard_map/ppermute | solution.py:90
  30.5 2.3 %collective-permute-start.1 = (bf16[96,4224]{1,0:T(8,128)(2,1)S(1)}, bf16[96,4224]{1,0:T(8,128)(2,1)S(1)}, u32[]{:S(2)}, u32[]{:S(2)}) collective-permute-start(bf16[96,4224]{1,0:T(8,128)(2,1)S(1)} %all_gather.3), channel_id=1, source_target_pairs={{0,1},{1,0},{2,3},{3,2},{4,5},{5,4},{6,7},{7,6},{8,9},{9,8},{10,11... | collective-permute-start | bytes 2433032 | tf_op jit(solution)/shard_map/ppermute | solution.py:105
  33.1 1.2 %copy-start.1 = (bf16[192,4224]{1,0:T(8,128)(2,1)}, bf16[192,4224]{1,0:T(8,128)(2,1)S(1)}, u32[]{:S(2)}) copy-start(bf16[192,4224]{1,0:T(8,128)(2,1)S(1)} %maximum_select_fusion) | copy-start | bytes 4866052
